TPU v7x, 512 devices: a whole 4x8x8 slice. The times are simulated.
512 devices in a mesh: dp: 64 (over z, y_hi, core), mp: 8 (over x, y_lo).
Axes of the slice: x: 4, y: 8 (y_hi: 4, y_lo: 2; y = y_hi * 2 + y_lo), z: 8, core: 2. Of those that a mesh axis runs over, the one named last changes fastest.
Arguments:
- queries: bfloat16 [32768, 8192], P('dp', 'mp'), may hold values from -45 to 45
- key_rows: bfloat16 [32768, 1024], P('dp', 'mp'), may hold values from -4 to 4
- value_rows: bfloat16 [32768, 1024], P('dp', 'mp'), may hold values from -6 to 6
- landmark_index: int32 [512], P('dp'), may hold values from 0 to 32767, as said below
- radius_in: float32 [512], replicated, may hold values from 0.5 to 4
- radius_out: float32 [512], replicated, may hold values from 0.02 to 0.5
Outputs:
- cross_covariance: float32 [512, 512], P('mp', 'dp')
Inputs may be any that keep to these rules, and one draw needn't show every extreme that they name: `landmark_index`: the 8 landmarks held by index d of dp name distinct tokens of sequence d, that is, positions d * 512 to (d + 1) * 512 - 1.
All inputs are finite; a program needn't handle non-finite values.
Results may differ from a plain program's by a relative error of at most 0.003.
Values may be sent and summed in bfloat16 or wider, within the bound.
No kernel may reach another device: no remote copies, remote signals or barrier semaphores. Data moves between devices by JAX's collectives and lax.ppermute only.
A program may use at most 64 MiB of HBM per device.

v0:
```python
import functools
import math

import jax
import jax.numpy as jnp
from jax import lax
from jax.sharding import PartitionSpec as P

D = 8192
HEAD_DIM = 128


EPSILON = 1e-06


def attend_head(queries, key_rows, value_rows, group_size, head_index):
    query_head = lax.dynamic_slice_in_dim(queries, head_index * HEAD_DIM, HEAD_DIM, 1)
    scores = lax.dot_general(
        query_head, key_rows, (((1,), (1,)), ((), ())), preferred_element_type=jnp.float32
    ) / math.sqrt(HEAD_DIM)
    length = queries.shape[0]
    row_position = lax.broadcasted_iota(jnp.int32, (length, length), 0)
    column_position = lax.broadcasted_iota(jnp.int32, (length, length), 1)
    scores = jnp.where(column_position <= row_position, scores, -jnp.inf)
    weights = jax.nn.softmax(scores, axis=-1).astype(jnp.bfloat16)
    return jnp.dot(weights, value_rows, preferred_element_type=jnp.float32).astype(jnp.bfloat16)


def squares_by_row(matrix):
    return jnp.sum(jnp.square(matrix.astype(jnp.float32)), axis=-1)


def inner_rows(left, right):
    return lax.dot_general(
        left, right, (((1,), (1,)), ((), ())), preferred_element_type=jnp.float32
    )


def inner_columns(left, right):
    return lax.dot_general(
        left, right, (((0,), (0,)), ((), ())), preferred_element_type=jnp.float32
    )


def center(features, totals, token_count):
    return (features.astype(jnp.float32) - totals / token_count).astype(jnp.bfloat16)


def shards(queries, key_rows, value_rows, landmark_index, radius_in, radius_out):
    length = queries.shape[0]
    heads_local = queries.shape[1] // HEAD_DIM
    group_size = heads_local // (key_rows.shape[1] // HEAD_DIM)
    per_head = lax.map(
        functools.partial(attend_head, queries, key_rows, value_rows, group_size),
        jnp.arange(heads_local, dtype=jnp.int32),
    )
    attended = jnp.transpose(per_head, (1, 0, 2)).reshape(length, heads_local * HEAD_DIM)
    landmarks = radius_in.shape[0]
    model_index = lax.axis_index("mp")
    data_index = lax.axis_index("dp")
    row_share = landmarks // lax.axis_size("mp")
    column_share = landmarks // lax.axis_size("dp")
    token_count = length * lax.axis_size("dp")
    widths = jnp.stack([radius_in, radius_out])
    own_rows = landmark_index % length
    landmark_rows = jnp.stack(
        [jnp.take(queries, own_rows, axis=0), jnp.take(attended, own_rows, axis=0)]
    )
    row_norms = jnp.stack([squares_by_row(queries), squares_by_row(attended)])
    landmark_piece = lax.all_gather(landmark_rows, "dp", axis=1, tiled=True)
    mark_norms = squares_by_row(landmark_piece)
    cross = jnp.stack(
        [inner_rows(queries, landmark_piece[0]), inner_rows(attended, landmark_piece[1])]
    )
    distance_part = row_norms[:, :, None] + mark_norms[:, None, :] - 2.0 * cross
    distance = lax.psum(distance_part, "mp")
    features = jnp.exp(-distance / (D * widths[:, None, :])).astype(jnp.bfloat16)
    row_features = lax.dynamic_slice_in_dim(features[0], model_index * row_share, row_share, 1)
    column_features = features[1]
    row_total, column_total = lax.psum(
        (
            jnp.sum(row_features.astype(jnp.float32), axis=0),
            jnp.sum(column_features.astype(jnp.float32), axis=0),
        ),
        "dp",
    )
    rows_centered = center(row_features, row_total[None, :], token_count)
    columns_centered = center(column_features, column_total[None, :], token_count)
    second = inner_columns(rows_centered, columns_centered)
    row_spread = jnp.sum(jnp.square(rows_centered.astype(jnp.float32)), axis=0)
    column_spread = jnp.sum(jnp.square(columns_centered.astype(jnp.float32)), axis=0)
    second, row_spread, column_spread = lax.psum((second, row_spread, column_spread), "dp")
    own_block = lax.dynamic_slice_in_dim(second, data_index * column_share, column_share, 1)
    column_spread = lax.dynamic_slice_in_dim(
        column_spread, data_index * column_share, column_share, 0
    )
    covariance = own_block / token_count
    spread_rows = row_spread / token_count
    spread_columns = column_spread / token_count
    return covariance / jnp.sqrt(
        (spread_rows + EPSILON)[:, None] * (spread_columns + EPSILON)[None, :]
    )


def solution(mesh):
    return jax.shard_map(
        shards,
        mesh=mesh,
        in_specs=(P("dp", "mp"), P("dp", "mp"), P("dp", "mp"), P("dp"), P(), P()),
        out_specs=P("mp", "dp"),
        check_vma=False,
    )
```

profile of v0, /device:TPU:1, one launch (start us, length us, event | category | flops | bytes accessed | tf_op | source)
XLA Modules:
  0.0 903.9 jit_solution(17541337728010904406)
XLA Ops:
  6.5 0.7 compare_and_fusion
  7.2 1.9 gather_fusion
  9.2 26.6 %while.10 = (s32[]{:T(128)}, bf16[8,512,128]{2,1,0:T(8,128)(2,1)S(1)}, s32[8]{0:T(128)S(1)}, bf16[512,1024]{1,0:T(8,128)(2,1)}, bf16[512,128]{1,0:T(8,128)(2,1)}...) while((s32[]{:T(128)}, bf16[8,512,128]{2,1,0:T(8,128)(2,1)S(1)}, ...), condition=%wide.region_4.5_spmd, body=%wide.region_1.4_spmd.sunk | while | flops 136641536 | bytes 4204747 | solution.py:53
  9.2 0.7 dynamic_slice.34
  10.6 1.3 fusion.39
  11.9 0.2 fusion.40
  12.1 0.4 fusion.41
  12.5 0.7 dynamic_slice.34
  13.9 1.3 fusion.39
  15.2 0.2 fusion.40
  15.4 0.4 fusion.41
  15.9 0.7 dynamic_slice.34
  17.2 1.3 fusion.39
  18.5 0.2 fusion.40
  18.7 0.4 fusion.41
  19.2 0.7 dynamic_slice.34
  20.5 1.3 fusion.39
  22.0 0.4 fusion.41
  22.5 0.7 dynamic_slice.34
  23.9 1.3 fusion.39
  25.4 0.4 fusion.41
  25.8 0.7 dynamic_slice.34
  27.2 1.3 fusion.39
  28.7 0.4 fusion.41
  29.2 0.7 dynamic_slice.34
  30.5 1.3 fusion.39
  32.0 0.4 fusion.41
  32.5 0.7 dynamic_slice.34
  33.9 1.3 fusion.39
  35.3 0.4 fusion.41
  36.0 0.6 gather_fusion.1
  36.6 0.6 pad_maximum_fusion
  37.3 0.3 multiply_reduce_fusion.2
  37.6 0.3 multiply_reduce_fusion.1
  37.9 89.6 %all-gather.2.cloned.1.call-done = bf16[2,512,1024]{2,1,0:T(8,128)(2,1)} async-done(((bf16[2,8,1024]{2,1,0:T(8,128)(2,1)}), bf16[2,512,1024]{2,1,0:T(8,128)(2,1)}) %all-gather.2.cloned.1.call-update) | async-done | bytes 2097168 | tf_op jit(solution)/shard_map/all_gather | solution.py:70
  127.4 2.1 convolution_bitcast_fusion
  129.6 0.5 multiply_reduce_fusion
  130.1 0.8 convolution_bitcast_fusion.1
  130.8 1.6 fusion.8
  132.5 0.6 copy-done.2
  133.1 110.2 %all-reduce.5.cloned.1.call-done = f32[2,512,512]{1,2,0:T(8,128)} async-done(((f32[2,512,512]{1,2,0:T(8,128)}), f32[2,512,512]{1,2,0:T(8,128)}) %all-reduce.5.cloned.1.call-update) | async-done | bytes 2097168 | tf_op jit(solution)/shard_map/psum | solution.py:76
  243.3 2.0 exponential_convert_fusion
  245.7 139.0 %all-reduce.1 = (f32[512]{0:T(512)S(1)}, f32[64]{0:T(128)S(1)}) all-reduce(f32[512]{0:T(512)S(1)} %convert_reduce_fusion, f32[64]{0:T(128)S(1)} %convert_reduce_fusion.1), channel_id=1, replica_groups=mesh['dp'=64,'mp'=8] {'dp'}, use_global_device_ids=true, to_apply=%region_11.13 | all-reduce | flops 576 | bytes 4608 | tf_op jit(solution)/shard_map/psum | solution.py:80
  384.9 1.1 fusion.13
  386.0 0.3 multiply_reduce_fusion.3
  386.3 143.5 %all-reduce = (f32[512]{0:T(512)S(1)}, f32[64]{0:T(128)S(1)}) all-reduce(f32[512]{0:T(512)S(1)} %multiply_reduce_fusion.3, f32[64]{0:T(128)S(1)} %multiply_reduce_fusion.4), channel_id=1, replica_groups=mesh['dp'=64,'mp'=8] {'dp'}, use_global_device_ids=true, to_apply=%region_16.18 | all-reduce | flops 576 | bytes 4608 | tf_op jit(solution)/shard_map/psum | solution.py:92
  529.9 366.1 %all-reduce.7.cloned.1.call-done = f32[64,512]{0,1:T(8,128)} async-done(((f32[64,512]{0,1:T(8,128)}), f32[64,512]{0,1:T(8,128)}) %all-reduce.7.cloned.1.call-update) | async-done | bytes 131088 | tf_op jit(solution)/shard_map/psum | solution.py:92
  896.0 1.3 rsqrt_multiply_fusion
  (49 shorter events, 2.0 us)
Async XLA Ops:
  6.5 120.9 %all-gather.2.cloned.1.call-start = ((), (), s32[]{:S(2)}) async-start(), calls=%async_computation | async-start | bytes 2129920 | tf_op jit(solution)/shard_map/all_gather | solution.py:70
  9.2 2.9 copy-start.4
  12.5 2.9 copy-start.4
  15.8 2.9 copy-start.4
  19.2 2.9 copy-start.4
  22.5 2.9 copy-start.4
  25.8 2.9 copy-start.4
  29.1 2.9 copy-start.4
  32.5 2.9 copy-start.4
  35.8 1.5 copy-start.1
  37.2 206.1 %all-reduce.5.cloned.1.call-start = ((), (), s32[]{:S(2)}) async-start(), calls=%async_computation.1 | async-start | bytes 4194304 | tf_op jit(solution)/shard_map/psum | solution.py:76
  127.4 2.1 copy-start
  132.4 0.7 copy-start.2
  132.4 0.7 copy-start.3
  132.4 763.6 %all-reduce.7.cloned.1.call-start = ((), (), s32[]{:S(2)}) async-start(), calls=%async_computation.2 | async-start | bytes 524288 | tf_op jit(solution)/shard_map/psum | solution.py:92
Sparse Core Ops, SparseCore 0:
  37.4 90.0 all-gather.1
  132.6 110.7 all-reduce.4
  386.4 509.5 all-reduce.6
where the time goes:
time: 904 us
  waiting for transfers between devices  566 us (63%)
  blocking collectives  283 us (31%)
  matrix products  17.8 us (2%)
  between operations  13.2 us (1%)
  other arithmetic  9.8 us (1%)
    psum x1, waiting for transfers between devices, shards(): lax.psum((second, row_spread, column_spread), 'dp')  366 us
    psum x1, blocking collectives, shards(): lax.psum((second, row_spread, column_spread), 'dp')  144 us
    psum x1, blocking collectives, shards(): lax.psum((jnp.sum(row_features.astype(jnp.float32), axis=0), jnp.sum(colu...  139 us
    psum x1, waiting for transfers between devices, shards(): distance = lax.psum(distance_part, 'mp')  110 us
    all_gather x1, waiting for transfers between devices, shards(): landmark_piece = lax.all_gather(landmark_rows, 'dp', axis=1, tiled=True)  89.6 us
  transfers between devices with their start and end apart: 3, of which 3 were waited for; matrix products, arithmetic and copies ran while one was open for 0% of the time, Pallas kernels for 0%

commit v1 on v0

v1 whole, which is shorter than its diff:
```python
import math

import jax
import jax.numpy as jnp
from jax import lax
from jax.sharding import PartitionSpec as P

D = 8192
HEAD_DIM = 128


EPSILON = 1e-06


def attend(queries, key_rows, value_rows):
    length = queries.shape[0]
    kv_heads = key_rows.shape[1] // HEAD_DIM
    group_size = queries.shape[1] // HEAD_DIM // kv_heads
    query_four = queries.reshape(length, kv_heads, group_size, HEAD_DIM)
    key_three = key_rows.reshape(length, kv_heads, HEAD_DIM)
    value_three = value_rows.reshape(length, kv_heads, HEAD_DIM)
    scores = jnp.einsum(
        "tkgd,skd->kgts", query_four, key_three, preferred_element_type=jnp.float32
    ) / math.sqrt(HEAD_DIM)
    row_position = lax.broadcasted_iota(jnp.int32, (length, length), 0)
    column_position = lax.broadcasted_iota(jnp.int32, (length, length), 1)
    scores = jnp.where(column_position <= row_position, scores, -jnp.inf)
    weights = jax.nn.softmax(scores, axis=-1).astype(jnp.bfloat16)
    mixture = jnp.einsum(
        "kgts,skd->tkgd", weights, value_three, preferred_element_type=jnp.float32
    )
    return mixture.astype(jnp.bfloat16).reshape(length, queries.shape[1])


def squares_by_row(matrix):
    return jnp.sum(jnp.square(matrix.astype(jnp.float32)), axis=-1)


def inner_rows(left, right):
    return lax.dot_general(
        left, right, (((1,), (1,)), ((), ())), preferred_element_type=jnp.float32
    )


def broadcast_gather(piece, axis_name):
    count = lax.axis_size(axis_name)
    spread = jnp.broadcast_to(piece[None], (count,) + piece.shape)
    return lax.all_to_all(spread, axis_name, 0, 0, tiled=True)


def shards(queries, key_rows, value_rows, landmark_index, radius_in, radius_out):
    length = queries.shape[0]
    model_count = lax.axis_size("mp")
    data_count = lax.axis_size("dp")
    model_index = lax.axis_index("mp")
    landmarks = radius_in.shape[0]
    row_share = landmarks // model_count
    column_share = landmarks // data_count
    token_count = length * data_count

    attended = attend(queries, key_rows, value_rows)

    own_rows = landmark_index % length
    landmark_rows = jnp.stack(
        [jnp.take(queries, own_rows, axis=0), jnp.take(attended, own_rows, axis=0)]
    )
    gathered = broadcast_gather(landmark_rows, "dp")
    landmark_piece = jnp.transpose(gathered, (1, 0, 2, 3)).reshape(
        2, landmarks, queries.shape[1]
    )

    row_norms = jnp.stack([squares_by_row(queries), squares_by_row(attended)])
    mark_norms = squares_by_row(landmark_piece)
    cross = jnp.stack(
        [inner_rows(queries, landmark_piece[0]), inner_rows(attended, landmark_piece[1])]
    )
    distance_part = row_norms[:, :, None] + mark_norms[:, None, :] - 2.0 * cross
    distance_part = distance_part.reshape(2, length, model_count, row_share)
    distance = jnp.sum(
        lax.all_to_all(distance_part, "mp", 2, 2, tiled=True), axis=2
    )

    widths = lax.dynamic_slice_in_dim(
        jnp.stack([radius_in, radius_out]), model_index * row_share, row_share, 1
    )
    features = jnp.exp(-distance / (D * widths[:, None, :])).astype(jnp.bfloat16)
    row_features = features[0]
    column_features = jnp.transpose(
        broadcast_gather(features[1], "mp"), (1, 0, 2)
    ).reshape(length, landmarks)

    rows32 = row_features.astype(jnp.float32)
    columns32 = column_features.astype(jnp.float32)
    row_mean = jnp.mean(rows32, axis=0)
    column_mean = jnp.mean(columns32, axis=0)
    rows_centered = rows32 - row_mean[None, :]
    columns_centered = columns32 - column_mean[None, :]
    second = lax.dot_general(
        rows_centered,
        columns_centered,
        (((0,), (0,)), ((), ())),
        precision=lax.Precision.HIGHEST,
        preferred_element_type=jnp.float32,
    )
    row_square = jnp.sum(jnp.square(rows_centered), axis=0)
    column_square = jnp.sum(jnp.square(columns_centered), axis=0)

    packed = jnp.concatenate(
        [
            jnp.transpose(
                second.reshape(row_share, data_count, column_share), (1, 0, 2)
            ).reshape(data_count, row_share * column_share),
            jnp.broadcast_to(row_mean[None], (data_count, row_share)),
            jnp.broadcast_to(row_square[None], (data_count, row_share)),
            column_mean.reshape(data_count, column_share),
            column_square.reshape(data_count, column_share),
        ],
        axis=1,
    )
    received = lax.all_to_all(packed, "dp", 0, 0, tiled=True)
    cut = row_share * column_share
    second_parts = received[:, :cut].reshape(data_count, row_share, column_share)
    row_means = received[:, cut : cut + row_share]
    row_squares = received[:, cut + row_share : cut + 2 * row_share]
    column_means = received[:, cut + 2 * row_share : cut + 2 * row_share + column_share]
    column_squares = received[:, cut + 2 * row_share + column_share :]

    row_shift = row_means - jnp.mean(row_means, axis=0)[None, :]
    column_shift = column_means - jnp.mean(column_means, axis=0)[None, :]
    between = jnp.sum(row_shift[:, :, None] * column_shift[:, None, :], axis=0)
    covariance = (jnp.sum(second_parts, axis=0) + length * between) / token_count
    spread_rows = (
        jnp.sum(row_squares, axis=0) + length * jnp.sum(jnp.square(row_shift), axis=0)
    ) / token_count
    spread_columns = (
        jnp.sum(column_squares, axis=0)
        + length * jnp.sum(jnp.square(column_shift), axis=0)
    ) / token_count
    return covariance / jnp.sqrt(
        (spread_rows + EPSILON)[:, None] * (spread_columns + EPSILON)[None, :]
    )


def solution(mesh):
    return jax.shard_map(
        shards,
        mesh=mesh,
        in_specs=(P("dp", "mp"), P("dp", "mp"), P("dp", "mp"), P("dp"), P(), P()),
        out_specs=P("mp", "dp"),
        check_vma=False,
    )
```

time: 904 us -> 179 us (0.20)
  waiting for transfers between devices: 566 us -> 99.2 us
  blocking collectives: 283 us -> 28 us
  starting transfers between devices: 0.09 us -> 25.3 us
  between operations: 13.2 us -> 0.3 us
    psum x2 -> x0, waiting for transfers between devices: 476 us -> none  [the longest x1 366 us: shards(): lax.psum((second, row_spread, column_spread), 'dp')]
    psum x2 -> x0, blocking collectives: 283 us -> none  [the longest x1 144 us: shards(): lax.psum((second, row_spread, column_spread), 'dp')]
    all_to_all x0 -> x3, waiting for transfers between devices: none -> 99.2 us  [the longest x2 72.8 us: broadcast_gather(): return lax.all_to_all(spread, axis_name, 0, 0, tiled=True)]
    all_gather x1 -> x0, waiting for transfers between devices: 89.6 us -> none  [shards(): landmark_piece = lax.all_gather(landmark_rows, 'dp', axis=1, tiled=True)]
    all_to_all x0 -> x1, blocking collectives: none -> 28 us  [shards(): received = lax.all_to_all(packed, 'dp', 0, 0, tiled=True)]
    all_to_all x0 -> x3, starting transfers between devices: none -> 25.3 us  [the longest x2 21.3 us: broadcast_gather(): return lax.all_to_all(spread, axis_name, 0, 0, tiled=True)]
where the time goes in v1:
time: 179 us; the launch traced here: 178 us
  waiting for transfers between devices  99.2 us (55%)
  blocking collectives  28 us (16%)
  starting transfers between devices  25.3 us (14%)
  matrix products  11.4 us (6%)
  local copies, waits for them, and re-layouts  8.74 us (5%)
  other arithmetic  5.44 us (3%)
    all_to_all x2, waiting for transfers between devices, broadcast_gather(): return lax.all_to_all(spread, axis_name, 0, 0, tiled=True)  72.8 us
    all_to_all x1, blocking collectives, shards(): received = lax.all_to_all(packed, 'dp', 0, 0, tiled=True)  28 us
    all_to_all x1, waiting for transfers between devices, shards(): lax.all_to_all(distance_part, 'mp', 2, 2, tiled=True)  26.3 us
    all_to_all x2, starting transfers between devices, broadcast_gather(): return lax.all_to_all(spread, axis_name, 0, 0, tiled=True)  21.3 us
    dot_general x2, matrix products, inner_rows(): lax.dot_general(left, right, (((1,), (1,)), ((), ())), preferred_element_...  4.02 us
    all_to_all x1, starting transfers between devices, shards(): lax.all_to_all(distance_part, 'mp', 2, 2, tiled=True)  4.02 us
  transfers between devices with their start and end apart: 3, of which 3 were waited for; matrix products, arithmetic and copies ran while one was open for 0% of the time, Pallas kernels for 0%

profile of v1, /device:TPU:1, one launch (start us, length us, event | category | flops | bytes accessed | tf_op | source)
XLA Modules:
  0.0 178.4 jit_solution(9404413491997611978)
XLA Ops:
  0.0 0.1 iota_compare_fusion
  0.1 0.8 copy-done
  0.9 2.7 %fusion.1 = (f32[8,512]{1,0:T(8,128)S(1)}, f32[512,512,8]{1,0,2:T(8,128)S(1)}) fusion(pred[512,512]{0,1:T(8,128)(4,1)S(1)} %iota_compare_fusion, bf16[512,128]{1,0:T(8,128)(2,1)S(1)} %copy-done, bf16[512,1024]{1,0:T(8,128)(2,1)} %param.8), kind=kOutput, calls=%fused_computation.6 | convolution fusion | flops 543158272 | bytes 9846784 | tf_op jit(solution)/shard_map/tkgd,skd->kgts/dot_general | solution.py:22
  3.6 1.7 fusion
  5.4 2.6 %multiply_reduce_fusion.1 = (f32[512]{0:T(512)S(1)}, bf16[8,512,128]{1,2,0:T(8,128)(2,1)S(1)}) fusion(bf16[512,128]{1,0:T(8,128)(2,1)S(1)} %copy-done.6, f32[8,512]{1,0:T(8,128)S(1)} %fusion, f32[8,512]{1,0:T(8,128)S(1)} %get-tuple-element.18, f32[512,512,8]{1,0,2:T(8,128)S(1)} %get-tuple-element.19, pred[512,512]{0,1:T(8,128)(4,1)S(1)} %iota_compare_fusion), kind=kOutput, calls=%fused_computation.13 | convolution fusion | flops 549453312 | bytes 9865216 | tf_op jit(solution)/shard_map/kgts,skd->tkgd/dot_general | solution.py:29
  8.0 0.5 copy.49
  8.6 0.6 gather_fusion
  9.1 0.6 gather_fusion.1
  9.7 0.1 select_bitcast_fusion.1
  9.8 1.6 broadcast_in_dim.29
  11.4 17.6 %all-to-all-start = ((bf16[64,2,8,1024]{3,2,1,0:T(8,128)(2,1)}), bf16[64,2,8,1024]{3,2,1,0:T(8,128)(2,1)S(1)}, u32[]{:S(2)}, u32[]{:S(2)}) async-start(bf16[64,2,8,1024]{3,2,1,0:T(8,128)(2,1)} %broadcast_in_dim.29), calls=%async_computation | async-start | bytes 4194304 | tf_op jit(solution)/shard_map/all_to_all | solution.py:48
  29.1 0.3 multiply_reduce_fusion.2
  29.4 64.8 %all-to-all-done = bf16[64,2,8,1024]{3,2,1,0:T(8,128)(2,1)S(1)} async-done(((bf16[64,2,8,1024]{3,2,1,0:T(8,128)(2,1)}), bf16[64,2,8,1024]{3,2,1,0:T(8,128)(2,1)S(1)}, u32[]{:S(2)}, u32[]{:S(2)}) %all-to-all-start) | async-done | bytes 2097184 | tf_op jit(solution)/shard_map/all_to_all | solution.py:48
  94.1 1.1 slice.43
  95.2 1.8 fusion.12
  97.0 0.5 multiply_reduce_fusion
  97.5 0.1 add.64
  97.6 2.2 %convolution_bitcast_fusion = f32[1,512,8,64]{1,3,2,0:T(8,128)S(1)} fusion(bf16[512,1024,1]{0,1,2:T(8,128)(2,1)} %bitcast.121, bf16[8,64,1024]{2,1,0:T(8,128)(2,1)} %bitcast.122), kind=kOutput, calls=%fused_computation.16 | convolution fusion | flops 536870912 | bytes 3145728 | tf_op jit(solution)/shard_map/dot_general | solution.py:40
  99.9 0.3 fusion.5
  100.2 1.6 copy.51
  101.8 4.0 %all-to-all-start.1 = ((f32[2,512,8,64]{1,3,0,2:T(8,128)}), f32[2,512,8,64]{1,3,0,2:T(8,128)S(1)}, u32[]{:S(2)}, u32[]{:S(2)}) async-start(f32[2,512,8,64]{1,3,0,2:T(8,128)} %copy.51), calls=%async_computation.1 | async-start | bytes 4194304 | tf_op jit(solution)/shard_map/all_to_all | solution.py:80
  105.8 0.1 fusion.26
  105.9 26.3 %all-to-all-done.1 = f32[2,512,8,64]{1,3,0,2:T(8,128)S(1)} async-done(((f32[2,512,8,64]{1,3,0,2:T(8,128)}), f32[2,512,8,64]{1,3,0,2:T(8,128)S(1)}, u32[]{:S(2)}, u32[]{:S(2)}) %all-to-all-start.1) | async-done | bytes 2097184 | tf_op jit(solution)/shard_map/all_to_all | solution.py:80
  132.2 0.2 reduce_sum.159
  132.5 0.1 exponential_convert_fusion
  132.6 0.8 broadcast_in_dim.31
  133.4 3.7 %all-to-all-start.2 = ((bf16[8,512,64]{1,2,0:T(8,128)(2,1)}), bf16[8,512,64]{1,2,0:T(8,128)(2,1)S(1)}, u32[]{:S(2)}, u32[]{:S(2)}) async-start(bf16[8,512,64]{1,2,0:T(8,128)(2,1)} %broadcast_in_dim.31), calls=%async_computation.2 | async-start | bytes 1048576 | tf_op jit(solution)/shard_map/all_to_all | solution.py:48
  137.1 0.1 convert_reduce_fusion
  137.2 0.2 fusion.20
  137.4 8.1 %all-to-all-done.2 = bf16[8,512,64]{1,2,0:T(8,128)(2,1)S(1)} async-done(((bf16[8,512,64]{1,2,0:T(8,128)(2,1)}), bf16[8,512,64]{1,2,0:T(8,128)(2,1)S(1)}, u32[]{:S(2)}, u32[]{:S(2)}) %all-to-all-start.2) | async-done | bytes 524320 | tf_op jit(solution)/shard_map/all_to_all | solution.py:48
  145.5 0.1 bitcast_reduce_fusion
  145.6 0.1 div.77
  145.7 0.1 div.78
  145.8 0.3 fusion.14
  146.1 0.1 reshape.139
  146.2 0.1 copy.55
  146.2 0.1 bitcast_subtract_fusion
  146.4 2.1 %convolution_bitcast_fusion.1 = f32[64,64,8]{0,1,2:T(8,128)S(1)} fusion(f32[64,8,512]{2,1,0:T(8,128)S(1)} %bitcast.112, f32[64]{0:T(128)S(1)} %broadcast_multiply_fusion.3, bf16[2,512,64]{1,2,0:T(8,128)(2,1)S(1)} %exponential_convert_fusion), kind=kOutput, calls=%fused_computation.17 | convolution fusion | flops 201392128 | bytes 1245696 | tf_op jit(solution)/shard_map/dot_general | solution.py:98
  148.5 0.2 bitcast_dynamic-update-slice_fusion
  148.7 0.1 broadcast_dynamic-update-slice_fusion.1
  148.8 0.1 broadcast_dynamic-update-slice_fusion
  148.9 0.2 copy.56
  149.1 28.0 %all_to_all.27 = f32[64,1,656]{2,1,0:T(1,128)S(1)} all-to-all(f32[64,1,656]{2,1,0:T(1,128)S(1)} %copy.56), channel_id=1, replica_groups=mesh['dp'=64,'mp'=8] {'dp'}, dimensions={0} | all-to-all | bytes 335872 | tf_op jit(solution)/shard_map/all_to_all | solution.py:120
  177.1 0.1 slice_reduce_fusion.2
  177.2 0.1 slice_reduce_fusion.1
  177.4 0.1 reduce_sum.165
  177.6 0.1 multiply_reduce_fusion.3
  177.7 0.7 rsqrt_multiply_fusion
  (35 shorter events, 0.3 us)
Async XLA Ops:
  0.0 0.9 copy-start
  3.6 1.7 copy-start.6
  5.3 3.2 %copy-start.7 = (s32[8]{0:T(128)S(1)}, s32[8]{0:T(128)}, u32[]{:S(2)}) copy-start(s32[8]{0:T(128)} %param.11) | copy-start | bytes 100
  5.3 3.2 %copy-start.1 = (bf16[512,1024]{1,0:T(8,128)(2,1)S(1)}, bf16[512,1024]{1,0:T(8,128)(2,1)}, u32[]{:S(2)}) copy-start(bf16[512,1024]{1,0:T(8,128)(2,1)} %param.8) | copy-start | bytes 3145732
  8.0 3.5 %copy-start.3 = (bf16[8,512,128]{1,2,0:T(8,128)(2,1)}, bf16[8,512,128]{1,2,0:T(8,128)(2,1)S(1)}, u32[]{:S(2)}) copy-start(bf16[8,512,128]{1,2,0:T(8,128)(2,1)S(1)} %get-tuple-element.21) | copy-start | bytes 3145732
  11.4 82.7 %all-to-all-start = ((bf16[64,2,8,1024]{3,2,1,0:T(8,128)(2,1)}), bf16[64,2,8,1024]{3,2,1,0:T(8,128)(2,1)S(1)}, u32[]{:S(2)}, u32[]{:S(2)}) async-start(bf16[64,2,8,1024]{3,2,1,0:T(8,128)(2,1)} %broadcast_in_dim.29), calls=%async_computation | async-start | bytes 4194304 | tf_op jit(solution)/shard_map/all_to_all | solution.py:48
  97.0 2.9 %copy-start.2 = (f32[512,512]{1,0:T(8,128)S(1)}, f32[512,512]{1,0:T(8,128)}, u32[]{:S(2)}) copy-start(f32[512,512]{1,0:T(8,128)} %fusion.12) | copy-start | bytes 3145732
  100.2 5.6 %copy-start.4 = (f32[512]{0:T(512)S(1)}, f32[512]{0:T(512)}, u32[]{:S(2)}) copy-start(f32[512]{0:T(512)} %param.13) | copy-start | bytes 6148
  100.2 5.6 %copy-start.5 = (f32[512]{0:T(512)S(1)}, f32[512]{0:T(512)}, u32[]{:S(2)}) copy-start(f32[512]{0:T(512)} %param.12) | copy-start | bytes 6148
  101.8 30.5 %all-to-all-start.1 = ((f32[2,512,8,64]{1,3,0,2:T(8,128)}), f32[2,512,8,64]{1,3,0,2:T(8,128)S(1)}, u32[]{:S(2)}, u32[]{:S(2)}) async-start(f32[2,512,8,64]{1,3,0,2:T(8,128)} %copy.51), calls=%async_computation.1 | async-start | bytes 4194304 | tf_op jit(solution)/shard_map/all_to_all | solution.py:80
  133.4 12.1 %all-to-all-start.2 = ((bf16[8,512,64]{1,2,0:T(8,128)(2,1)}), bf16[8,512,64]{1,2,0:T(8,128)(2,1)S(1)}, u32[]{:S(2)}, u32[]{:S(2)}) async-start(bf16[8,512,64]{1,2,0:T(8,128)(2,1)} %broadcast_in_dim.31), calls=%async_computation.2 | async-start | bytes 1048576 | tf_op jit(solution)/shard_map/all_to_all | solution.py:48

commit v2 on v1

--- a/solution.py
+++ b/solution.py
@@ -3,13 +3,18 @@
 import jax
 import jax.numpy as jnp
 from jax import lax
-from jax.sharding import PartitionSpec as P
+from jax.sharding import Mesh, PartitionSpec as P
 
 D = 8192
 HEAD_DIM = 128
 
 
 EPSILON = 1e-06
+
+CHIPS = ("z", "y_hi")
+CORE = "core"
+DATA = CHIPS + (CORE,)
+MODEL = ("x", "y_lo")
 
 
 def attend(queries, key_rows, value_rows):
@@ -42,6 +47,44 @@
     )
 
 
+def attend_rows(queries, key_rows, value_rows, rows):
+    length = queries.shape[0]
+    kv_heads = key_rows.shape[1] // HEAD_DIM
+    group_size = queries.shape[1] // HEAD_DIM // kv_heads
+    picked = jnp.take(queries, rows, axis=0)
+    query_four = picked.reshape(rows.shape[0], kv_heads, group_size, HEAD_DIM)
+    key_three = key_rows.reshape(length, kv_heads, HEAD_DIM)
+    value_three = value_rows.reshape(length, kv_heads, HEAD_DIM)
+    scores = jnp.einsum(
+        "tkgd,skd->kgts", query_four, key_three, preferred_element_type=jnp.float32
+    ) / math.sqrt(HEAD_DIM)
+    column_position = lax.broadcasted_iota(jnp.int32, (rows.shape[0], length), 1)
+    scores = jnp.where(column_position <= rows[:, None], scores, -jnp.inf)
+    weights = jax.nn.softmax(scores, axis=-1).astype(jnp.bfloat16)
+    mixture = jnp.einsum(
+        "kgts,skd->tkgd", weights, value_three, preferred_element_type=jnp.float32
+    )
+    return mixture.astype(jnp.bfloat16).reshape(rows.shape[0], queries.shape[1])
+
+
+def swap_cores(piece):
+    return lax.ppermute(piece, CORE, [(0, 1), (1, 0)])
+
+
+def gather_marks(query_marks, output_marks):
+    core = lax.axis_index(CORE)
+    own = jnp.stack([query_marks, output_marks])
+    other = swap_cores(own)
+    first = core == 0
+    pair = jnp.where(first, jnp.stack([own, other], 1), jnp.stack([other, own], 1))
+    mine = jnp.where(first, pair[0], pair[1])
+    fetched = broadcast_gather(mine, CHIPS)
+    swapped = swap_cores(fetched)
+    query_rows = jnp.where(first, fetched, swapped)
+    output_rows = jnp.where(first, swapped, fetched)
+    return jnp.stack([query_rows, output_rows])
+
+
 def broadcast_gather(piece, axis_name):
     count = lax.axis_size(axis_name)
     spread = jnp.broadcast_to(piece[None], (count,) + piece.shape)
@@ -50,24 +93,21 @@
 
 def shards(queries, key_rows, value_rows, landmark_index, radius_in, radius_out):
     length = queries.shape[0]
-    model_count = lax.axis_size("mp")
-    data_count = lax.axis_size("dp")
-    model_index = lax.axis_index("mp")
+    model_count = lax.axis_size(MODEL)
+    data_count = lax.axis_size(DATA)
+    model_index = lax.axis_index(MODEL)
     landmarks = radius_in.shape[0]
     row_share = landmarks // model_count
     column_share = landmarks // data_count
     token_count = length * data_count
 
+    own_rows = landmark_index % length
+    gathered = gather_marks(
+        jnp.take(queries, own_rows, axis=0),
+        attend_rows(queries, key_rows, value_rows, own_rows),
+    )
+    landmark_piece = gathered.reshape(2, landmarks, queries.shape[1])
     attended = attend(queries, key_rows, value_rows)
-
-    own_rows = landmark_index % length
-    landmark_rows = jnp.stack(
-        [jnp.take(queries, own_rows, axis=0), jnp.take(attended, own_rows, axis=0)]
-    )
-    gathered = broadcast_gather(landmark_rows, "dp")
-    landmark_piece = jnp.transpose(gathered, (1, 0, 2, 3)).reshape(
-        2, landmarks, queries.shape[1]
-    )
 
     row_norms = jnp.stack([squares_by_row(queries), squares_by_row(attended)])
     mark_norms = squares_by_row(landmark_piece)
@@ -77,7 +117,7 @@
     distance_part = row_norms[:, :, None] + mark_norms[:, None, :] - 2.0 * cross
     distance_part = distance_part.reshape(2, length, model_count, row_share)
     distance = jnp.sum(
-        lax.all_to_all(distance_part, "mp", 2, 2, tiled=True), axis=2
+        lax.all_to_all(distance_part, MODEL, 2, 2, tiled=True), axis=2
     )
 
     widths = lax.dynamic_slice_in_dim(
@@ -86,7 +126,7 @@
     features = jnp.exp(-distance / (D * widths[:, None, :])).astype(jnp.bfloat16)
     row_features = features[0]
     column_features = jnp.transpose(
-        broadcast_gather(features[1], "mp"), (1, 0, 2)
+        broadcast_gather(features[1], MODEL), (1, 0, 2)
     ).reshape(length, landmarks)
 
     rows32 = row_features.astype(jnp.float32)
@@ -117,7 +157,7 @@
         ],
         axis=1,
     )
-    received = lax.all_to_all(packed, "dp", 0, 0, tiled=True)
+    received = lax.all_to_all(packed, DATA, 0, 0, tiled=True)
     cut = row_share * column_share
     second_parts = received[:, :cut].reshape(data_count, row_share, column_share)
     row_means = received[:, cut : cut + row_share]
@@ -142,10 +182,13 @@
 
 
 def solution(mesh):
+    data_count, model_count = mesh.devices.shape
+    chips = mesh.devices.reshape(data_count // 8, 4, 2, model_count // 2, 2)
+    split = Mesh(chips, DATA + MODEL)
     return jax.shard_map(
         shards,
-        mesh=mesh,
-        in_specs=(P("dp", "mp"), P("dp", "mp"), P("dp", "mp"), P("dp"), P(), P()),
-        out_specs=P("mp", "dp"),
+        mesh=split,
+        in_specs=(P(DATA, MODEL), P(DATA, MODEL), P(DATA, MODEL), P(DATA), P(), P()),
+        out_specs=P(MODEL, DATA),
         check_vma=False,
     )

time: 179 us -> 147 us (0.82)
  waiting for transfers between devices: 99.2 us -> 61 us
  starting transfers between devices: 25.3 us -> 31.8 us
  blocking collectives: 28 us -> 22.4 us
  matrix products: 11.4 us -> 14.6 us
    all_to_all x2, waiting for transfers between devices: 72.8 us -> 33.4 us  [broadcast_gather(): return lax.all_to_all(spread, axis_name, 0, 0, tiled=True)]
    ppermute x0 -> x2, starting transfers between devices: none -> 13.7 us  [swap_cores(): return lax.ppermute(piece, CORE, [(0, 1), (1, 0)])]
    all_to_all x2, starting transfers between devices: 21.3 us -> 14 us  [broadcast_gather(): return lax.all_to_all(spread, axis_name, 0, 0, tiled=True)]
    all_to_all x1, blocking collectives: 28 us -> 22.4 us  [shards(): received = lax.all_to_all(packed, DATA, 0, 0, tiled=True)]
    dot_general x1, matrix products: 2.59 us -> 6.86 us  [attend(): jnp.einsum('kgts,skd->tkgd', weights, value_three, preferred_element_type...]
    unnamed x21 -> x17, local copies, waits for them, and re-layouts: 1.18 us -> 3.55 us
  transfers between devices with their start and end apart: 3 -> 5, of which waited for: 3 -> 4; matrix products, arithmetic and copies ran while one was open for 0% -> 8% of each run, Pallas kernels for 0% -> 0%
where the time goes in v2:
time: 147 us
  waiting for transfers between devices  61 us (41%)
  starting transfers between devices  31.8 us (22%)
  blocking collectives  22.4 us (15%)
  matrix products  14.6 us (10%)
  local copies, waits for them, and re-layouts  9.86 us (7%)
  other arithmetic  6.67 us (5%)
    all_to_all x2, waiting for transfers between devices, broadcast_gather(): return lax.all_to_all(spread, axis_name, 0, 0, tiled=True)  33.4 us
    all_to_all x1, waiting for transfers between devices, shards(): lax.all_to_all(distance_part, MODEL, 2, 2, tiled=True)  26.7 us
    all_to_all x1, blocking collectives, shards(): received = lax.all_to_all(packed, DATA, 0, 0, tiled=True)  22.4 us
    all_to_all x2, starting transfers between devices, broadcast_gather(): return lax.all_to_all(spread, axis_name, 0, 0, tiled=True)  14 us
    ppermute x2, starting transfers between devices, swap_cores(): return lax.ppermute(piece, CORE, [(0, 1), (1, 0)])  13.7 us
    dot_general x1, matrix products, attend(): jnp.einsum('kgts,skd->tkgd', weights, value_three, preferred_element_type...  6.86 us
    all_to_all x1, starting transfers between devices, shards(): lax.all_to_all(distance_part, MODEL, 2, 2, tiled=True)  4.02 us
    unnamed x17, local copies, waits for them, and re-layouts  3.55 us
  transfers between devices with their start and end apart: 5, of which 4 were waited for; matrix products, arithmetic and copies ran while one was open for 8% of the time, Pallas kernels for 0%

profile of v2, /device:TPU:1, one launch (start us, length us, event | category | flops | bytes accessed | tf_op | source)
XLA Modules:
  0.0 146.6 jit_solution(16576086597211836817)
XLA Ops:
  0.0 0.8 compare_and_fusion
  0.9 1.9 %gather_fusion = bf16[8,1024]{1,0:T(8,128)(2,1)S(1)} fusion(bf16[512,1024]{1,0:T(8,128)(2,1)} %param.8, s32[1024]{0:T(1024)S(1)} %pad_clamp_fusion), kind=kCustom, calls=%fused_computation.clone | custom fusion | bytes 32800 | tf_op jit(solution)/shard_map/jit(_take)/gather | solution.py:106
  2.8 0.1 fusion.35
  2.9 0.3 fusion.42
  3.1 0.2 fusion.27
  3.3 0.1 fusion.30
  3.4 1.1 fusion.11
  4.5 8.8 %collective-permute-start = (bf16[2,8,1024]{2,1,0:T(8,128)(2,1)S(1)}, bf16[2,8,1024]{2,1,0:T(8,128)(2,1)S(1)}, u32[]{:S(2)}, u32[]{:S(2)}) collective-permute-start(bf16[2,8,1024]{2,1,0:T(8,128)(2,1)S(1)} %get-tuple-element.19), channel_id=1, source_target_pairs={{0,8},{8,0},{1,9},{9,1},{2,10},{10,2},{3,11},{11,3},{4,12},{12,4},... | collective-permute-start | bytes 98312 | tf_op jit(solution)/shard_map/ppermute | solution.py:71
  13.3 0.8 collective-permute-done
  14.2 1.2 broadcast_in_dim.42
  15.4 10.3 %all-to-all-start = ((bf16[32,2,8,1024]{3,2,1,0:T(8,128)(2,1)}), bf16[32,2,8,1024]{3,2,1,0:T(8,128)(2,1)S(1)}, u32[]{:S(2)}, u32[]{:S(2)}) async-start(bf16[32,2,8,1024]{3,2,1,0:T(8,128)(2,1)} %broadcast_in_dim.42), calls=%async_computation | async-start | bytes 2097152 | tf_op jit(solution)/shard_map/all_to_all | solution.py:91
  25.7 0.1 iota_compare_fusion
  25.8 0.3 multiply_reduce_fusion.2
  26.1 1.7 %fusion.1 = (f32[8,512]{1,0:T(8,128)S(1)}, f32[512,512,8]{1,0,2:T(8,128)S(1)}) fusion(pred[512,512]{0,1:T(8,128)(4,1)S(1)} %iota_compare_fusion, bf16[512,128]{1,0:T(8,128)(2,1)S(1)} %copy-done, bf16[512,1024]{1,0:T(8,128)(2,1)S(1)} %copy-done.2), kind=kOutput, calls=%fused_computation.5 | convolution fusion | flops 543158272 | bytes 9846784 | tf_op jit(solution)/shard_map/tkgd,skd->kgts/dot_general | solution.py:27
  27.8 3.2 %copy-done.1 = f32[512,512,8]{1,0,2:T(8,128)} copy-done((f32[512,512,8]{1,0,2:T(8,128)}, f32[512,512,8]{1,0,2:T(8,128)S(1)}, u32[]{:S(2)}) %copy-start.1) | copy-done | bytes 8388632
  31.0 1.7 %fusion = f32[8,512]{1,0:T(8,128)S(1)} fusion(f32[512,512,8]{1,0,2:T(8,128)S(1)} %get-tuple-element.23, f32[8,512]{1,0:T(8,128)S(1)} %get-tuple-element.22, pred[512,512]{0,1:T(8,128)(4,1)S(1)} %iota_compare_fusion), kind=kLoop, calls=%fused_computation.4 | loop fusion | flops 8384512 | bytes 8683520 | tf_op jit(solution)/shard_map/reduce_sum | solution.py:33
  32.7 25.0 %all-to-all-done = bf16[32,2,8,1024]{3,2,1,0:T(8,128)(2,1)S(1)} async-done(((bf16[32,2,8,1024]{3,2,1,0:T(8,128)(2,1)}), bf16[32,2,8,1024]{3,2,1,0:T(8,128)(2,1)S(1)}, u32[]{:S(2)}, u32[]{:S(2)}) %all-to-all-start) | async-done | bytes 1048608 | tf_op jit(solution)/shard_map/all_to_all | solution.py:91
  57.7 5.0 %collective-permute-start.1 = (bf16[32,2,8,1024]{3,2,1,0:T(8,128)(2,1)S(1)}, bf16[32,2,8,1024]{3,2,1,0:T(8,128)(2,1)S(1)}, u32[]{:S(2)}, u32[]{:S(2)}) collective-permute-start(bf16[32,2,8,1024]{3,2,1,0:T(8,128)(2,1)S(1)} %all-to-all-done), channel_id=1, source_target_pairs={{0,8},{8,0},{1,9},{9,1},{2,10},{10,2},{3,11},{11,3},{4,12},{12,4},... | collective-permute-start | bytes 3145736 | tf_op jit(solution)/shard_map/ppermute | solution.py:71
  62.6 6.9 %multiply_reduce_fusion.1 = (f32[512]{0:T(512)S(1)}, bf16[8,512,128]{1,2,0:T(8,128)(2,1)}) fusion(bf16[512,128]{1,0:T(8,128)(2,1)S(1)} %copy-done.3, f32[8,512]{1,0:T(8,128)S(1)} %fusion, f32[8,512]{1,0:T(8,128)S(1)} %get-tuple-element.22, f32[512,512,8]{1,0,2:T(8,128)} %copy-done.1, pred[512,512]{0,1:T(8,128)(4,1)S(1)} %iota_compare_fusion), kind=kOutput, calls=%fused_computation.12 | convolution fusion | flops 549453312 | bytes 9865216 | tf_op jit(solution)/shard_map/kgts,skd->tkgd/dot_general | solution.py:34
  69.5 0.1 broadcast_select_fusion.1
  69.7 0.7 fusion.43
  70.4 0.5 multiply_reduce_fusion
  70.9 0.1 add.67
  71.0 1.9 %convolution_bitcast_fusion = f32[1,512,8,64]{1,3,2,0:T(8,128)S(1)} fusion(bf16[512,1024,1]{0,1,2:T(8,128)(2,1)} %bitcast.156, bf16[8,64,1024]{2,1,0:T(8,128)(2,1)S(1)} %bitcast.140), kind=kOutput, calls=%fused_computation.15 | convolution fusion | flops 536870912 | bytes 3145728 | tf_op jit(solution)/shard_map/dot_general | solution.py:45
  72.9 0.3 fusion.5
  73.3 1.6 %copy.46 = f32[2,512,8,64]{1,3,0,2:T(8,128)} copy(f32[2,512,8,64]{1,3,2,0:T(8,128)S(1)} %fusion.5) | data formatting | bytes 4194304 | tf_op jit(solution)/shard_map/sub | solution.py:117
  74.8 4.0 %all-to-all-start.1 = ((f32[2,512,8,64]{1,3,0,2:T(8,128)}), f32[2,512,8,64]{1,3,0,2:T(8,128)S(1)}, u32[]{:S(2)}, u32[]{:S(2)}) async-start(f32[2,512,8,64]{1,3,0,2:T(8,128)} %copy.46), calls=%async_computation.1 | async-start | bytes 4194304 | tf_op jit(solution)/shard_map/all_to_all | solution.py:120
  78.9 0.1 fusion.37
  79.0 26.7 %all-to-all-done.1 = f32[2,512,8,64]{1,3,0,2:T(8,128)S(1)} async-done(((f32[2,512,8,64]{1,3,0,2:T(8,128)}), f32[2,512,8,64]{1,3,0,2:T(8,128)S(1)}, u32[]{:S(2)}, u32[]{:S(2)}) %all-to-all-start.1) | async-done | bytes 2097184 | tf_op jit(solution)/shard_map/all_to_all | solution.py:120
  105.7 0.2 reduce_sum.169
  105.9 0.1 exponential_convert_fusion
  106.1 0.8 broadcast_in_dim.44
  106.9 3.7 %all-to-all-start.2 = ((bf16[8,512,64]{1,2,0:T(8,128)(2,1)}), bf16[8,512,64]{1,2,0:T(8,128)(2,1)S(1)}, u32[]{:S(2)}, u32[]{:S(2)}) async-start(bf16[8,512,64]{1,2,0:T(8,128)(2,1)} %broadcast_in_dim.44), calls=%async_computation.2 | async-start | bytes 1048576 | tf_op jit(solution)/shard_map/all_to_all | solution.py:91
  110.6 0.1 convert_reduce_fusion
  110.7 0.2 fusion.22
  110.9 8.5 %all-to-all-done.2 = bf16[8,512,64]{1,2,0:T(8,128)(2,1)S(1)} async-done(((bf16[8,512,64]{1,2,0:T(8,128)(2,1)}), bf16[8,512,64]{1,2,0:T(8,128)(2,1)S(1)}, u32[]{:S(2)}, u32[]{:S(2)}) %all-to-all-start.2) | async-done | bytes 524320 | tf_op jit(solution)/shard_map/all_to_all | solution.py:91
  119.3 0.1 bitcast_reduce_fusion
  119.6 0.1 bitcast_subtract_fusion
  119.8 2.1 %convolution_bitcast_fusion.1 = f32[64,64,8]{0,1,2:T(8,128)S(1)} fusion(f32[64,8,512]{2,1,0:T(8,128)S(1)} %bitcast.143, f32[64]{0:T(128)S(1)} %broadcast_multiply_fusion.3, bf16[2,512,64]{1,2,0:T(8,128)(2,1)S(1)} %exponential_convert_fusion), kind=kOutput, calls=%fused_computation.16 | convolution fusion | flops 201392128 | bytes 1245696 | tf_op jit(solution)/shard_map/dot_general | solution.py:138
  121.9 0.2 bitcast_dynamic-update-slice_fusion
  122.2 0.3 fusion.16
  122.7 0.2 copy.51
  122.9 22.4 %all_to_all.27 = f32[64,1,656]{2,1,0:T(1,128)S(1)} all-to-all(f32[64,1,656]{2,1,0:T(1,128)S(1)} %copy.51), channel_id=1, replica_groups=mesh['z'=8,'y_hi'=4,'core'=2,'x'=4,'y_lo'=2] {'z','y_hi','core'}, dimensions={0} | all-to-all | bytes 335872 | tf_op jit(solution)/shard_map/all_to_all | solution.py:160
  145.3 0.1 slice_reduce_fusion.1
  145.4 0.1 slice_reduce_fusion.2
  145.5 0.1 reduce_sum.175
  145.8 0.1 multiply_reduce_fusion.3
  145.9 0.7 rsqrt_multiply_fusion
  (40 shorter events, 0.8 us)
Async XLA Ops:
  0.0 2.9 %copy-start = (bf16[512,128]{1,0:T(8,128)(2,1)S(1)}, bf16[512,128]{1,0:T(8,128)(2,1)}, u32[]{:S(2)}) copy-start(bf16[512,128]{1,0:T(8,128)(2,1)} %param.9) | copy-start | bytes 393220
  0.0 25.8 %copy-start.2 = (bf16[512,1024]{1,0:T(8,128)(2,1)S(1)}, bf16[512,1024]{1,0:T(8,128)(2,1)}, u32[]{:S(2)}) copy-start(bf16[512,1024]{1,0:T(8,128)(2,1)} %param.8) | copy-start | bytes 3145732
  4.5 9.6 %collective-permute-start = (bf16[2,8,1024]{2,1,0:T(8,128)(2,1)S(1)}, bf16[2,8,1024]{2,1,0:T(8,128)(2,1)S(1)}, u32[]{:S(2)}, u32[]{:S(2)}) collective-permute-start(bf16[2,8,1024]{2,1,0:T(8,128)(2,1)S(1)} %get-tuple-element.19), channel_id=1, source_target_pairs={{0,8},{8,0},{1,9},{9,1},{2,10},{10,2},{3,11},{11,3},{4,12},{12,4},... | collective-permute-start | bytes 98312 | tf_op jit(solution)/shard_map/ppermute | solution.py:71
  15.4 42.3 %all-to-all-start = ((bf16[32,2,8,1024]{3,2,1,0:T(8,128)(2,1)}), bf16[32,2,8,1024]{3,2,1,0:T(8,128)(2,1)S(1)}, u32[]{:S(2)}, u32[]{:S(2)}) async-start(bf16[32,2,8,1024]{3,2,1,0:T(8,128)(2,1)} %broadcast_in_dim.42), calls=%async_computation | async-start | bytes 2097152 | tf_op jit(solution)/shard_map/all_to_all | solution.py:91
  27.7 3.2 %copy-start.1 = (f32[512,512,8]{1,0,2:T(8,128)}, f32[512,512,8]{1,0,2:T(8,128)S(1)}, u32[]{:S(2)}) copy-start(f32[512,512,8]{1,0,2:T(8,128)S(1)} %get-tuple-element.23) | copy-start | bytes 25165828
  31.0 31.7 %copy-start.3 = (bf16[512,128]{1,0:T(8,128)(2,1)S(1)}, bf16[512,128]{1,0:T(8,128)(2,1)}, u32[]{:S(2)}) copy-start(bf16[512,128]{1,0:T(8,128)(2,1)} %param.10) | copy-start | bytes 393220
  57.7 11.9 %collective-permute-start.1 = (bf16[32,2,8,1024]{3,2,1,0:T(8,128)(2,1)S(1)}, bf16[32,2,8,1024]{3,2,1,0:T(8,128)(2,1)S(1)}, u32[]{:S(2)}, u32[]{:S(2)}) collective-permute-start(bf16[32,2,8,1024]{3,2,1,0:T(8,128)(2,1)S(1)} %all-to-all-done), channel_id=1, source_target_pairs={{0,8},{8,0},{1,9},{9,1},{2,10},{10,2},{3,11},{11,3},{4,12},{12,4},... | collective-permute-start | bytes 3145736 | tf_op jit(solution)/shard_map/ppermute | solution.py:71
  73.2 5.6 %copy-start.4 = (f32[512]{0:T(512)S(1)}, f32[512]{0:T(512)}, u32[]{:S(2)}) copy-start(f32[512]{0:T(512)} %param.13) | copy-start | bytes 6148
  73.2 5.6 %copy-start.5 = (f32[512]{0:T(512)S(1)}, f32[512]{0:T(512)}, u32[]{:S(2)}) copy-start(f32[512]{0:T(512)} %param.12) | copy-start | bytes 6148
  74.8 30.8 %all-to-all-start.1 = ((f32[2,512,8,64]{1,3,0,2:T(8,128)}), f32[2,512,8,64]{1,3,0,2:T(8,128)S(1)}, u32[]{:S(2)}, u32[]{:S(2)}) async-start(f32[2,512,8,64]{1,3,0,2:T(8,128)} %copy.46), calls=%async_computation.1 | async-start | bytes 4194304 | tf_op jit(solution)/shard_map/all_to_all | solution.py:120
  106.9 12.5 %all-to-all-start.2 = ((bf16[8,512,64]{1,2,0:T(8,128)(2,1)}), bf16[8,512,64]{1,2,0:T(8,128)(2,1)S(1)}, u32[]{:S(2)}, u32[]{:S(2)}) async-start(bf16[8,512,64]{1,2,0:T(8,128)(2,1)} %broadcast_in_dim.44), calls=%async_computation.2 | async-start | bytes 1048576 | tf_op jit(solution)/shard_map/all_to_all | solution.py:91

commit v3 on v2

--- a/solution.py
+++ b/solution.py
@@ -71,18 +71,31 @@
     return lax.ppermute(piece, CORE, [(0, 1), (1, 0)])
 
 
-def gather_marks(query_marks, output_marks):
-    core = lax.axis_index(CORE)
-    own = jnp.stack([query_marks, output_marks])
-    other = swap_cores(own)
-    first = core == 0
-    pair = jnp.where(first, jnp.stack([own, other], 1), jnp.stack([other, own], 1))
-    mine = jnp.where(first, pair[0], pair[1])
-    fetched = broadcast_gather(mine, CHIPS)
-    swapped = swap_cores(fetched)
-    query_rows = jnp.where(first, fetched, swapped)
-    output_rows = jnp.where(first, swapped, fetched)
-    return jnp.stack([query_rows, output_rows])
+def by_core(first, own_core, other_core, axis):
+    return jnp.where(
+        first,
+        jnp.stack([own_core, other_core], axis),
+        jnp.stack([other_core, own_core], axis),
+    )
+
+
+def merge_pair(count, second, row_mean, row_square, column_mean, column_square):
+    pieces = (second, row_mean, row_square, column_mean, column_square)
+    flat = swap_cores(jnp.concatenate([piece.reshape(-1) for piece in pieces]))
+    other, start = [], 0
+    for piece in pieces:
+        other.append(flat[start : start + piece.size].reshape(piece.shape))
+        start += piece.size
+    row_gap = row_mean - other[1]
+    column_gap = column_mean - other[3]
+    half = 0.5 * count
+    return (
+        second + other[0] + half * row_gap[:, None] * column_gap[None, :],
+        0.5 * (row_mean + other[1]),
+        row_square + other[2] + half * jnp.square(row_gap),
+        0.5 * (column_mean + other[3]),
+        column_square + other[4] + half * jnp.square(column_gap),
+    )
 
 
 def broadcast_gather(piece, axis_name):
@@ -101,20 +114,34 @@
     column_share = landmarks // data_count
     token_count = length * data_count
 
+    first = lax.axis_index(CORE) == 0
     own_rows = landmark_index % length
-    gathered = gather_marks(
-        jnp.take(queries, own_rows, axis=0),
-        attend_rows(queries, key_rows, value_rows, own_rows),
-    )
-    landmark_piece = gathered.reshape(2, landmarks, queries.shape[1])
+    marks = jnp.stack(
+        [
+            jnp.take(queries, own_rows, axis=0),
+            attend_rows(queries, key_rows, value_rows, own_rows),
+        ],
+        1,
+    )
+    fetched = broadcast_gather(marks, CHIPS)
+    swapped = swap_cores(fetched)
     attended = attend(queries, key_rows, value_rows)
-
-    row_norms = jnp.stack([squares_by_row(queries), squares_by_row(attended)])
-    mark_norms = squares_by_row(landmark_piece)
-    cross = jnp.stack(
-        [inner_rows(queries, landmark_piece[0]), inner_rows(attended, landmark_piece[1])]
-    )
-    distance_part = row_norms[:, :, None] + mark_norms[:, None, :] - 2.0 * cross
+    rows = jnp.stack([queries, attended])
+    row_norms = squares_by_row(rows)
+
+    def part_of(piece):
+        marks_of = [piece[:, :, kind].reshape(-1, queries.shape[1]) for kind in range(2)]
+        return jnp.stack(
+            [
+                squares_by_row(marks_of[kind])[None, :]
+                - 2.0 * inner_rows(rows[kind], marks_of[kind])
+                for kind in range(2)
+            ]
+        ).reshape(2, length, -1, marks.shape[0])
+
+    distance_part = row_norms[:, :, None, None, None] + by_core(
+        first, part_of(fetched), part_of(swapped), 3
+    )
     distance_part = distance_part.reshape(2, length, model_count, row_share)
     distance = jnp.sum(
         lax.all_to_all(distance_part, MODEL, 2, 2, tiled=True), axis=2
@@ -145,25 +172,35 @@
     row_square = jnp.sum(jnp.square(rows_centered), axis=0)
     column_square = jnp.sum(jnp.square(columns_centered), axis=0)
 
+    second, row_mean, row_square, column_mean, column_square = merge_pair(
+        length, second, row_mean, row_square, column_mean, column_square
+    )
+    chip_count = data_count // 2
+
+    def for_core(values):
+        split = values.reshape(values.shape[:-1] + (chip_count, 2, column_share))
+        return jnp.where(first, split[..., 0, :], split[..., 1, :])
+
     packed = jnp.concatenate(
         [
-            jnp.transpose(
-                second.reshape(row_share, data_count, column_share), (1, 0, 2)
-            ).reshape(data_count, row_share * column_share),
-            jnp.broadcast_to(row_mean[None], (data_count, row_share)),
-            jnp.broadcast_to(row_square[None], (data_count, row_share)),
-            column_mean.reshape(data_count, column_share),
-            column_square.reshape(data_count, column_share),
+            jnp.transpose(for_core(second), (1, 0, 2)).reshape(
+                chip_count, row_share * column_share
+            ),
+            jnp.broadcast_to(row_mean[None], (chip_count, row_share)),
+            jnp.broadcast_to(row_square[None], (chip_count, row_share)),
+            for_core(column_mean),
+            for_core(column_square),
         ],
         axis=1,
     )
-    received = lax.all_to_all(packed, DATA, 0, 0, tiled=True)
+    received = lax.all_to_all(packed, CHIPS, 0, 0, tiled=True)
     cut = row_share * column_share
-    second_parts = received[:, :cut].reshape(data_count, row_share, column_share)
+    second_parts = received[:, :cut].reshape(chip_count, row_share, column_share)
     row_means = received[:, cut : cut + row_share]
     row_squares = received[:, cut + row_share : cut + 2 * row_share]
     column_means = received[:, cut + 2 * row_share : cut + 2 * row_share + column_share]
     column_squares = received[:, cut + 2 * row_share + column_share :]
+    length = 2 * length
 
     row_shift = row_means - jnp.mean(row_means, axis=0)[None, :]
     column_shift = column_means - jnp.mean(column_means, axis=0)[None, :]

time: 147 us -> 151 us (1.027)
  blocking collectives: 22.4 us -> 17 us
  local copies, waits for them, and re-layouts: 9.86 us -> 13.1 us
  matrix products: 14.6 us -> 17.6 us
  other arithmetic: 6.67 us -> 8.38 us
    all_to_all x2, starting transfers between devices: 14 us -> 20 us  [broadcast_gather(): return lax.all_to_all(spread, axis_name, 0, 0, tiled=True)]
    all_to_all x1, blocking collectives: 22.4 us -> 17 us  [shards(): received = lax.all_to_all(packed, CHIPS, 0, 0, tiled=True)]
    ppermute x2, starting transfers between devices: 13.7 us -> 9 us  [swap_cores(): return lax.ppermute(piece, CORE, [(0, 1), (1, 0)])]
    dot_general x2 -> x4, matrix products: 2.68 us -> 6.74 us  [inner_rows(): lax.dot_general(left, right, (((1,), (1,)), ((), ())), preferred_element_...]
    add x1 -> x2, local copies, waits for them, and re-layouts: 0.08 us -> 1.7 us  [the longest x1 1.58 us: shards(): row_norms[:, :, None, None, None]]
    reduce_sum x2 -> x3, other arithmetic: 0.77 us -> 2.33 us  [squares_by_row(): return jnp.sum(jnp.square(matrix.astype(jnp.float32)), axis=-1)]
    unnamed x17 -> x20, local copies, waits for them, and re-layouts: 3.55 us -> 3.29 us
  transfers between devices with their start and end apart: 5 -> 5, of which waited for: 4 -> 4; matrix products, arithmetic and copies ran while one was open for 8% -> 11% of each run, Pallas kernels for 0% -> 0%
where the time goes in v3:
time: 151 us; the launch traced here: 150 us
  waiting for transfers between devices  60.7 us (40%)
  starting transfers between devices  33 us (22%)
  matrix products  17.6 us (12%)
  blocking collectives  17 us (11%)
  local copies, waits for them, and re-layouts  13.1 us (9%)
  other arithmetic  8.38 us (6%)
    all_to_all x2, waiting for transfers between devices, broadcast_gather(): return lax.all_to_all(spread, axis_name, 0, 0, tiled=True)  33.2 us
    all_to_all x1, waiting for transfers between devices, shards(): lax.all_to_all(distance_part, MODEL, 2, 2, tiled=True)  26.7 us
    all_to_all x2, starting transfers between devices, broadcast_gather(): return lax.all_to_all(spread, axis_name, 0, 0, tiled=True)  20 us
    all_to_all x1, blocking collectives, shards(): received = lax.all_to_all(packed, CHIPS, 0, 0, tiled=True)  17 us
    ppermute x2, starting transfers between devices, swap_cores(): return lax.ppermute(piece, CORE, [(0, 1), (1, 0)])  9 us
    dot_general x4, matrix products, inner_rows(): lax.dot_general(left, right, (((1,), (1,)), ((), ())), preferred_element_...  6.74 us
    dot_general x1, matrix products, attend(): jnp.einsum('kgts,skd->tkgd', weights, value_three, preferred_element_type...  6.69 us
    all_to_all x1, starting transfers between devices, shards(): lax.all_to_all(distance_part, MODEL, 2, 2, tiled=True)  3.97 us
  transfers between devices with their start and end apart: 5, of which 4 were waited for; matrix products, arithmetic and copies ran while one was open for 11% of the time, Pallas kernels for 0%

profile of v3, /device:TPU:1, one launch (start us, length us, event | category | flops | bytes accessed | tf_op | source)
XLA Modules:
  0.0 150.2 jit_solution(17591024143425929126)
XLA Ops:
  0.0 0.8 compare_and_fusion
  0.9 1.9 %gather_fusion = bf16[8,1024]{1,0:T(8,128)(2,1)S(1)} fusion(bf16[512,1024]{1,0:T(8,128)(2,1)} %param.8, s32[1024]{0:T(1024)S(1)} %pad_clamp_fusion), kind=kCustom, calls=%fused_computation.clone | custom fusion | bytes 32800 | tf_op jit(solution)/shard_map/jit(_take)/gather | solution.py:121
  2.9 0.3 fusion.56
  3.1 0.2 fusion.41
  3.3 0.1 fusion.44
  3.4 1.1 fusion.18
  4.5 1.2 broadcast_in_dim.39
  5.7 16.5 %all-to-all-start = ((bf16[32,8,2,1024]{3,1,2,0:T(8,128)(2,1)}), bf16[32,8,2,1024]{3,1,2,0:T(8,128)(2,1)S(1)}, u32[]{:S(2)}, u32[]{:S(2)}) async-start(bf16[32,8,2,1024]{3,1,2,0:T(8,128)(2,1)} %broadcast_in_dim.39), calls=%async_computation | async-start | bytes 2097152 | tf_op jit(solution)/shard_map/all_to_all | solution.py:104
  22.3 1.7 %fusion.1 = (f32[8,512]{1,0:T(8,128)S(1)}, f32[512,512,8]{1,0,2:T(8,128)S(1)}) fusion(pred[512,512]{0,1:T(8,128)(4,1)S(1)} %iota_compare_fusion, bf16[512,128]{1,0:T(8,128)(2,1)S(1)} %copy-done, bf16[512,1024]{1,0:T(8,128)(2,1)S(1)} %copy-done.2), kind=kOutput, calls=%fused_computation.5 | convolution fusion | flops 543158272 | bytes 9846784 | tf_op jit(solution)/shard_map/tkgd,skd->kgts/dot_general | solution.py:27
  24.0 3.2 %copy-done.1 = f32[512,512,8]{1,0,2:T(8,128)} copy-done((f32[512,512,8]{1,0,2:T(8,128)}, f32[512,512,8]{1,0,2:T(8,128)S(1)}, u32[]{:S(2)}) %copy-start.1) | copy-done | bytes 8388632
  27.2 1.7 %fusion = f32[8,512]{1,0:T(8,128)S(1)} fusion(f32[512,512,8]{1,0,2:T(8,128)S(1)} %get-tuple-element.33, f32[8,512]{1,0:T(8,128)S(1)} %get-tuple-element.32, pred[512,512]{0,1:T(8,128)(4,1)S(1)} %iota_compare_fusion), kind=kLoop, calls=%fused_computation.4 | loop fusion | flops 8384512 | bytes 8683520 | tf_op jit(solution)/shard_map/reduce_sum | solution.py:33
  29.0 24.6 %all-to-all-done = bf16[32,8,2,1024]{3,1,2,0:T(8,128)(2,1)S(1)} async-done(((bf16[32,8,2,1024]{3,1,2,0:T(8,128)(2,1)}), bf16[32,8,2,1024]{3,1,2,0:T(8,128)(2,1)S(1)}, u32[]{:S(2)}, u32[]{:S(2)}) %all-to-all-start) | async-done | bytes 1048608 | tf_op jit(solution)/shard_map/all_to_all | solution.py:104
  53.6 1.1 copy.59
  54.6 5.1 %collective-permute-start = (bf16[32,8,2,1024]{3,1,0,2:T(8,128)(2,1)}, bf16[32,8,2,1024]{3,1,0,2:T(8,128)(2,1)}, u32[]{:S(2)}, u32[]{:S(2)}) collective-permute-start(bf16[32,8,2,1024]{3,1,0,2:T(8,128)(2,1)} %copy.59), channel_id=1, source_target_pairs={{0,8},{8,0},{1,9},{9,1},{2,10},{10,2},{3,11},{11,3},{4,12},{12,4},... | collective-permute-start | bytes 3145736 | tf_op jit(solution)/shard_map/ppermute | solution.py:71
  59.7 6.7 %fusion.5 = bf16[8,512,128]{1,2,0:T(8,128)(2,1)} fusion(f32[8,512]{1,0:T(8,128)S(1)} %fusion, f32[8,512]{1,0:T(8,128)S(1)} %get-tuple-element.32, f32[512,512,8]{1,0,2:T(8,128)} %copy-done.1, pred[512,512]{0,1:T(8,128)(4,1)S(1)} %iota_compare_fusion, bf16[512,128]{1,0:T(8,128)(2,1)S(1)} %copy-done.6), kind=kOutput, calls=%fused_computation.11 | convolution fusion | flops 547880960 | bytes 9863168 | tf_op jit(solution)/shard_map/kgts,skd->tkgd/dot_general | solution.py:34
  66.4 1.5 copy.56
  67.9 0.5 multiply_reduce_fusion
  68.4 0.3 multiply_reduce_fusion.5
  68.8 1.3 fusion.9
  70.1 2.5 %fusion.13 = f32[1,512,32,1,8]{1,4,3,2,0:T(8,128)} fusion(bf16[512,1024]{0,1:T(8,128)(2,1)} %bitcast.155, f32[256]{0:T(256)S(1)} %sub.122, bf16[32,8,2,1024]{3,1,2,0:T(8,128)(2,1)S(1)} %all-to-all-done), kind=kOutput, calls=%fused_computation.21 | convolution fusion | flops 268697600 | bytes 2098176 | tf_op jit(solution)/shard_map/dot_general | solution.py:45
  72.6 1.6 %multiply_reduce_fusion.3 = (f32[32,8]{1,0:T(8,128)S(1)}, f32[32,8]{1,0:T(8,128)S(1)}) fusion(bf16[32,8,2,1024]{3,1,0,2:T(8,128)(2,1)} %collective-permute-done), kind=kLoop, calls=%fused_computation.36 | loop fusion | flops 1572352 | bytes 1050624 | tf_op jit(solution)/shard_map/reduce_sum | solution.py:41
  74.4 1.5 fusion.15
  75.8 1.5 %fusion.11 = f32[1,512,32,1,8]{1,4,3,2,0:T(8,128)S(1)} fusion(bf16[512,1024]{1,0:T(8,128)(2,1)S(1)} %copy-done.2, bf16[32,8,2,1024]{3,1,0,2:T(8,128)(2,1)} %collective-permute-done, f32[256]{0:T(256)S(1)} %sub.125), kind=kOutput, calls=%fused_computation.19 | convolution fusion | flops 268697600 | bytes 2098176 | tf_op jit(solution)/shard_map/dot_general | solution.py:45
  77.4 0.3 maximum_select_fusion
  77.7 0.3 broadcast_add_fusion
  78.0 1.6 %copy.66 = f32[2,512,8,64]{1,3,0,2:T(8,128)} copy(f32[2,512,8,64]{1,3,2,0:T(8,128)S(1)} %broadcast_add_fusion) | data formatting | bytes 4194304 | tf_op jit(solution)/shard_map/add | solution.py:142
  79.6 4.0 %all-to-all-start.1 = ((f32[2,512,8,64]{1,3,0,2:T(8,128)}), f32[2,512,8,64]{1,3,0,2:T(8,128)S(1)}, u32[]{:S(2)}, u32[]{:S(2)}) async-start(f32[2,512,8,64]{1,3,0,2:T(8,128)} %copy.66), calls=%async_computation.1 | async-start | bytes 4194304 | tf_op jit(solution)/shard_map/all_to_all | solution.py:147
  83.6 26.7 %all-to-all-done.1 = f32[2,512,8,64]{1,3,0,2:T(8,128)S(1)} async-done(((f32[2,512,8,64]{1,3,0,2:T(8,128)}), f32[2,512,8,64]{1,3,0,2:T(8,128)S(1)}, u32[]{:S(2)}, u32[]{:S(2)}) %all-to-all-start.1) | async-done | bytes 2097184 | tf_op jit(solution)/shard_map/all_to_all | solution.py:147
  110.4 0.2 reduce_sum.193
  110.6 0.1 exponential_convert_fusion
  110.7 0.8 broadcast_in_dim.41
  111.6 3.5 %all-to-all-start.2 = ((bf16[8,512,64]{1,2,0:T(8,128)(2,1)}), bf16[8,512,64]{1,2,0:T(8,128)(2,1)S(1)}, u32[]{:S(2)}, u32[]{:S(2)}) async-start(bf16[8,512,64]{1,2,0:T(8,128)(2,1)} %broadcast_in_dim.41), calls=%async_computation.2 | async-start | bytes 1048576 | tf_op jit(solution)/shard_map/all_to_all | solution.py:104
  115.1 0.1 convert_reduce_fusion
  115.2 0.2 fusion.35
  115.4 8.6 %all-to-all-done.2 = bf16[8,512,64]{1,2,0:T(8,128)(2,1)S(1)} async-done(((bf16[8,512,64]{1,2,0:T(8,128)(2,1)}), bf16[8,512,64]{1,2,0:T(8,128)(2,1)S(1)}, u32[]{:S(2)}, u32[]{:S(2)}) %all-to-all-start.2) | async-done | bytes 524320 | tf_op jit(solution)/shard_map/all_to_all | solution.py:104
  124.0 0.1 bitcast_reduce_fusion
  124.3 0.3 multiply_reduce_fusion.1
  124.6 1.1 fusion.31
  125.9 3.9 %collective-permute-start.1 = (f32[33920]{0:T(1024)S(1)}, f32[33920]{0:T(1024)S(1)}, u32[]{:S(2)}, u32[]{:S(2)}) collective-permute-start(f32[33920]{0:T(1024)S(1)} %concatenate.8), channel_id=1, source_target_pairs={{0,8},{8,0},{1,9},{9,1},{2,10},{10,2},{3,11},{11,3},{4,12},{12,4},... | collective-permute-start | bytes 407048 | tf_op jit(solution)/shard_map/ppermute | solution.py:71
  130.0 0.8 collective-permute-done.1
  131.0 0.1 copy.67
  131.2 0.2 copy.68
  131.3 0.1 copy.69
  131.4 0.1 slice.100
  131.6 0.1 slice.104
  132.0 17.0 %all_to_all.27 = f32[32,1,656]{2,1,0:T(1,128)S(1)} all-to-all(f32[32,1,656]{2,1,0:T(1,128)S(1)} %all_to_all.20), channel_id=1, replica_groups=mesh['z'=8,'y_hi'=4,'core'=2,'x'=4,'y_lo'=2] {'z','y_hi'}, dimensions={0} | all-to-all | bytes 167936 | tf_op jit(solution)/shard_map/all_to_all | solution.py:196
  149.4 0.1 multiply_reduce_fusion.6
  149.5 0.7 rsqrt_multiply_fusion
  (62 shorter events, 2.1 us)
Async XLA Ops:
  0.0 2.9 %copy-start = (bf16[512,128]{1,0:T(8,128)(2,1)S(1)}, bf16[512,128]{1,0:T(8,128)(2,1)}, u32[]{:S(2)}) copy-start(bf16[512,128]{1,0:T(8,128)(2,1)} %param.9) | copy-start | bytes 393220
  0.0 22.3 %copy-start.2 = (bf16[512,1024]{1,0:T(8,128)(2,1)S(1)}, bf16[512,1024]{1,0:T(8,128)(2,1)}, u32[]{:S(2)}) copy-start(bf16[512,1024]{1,0:T(8,128)(2,1)} %param.8) | copy-start | bytes 3145732
  5.7 47.9 %all-to-all-start = ((bf16[32,8,2,1024]{3,1,2,0:T(8,128)(2,1)}), bf16[32,8,2,1024]{3,1,2,0:T(8,128)(2,1)S(1)}, u32[]{:S(2)}, u32[]{:S(2)}) async-start(bf16[32,8,2,1024]{3,1,2,0:T(8,128)(2,1)} %broadcast_in_dim.39), calls=%async_computation | async-start | bytes 2097152 | tf_op jit(solution)/shard_map/all_to_all | solution.py:104
  24.0 3.2 %copy-start.1 = (f32[512,512,8]{1,0,2:T(8,128)}, f32[512,512,8]{1,0,2:T(8,128)S(1)}, u32[]{:S(2)}) copy-start(f32[512,512,8]{1,0,2:T(8,128)S(1)} %get-tuple-element.33) | copy-start | bytes 25165828
  27.2 32.5 %copy-start.6 = (bf16[512,128]{1,0:T(8,128)(2,1)S(1)}, bf16[512,128]{1,0:T(8,128)(2,1)}, u32[]{:S(2)}) copy-start(bf16[512,128]{1,0:T(8,128)(2,1)} %param.10) | copy-start | bytes 393220
  54.6 18.0 %collective-permute-start = (bf16[32,8,2,1024]{3,1,0,2:T(8,128)(2,1)}, bf16[32,8,2,1024]{3,1,0,2:T(8,128)(2,1)}, u32[]{:S(2)}, u32[]{:S(2)}) collective-permute-start(bf16[32,8,2,1024]{3,1,0,2:T(8,128)(2,1)} %copy.59), channel_id=1, source_target_pairs={{0,8},{8,0},{1,9},{9,1},{2,10},{10,2},{3,11},{11,3},{4,12},{12,4},... | collective-permute-start | bytes 3145736 | tf_op jit(solution)/shard_map/ppermute | solution.py:71
  68.4 6.0 %copy-start.3 = (bf16[8,512,128]{1,2,0:T(8,128)(2,1)S(1)}, bf16[8,512,128]{1,2,0:T(8,128)(2,1)}, u32[]{:S(2)}) copy-start(bf16[8,512,128]{1,2,0:T(8,128)(2,1)} %fusion.5) | copy-start | bytes 3145732
  72.6 4.8 %copy-start.4 = (f32[1,512,32,1,8]{1,4,3,2,0:T(8,128)S(1)}, f32[1,512,32,1,8]{1,4,3,2,0:T(8,128)}, u32[]{:S(2)}) copy-start(f32[1,512,32,1,8]{1,4,3,2,0:T(8,128)} %fusion.9) | copy-start | bytes 1572868
  72.6 4.8 %copy-start.5 = (f32[1,512,32,1,8]{1,4,3,2,0:T(8,128)S(1)}, f32[1,512,32,1,8]{1,4,3,2,0:T(8,128)}, u32[]{:S(2)}) copy-start(f32[1,512,32,1,8]{1,4,3,2,0:T(8,128)} %fusion.13) | copy-start | bytes 1572868
  78.0 5.6 %copy-start.7 = (f32[512]{0:T(512)S(1)}, f32[512]{0:T(512)}, u32[]{:S(2)}) copy-start(f32[512]{0:T(512)} %param.13) | copy-start | bytes 6148
  78.0 5.6 %copy-start.8 = (f32[512]{0:T(512)S(1)}, f32[512]{0:T(512)}, u32[]{:S(2)}) copy-start(f32[512]{0:T(512)} %param.12) | copy-start | bytes 6148
  79.6 30.8 %all-to-all-start.1 = ((f32[2,512,8,64]{1,3,0,2:T(8,128)}), f32[2,512,8,64]{1,3,0,2:T(8,128)S(1)}, u32[]{:S(2)}, u32[]{:S(2)}) async-start(f32[2,512,8,64]{1,3,0,2:T(8,128)} %copy.66), calls=%async_computation.1 | async-start | bytes 4194304 | tf_op jit(solution)/shard_map/all_to_all | solution.py:147
  111.6 12.5 %all-to-all-start.2 = ((bf16[8,512,64]{1,2,0:T(8,128)(2,1)}), bf16[8,512,64]{1,2,0:T(8,128)(2,1)S(1)}, u32[]{:S(2)}, u32[]{:S(2)}) async-start(bf16[8,512,64]{1,2,0:T(8,128)(2,1)} %broadcast_in_dim.41), calls=%async_computation.2 | async-start | bytes 1048576 | tf_op jit(solution)/shard_map/all_to_all | solution.py:104
  125.9 4.9 %collective-permute-start.1 = (f32[33920]{0:T(1024)S(1)}, f32[33920]{0:T(1024)S(1)}, u32[]{:S(2)}, u32[]{:S(2)}) collective-permute-start(f32[33920]{0:T(1024)S(1)} %concatenate.8), channel_id=1, source_target_pairs={{0,8},{8,0},{1,9},{9,1},{2,10},{10,2},{3,11},{11,3},{4,12},{12,4},... | collective-permute-start | bytes 407048 | tf_op jit(solution)/shard_map/ppermute | solution.py:71

commit v4 on v2

--- a/solution.py
+++ b/solution.py
@@ -145,39 +145,51 @@
     row_square = jnp.sum(jnp.square(rows_centered), axis=0)
     column_square = jnp.sum(jnp.square(columns_centered), axis=0)
 
+    stats = (second, row_mean, row_square, column_mean, column_square)
+    stats = exchange_merge(stats, "z", 8, length)
+    stats = exchange_merge(stats, ("y_hi", CORE), 8, 8 * length)
+    second, row_mean, row_square, column_mean, column_square = stats
+    return second / token_count / jnp.sqrt(
+        (row_square / token_count + EPSILON)[:, None]
+        * (column_square / token_count + EPSILON)[None, :]
+    )
+
+
+def exchange_merge(stats, axis_name, count, group_tokens):
+    second, row_mean, row_square, column_mean, column_square = stats
+    rows, columns = second.shape
+    share = columns // count
     packed = jnp.concatenate(
         [
-            jnp.transpose(
-                second.reshape(row_share, data_count, column_share), (1, 0, 2)
-            ).reshape(data_count, row_share * column_share),
-            jnp.broadcast_to(row_mean[None], (data_count, row_share)),
-            jnp.broadcast_to(row_square[None], (data_count, row_share)),
-            column_mean.reshape(data_count, column_share),
-            column_square.reshape(data_count, column_share),
+            jnp.transpose(second.reshape(rows, count, share), (1, 0, 2)).reshape(
+                count, rows * share
+            ),
+            jnp.broadcast_to(row_mean[None], (count, rows)),
+            jnp.broadcast_to(row_square[None], (count, rows)),
+            column_mean.reshape(count, share),
+            column_square.reshape(count, share),
         ],
         axis=1,
     )
-    received = lax.all_to_all(packed, DATA, 0, 0, tiled=True)
-    cut = row_share * column_share
-    second_parts = received[:, :cut].reshape(data_count, row_share, column_share)
-    row_means = received[:, cut : cut + row_share]
-    row_squares = received[:, cut + row_share : cut + 2 * row_share]
-    column_means = received[:, cut + 2 * row_share : cut + 2 * row_share + column_share]
-    column_squares = received[:, cut + 2 * row_share + column_share :]
-
-    row_shift = row_means - jnp.mean(row_means, axis=0)[None, :]
-    column_shift = column_means - jnp.mean(column_means, axis=0)[None, :]
+    received = lax.all_to_all(packed, axis_name, 0, 0, tiled=True)
+    cut = rows * share
+    seconds = received[:, :cut].reshape(count, rows, share)
+    row_means = received[:, cut : cut + rows]
+    row_squares = received[:, cut + rows : cut + 2 * rows]
+    column_means = received[:, cut + 2 * rows : cut + 2 * rows + share]
+    column_squares = received[:, cut + 2 * rows + share :]
+    row_total = jnp.mean(row_means, axis=0)
+    column_total = jnp.mean(column_means, axis=0)
+    row_shift = row_means - row_total[None, :]
+    column_shift = column_means - column_total[None, :]
     between = jnp.sum(row_shift[:, :, None] * column_shift[:, None, :], axis=0)
-    covariance = (jnp.sum(second_parts, axis=0) + length * between) / token_count
-    spread_rows = (
-        jnp.sum(row_squares, axis=0) + length * jnp.sum(jnp.square(row_shift), axis=0)
-    ) / token_count
-    spread_columns = (
+    return (
+        jnp.sum(seconds, axis=0) + group_tokens * between,
+        row_total,
+        jnp.sum(row_squares, axis=0) + group_tokens * jnp.sum(jnp.square(row_shift), axis=0),
+        column_total,
         jnp.sum(column_squares, axis=0)
-        + length * jnp.sum(jnp.square(column_shift), axis=0)
-    ) / token_count
-    return covariance / jnp.sqrt(
-        (spread_rows + EPSILON)[:, None] * (spread_columns + EPSILON)[None, :]
+        + group_tokens * jnp.sum(jnp.square(column_shift), axis=0),
     )
 
 

time: 147 us -> 151 us (1.027)
  blocking collectives: 22.4 us -> 25.5 us
    all_to_all x1 -> x2, blocking collectives: 22.4 us -> 25.5 us  [exchange_merge(): received = lax.all_to_all(packed, axis_name, 0, 0, tiled=True)]
    unnamed x17 -> x14, local copies, waits for them, and re-layouts: 3.55 us -> 3.25 us
  transfers between devices with their start and end apart: 5 -> 5, of which waited for: 4 -> 4; matrix products, arithmetic and copies ran while one was open for 8% -> 7% of each run, Pallas kernels for 0% -> 0%
where the time goes in v4:
time: 151 us; the launch traced here: 150 us
  waiting for transfers between devices  61.2 us (41%)
  starting transfers between devices  31.6 us (21%)
  blocking collectives  25.5 us (17%)
  matrix products  14.2 us (9%)
  local copies, waits for them, and re-layouts  10.3 us (7%)
  other arithmetic  6.88 us (5%)
    all_to_all x2, waiting for transfers between devices, broadcast_gather(): return lax.all_to_all(spread, axis_name, 0, 0, tiled=True)  33.6 us
    all_to_all x1, waiting for transfers between devices, shards(): lax.all_to_all(distance_part, MODEL, 2, 2, tiled=True)  26.7 us
    all_to_all x2, blocking collectives, exchange_merge(): received = lax.all_to_all(packed, axis_name, 0, 0, tiled=True)  25.5 us
    all_to_all x2, starting transfers between devices, broadcast_gather(): return lax.all_to_all(spread, axis_name, 0, 0, tiled=True)  13.8 us
    ppermute x2, starting transfers between devices, swap_cores(): return lax.ppermute(piece, CORE, [(0, 1), (1, 0)])  13.7 us
    dot_general x1, matrix products, attend(): jnp.einsum('kgts,skd->tkgd', weights, value_three, preferred_element_type...  6.86 us
    all_to_all x1, starting transfers between devices, shards(): lax.all_to_all(distance_part, MODEL, 2, 2, tiled=True)  4.01 us
    unnamed x14, local copies, waits for them, and re-layouts  3.25 us
  transfers between devices with their start and end apart: 5, of which 4 were waited for; matrix products, arithmetic and copies ran while one was open for 7% of the time, Pallas kernels for 0%

profile of v4, /device:TPU:1, one launch (start us, length us, event | category | flops | bytes accessed | tf_op | source)
XLA Modules:
  0.0 150.0 jit_solution(6644089458954400661)
XLA Ops:
  0.0 0.8 compare_and_fusion
  0.9 1.9 %gather_fusion = bf16[8,1024]{1,0:T(8,128)(2,1)S(1)} fusion(bf16[512,1024]{1,0:T(8,128)(2,1)} %param.8, s32[1024]{0:T(1024)S(1)} %pad_clamp_fusion), kind=kCustom, calls=%fused_computation.clone | custom fusion | bytes 32800 | tf_op jit(solution)/shard_map/jit(_take)/gather | solution.py:106
  2.9 0.3 fusion.41
  3.1 0.2 fusion.26
  3.3 0.1 fusion.29
  3.4 1.1 fusion.11
  4.5 8.8 %collective-permute-start = (bf16[2,8,1024]{2,1,0:T(8,128)(2,1)S(1)}, bf16[2,8,1024]{2,1,0:T(8,128)(2,1)S(1)}, u32[]{:S(2)}, u32[]{:S(2)}) collective-permute-start(bf16[2,8,1024]{2,1,0:T(8,128)(2,1)S(1)} %get-tuple-element.29), channel_id=1, source_target_pairs={{0,8},{8,0},{1,9},{9,1},{2,10},{10,2},{3,11},{11,3},{4,12},{12,4},... | collective-permute-start | bytes 98312 | tf_op jit(solution)/shard_map/ppermute | solution.py:71
  13.3 0.8 collective-permute-done
  14.2 1.2 broadcast_in_dim.44
  15.4 10.3 %all-to-all-start = ((bf16[32,2,8,1024]{3,2,1,0:T(8,128)(2,1)}), bf16[32,2,8,1024]{3,2,1,0:T(8,128)(2,1)S(1)}, u32[]{:S(2)}, u32[]{:S(2)}) async-start(bf16[32,2,8,1024]{3,2,1,0:T(8,128)(2,1)} %broadcast_in_dim.44), calls=%async_computation | async-start | bytes 2097152 | tf_op jit(solution)/shard_map/all_to_all | solution.py:91
  25.8 0.3 multiply_reduce_fusion.2
  26.1 1.7 %fusion.1 = (f32[8,512]{1,0:T(8,128)S(1)}, f32[512,512,8]{1,0,2:T(8,128)S(1)}) fusion(pred[512,512]{0,1:T(8,128)(4,1)S(1)} %iota_compare_fusion, bf16[512,128]{1,0:T(8,128)(2,1)S(1)} %copy-done, bf16[512,1024]{1,0:T(8,128)(2,1)S(1)} %copy-done.2), kind=kOutput, calls=%fused_computation.5 | convolution fusion | flops 543158272 | bytes 9846784 | tf_op jit(solution)/shard_map/tkgd,skd->kgts/dot_general | solution.py:27
  27.8 3.2 %copy-done.1 = f32[512,512,8]{1,0,2:T(8,128)} copy-done((f32[512,512,8]{1,0,2:T(8,128)}, f32[512,512,8]{1,0,2:T(8,128)S(1)}, u32[]{:S(2)}) %copy-start.1) | copy-done | bytes 8388632
  31.0 1.7 %fusion = f32[8,512]{1,0:T(8,128)S(1)} fusion(f32[512,512,8]{1,0,2:T(8,128)S(1)} %get-tuple-element.33, f32[8,512]{1,0:T(8,128)S(1)} %get-tuple-element.32, pred[512,512]{0,1:T(8,128)(4,1)S(1)} %iota_compare_fusion), kind=kLoop, calls=%fused_computation.4 | loop fusion | flops 8384512 | bytes 8683520 | tf_op jit(solution)/shard_map/reduce_sum | solution.py:33
  32.7 25.0 %all-to-all-done = bf16[32,2,8,1024]{3,2,1,0:T(8,128)(2,1)S(1)} async-done(((bf16[32,2,8,1024]{3,2,1,0:T(8,128)(2,1)}), bf16[32,2,8,1024]{3,2,1,0:T(8,128)(2,1)S(1)}, u32[]{:S(2)}, u32[]{:S(2)}) %all-to-all-start) | async-done | bytes 1048608 | tf_op jit(solution)/shard_map/all_to_all | solution.py:91
  57.7 5.0 %collective-permute-start.1 = (bf16[32,2,8,1024]{3,2,1,0:T(8,128)(2,1)S(1)}, bf16[32,2,8,1024]{3,2,1,0:T(8,128)(2,1)S(1)}, u32[]{:S(2)}, u32[]{:S(2)}) collective-permute-start(bf16[32,2,8,1024]{3,2,1,0:T(8,128)(2,1)S(1)} %all-to-all-done), channel_id=1, source_target_pairs={{0,8},{8,0},{1,9},{9,1},{2,10},{10,2},{3,11},{11,3},{4,12},{12,4},... | collective-permute-start | bytes 3145736 | tf_op jit(solution)/shard_map/ppermute | solution.py:71
  62.6 6.9 %multiply_reduce_fusion.1 = (f32[512]{0:T(512)S(1)}, bf16[8,512,128]{1,2,0:T(8,128)(2,1)}) fusion(bf16[512,128]{1,0:T(8,128)(2,1)S(1)} %copy-done.3, f32[8,512]{1,0:T(8,128)S(1)} %fusion, f32[8,512]{1,0:T(8,128)S(1)} %get-tuple-element.32, f32[512,512,8]{1,0,2:T(8,128)} %copy-done.1, pred[512,512]{0,1:T(8,128)(4,1)S(1)} %iota_compare_fusion), kind=kOutput, calls=%fused_computation.12 | convolution fusion | flops 549453312 | bytes 9865216 | tf_op jit(solution)/shard_map/kgts,skd->tkgd/dot_general | solution.py:34
  69.5 0.1 broadcast_select_fusion.1
  69.7 0.7 fusion.42
  70.4 0.5 multiply_reduce_fusion
  71.0 1.9 %convolution_bitcast_fusion = f32[1,512,8,64]{1,3,2,0:T(8,128)S(1)} fusion(bf16[512,1024,1]{0,1,2:T(8,128)(2,1)} %bitcast.165, bf16[8,64,1024]{2,1,0:T(8,128)(2,1)S(1)} %bitcast.145), kind=kOutput, calls=%fused_computation.15 | convolution fusion | flops 536870912 | bytes 3145728 | tf_op jit(solution)/shard_map/dot_general | solution.py:45
  72.9 0.3 fusion.5
  73.3 1.6 %copy.39 = f32[2,512,8,64]{1,3,0,2:T(8,128)} copy(f32[2,512,8,64]{1,3,2,0:T(8,128)S(1)} %fusion.5) | data formatting | bytes 4194304 | tf_op jit(solution)/shard_map/sub | solution.py:117
  74.8 4.0 %all-to-all-start.1 = ((f32[2,512,8,64]{1,3,0,2:T(8,128)}), f32[2,512,8,64]{1,3,0,2:T(8,128)S(1)}, u32[]{:S(2)}, u32[]{:S(2)}) async-start(f32[2,512,8,64]{1,3,0,2:T(8,128)} %copy.39), calls=%async_computation.1 | async-start | bytes 4194304 | tf_op jit(solution)/shard_map/all_to_all | solution.py:120
  78.9 26.7 %all-to-all-done.1 = f32[2,512,8,64]{1,3,0,2:T(8,128)S(1)} async-done(((f32[2,512,8,64]{1,3,0,2:T(8,128)}), f32[2,512,8,64]{1,3,0,2:T(8,128)S(1)}, u32[]{:S(2)}, u32[]{:S(2)}) %all-to-all-start.1) | async-done | bytes 2097184 | tf_op jit(solution)/shard_map/all_to_all | solution.py:120
  105.7 0.2 reduce_sum.243
  105.9 0.1 exponential_convert_fusion
  106.0 0.8 broadcast_in_dim.46
  106.9 3.5 %all-to-all-start.2 = ((bf16[8,512,64]{1,2,0:T(8,128)(2,1)}), bf16[8,512,64]{1,2,0:T(8,128)(2,1)S(1)}, u32[]{:S(2)}, u32[]{:S(2)}) async-start(bf16[8,512,64]{1,2,0:T(8,128)(2,1)} %broadcast_in_dim.46), calls=%async_computation.2 | async-start | bytes 1048576 | tf_op jit(solution)/shard_map/all_to_all | solution.py:91
  110.4 0.1 convert_reduce_fusion
  110.5 0.2 fusion.21
  110.7 8.6 %all-to-all-done.2 = bf16[8,512,64]{1,2,0:T(8,128)(2,1)S(1)} async-done(((bf16[8,512,64]{1,2,0:T(8,128)(2,1)}), bf16[8,512,64]{1,2,0:T(8,128)(2,1)S(1)}, u32[]{:S(2)}, u32[]{:S(2)}) %all-to-all-start.2) | async-done | bytes 524320 | tf_op jit(solution)/shard_map/all_to_all | solution.py:91
  119.3 0.1 bitcast_reduce_fusion
  119.5 0.1 bitcast_subtract_fusion
  119.7 1.7 %convolution_bitcast_fusion.1 = f32[8,64,64]{2,1,0:T(8,128)S(1)} fusion(f32[8,64,512]{2,1,0:T(8,128)S(1)} %bitcast.148, f32[64]{0:T(128)S(1)} %broadcast_multiply_fusion.6, bf16[2,512,64]{1,2,0:T(8,128)(2,1)S(1)} %exponential_convert_fusion), kind=kOutput, calls=%fused_computation.16 | convolution fusion | flops 201392128 | bytes 1245696 | tf_op jit(solution)/shard_map/dot_general | solution.py:138
  121.4 0.1 reshape.206
  121.5 0.3 fusion.16
  121.9 0.1 all_to_all.28
  122.0 11.6 %all_to_all.39 = f32[8,1,4352]{2,1,0:T(1,128)S(1)} all-to-all(f32[8,1,4352]{2,1,0:T(1,128)S(1)} %all_to_all.28), channel_id=1, replica_groups=mesh['z'=8,'y_hi'=4,'core'=2,'x'=4,'y_lo'=2] {'z'}, dimensions={0} | all-to-all | bytes 278528 | tf_op jit(solution)/shard_map/all_to_all | solution.py:174
  133.6 0.1 slice_reduce_fusion.4
  133.7 0.2 reduce_sum.249
  134.0 0.1 multiply_reduce_fusion.3
  134.2 0.2 copy.41
  134.5 0.2 reshape.207
  134.9 13.9 %all_to_all.40 = f32[8,1,656]{2,1,0:T(1,128)S(1)} all-to-all(f32[8,1,656]{2,1,0:T(1,128)S(1)} %copy.43), channel_id=1, replica_groups=mesh['z'=8,'y_hi'=4,'core'=2,'x'=4,'y_lo'=2] {'y_hi','core'}, dimensions={0} | all-to-all | bytes 41984 | tf_op jit(solution)/shard_map/all_to_all | solution.py:174
  148.8 0.1 slice_reduce_fusion.2
  148.9 0.1 slice_reduce_fusion.3
  149.3 0.7 rsqrt_multiply_fusion
  (57 shorter events, 1.5 us)
Async XLA Ops:
  0.0 2.9 %copy-start = (bf16[512,128]{1,0:T(8,128)(2,1)S(1)}, bf16[512,128]{1,0:T(8,128)(2,1)}, u32[]{:S(2)}) copy-start(bf16[512,128]{1,0:T(8,128)(2,1)} %param.9) | copy-start | bytes 393220
  0.0 25.8 %copy-start.2 = (bf16[512,1024]{1,0:T(8,128)(2,1)S(1)}, bf16[512,1024]{1,0:T(8,128)(2,1)}, u32[]{:S(2)}) copy-start(bf16[512,1024]{1,0:T(8,128)(2,1)} %param.8) | copy-start | bytes 3145732
  4.5 9.6 %collective-permute-start = (bf16[2,8,1024]{2,1,0:T(8,128)(2,1)S(1)}, bf16[2,8,1024]{2,1,0:T(8,128)(2,1)S(1)}, u32[]{:S(2)}, u32[]{:S(2)}) collective-permute-start(bf16[2,8,1024]{2,1,0:T(8,128)(2,1)S(1)} %get-tuple-element.29), channel_id=1, source_target_pairs={{0,8},{8,0},{1,9},{9,1},{2,10},{10,2},{3,11},{11,3},{4,12},{12,4},... | collective-permute-start | bytes 98312 | tf_op jit(solution)/shard_map/ppermute | solution.py:71
  15.4 42.3 %all-to-all-start = ((bf16[32,2,8,1024]{3,2,1,0:T(8,128)(2,1)}), bf16[32,2,8,1024]{3,2,1,0:T(8,128)(2,1)S(1)}, u32[]{:S(2)}, u32[]{:S(2)}) async-start(bf16[32,2,8,1024]{3,2,1,0:T(8,128)(2,1)} %broadcast_in_dim.44), calls=%async_computation | async-start | bytes 2097152 | tf_op jit(solution)/shard_map/all_to_all | solution.py:91
  27.7 3.2 %copy-start.1 = (f32[512,512,8]{1,0,2:T(8,128)}, f32[512,512,8]{1,0,2:T(8,128)S(1)}, u32[]{:S(2)}) copy-start(f32[512,512,8]{1,0,2:T(8,128)S(1)} %get-tuple-element.33) | copy-start | bytes 25165828
  31.0 31.7 %copy-start.3 = (bf16[512,128]{1,0:T(8,128)(2,1)S(1)}, bf16[512,128]{1,0:T(8,128)(2,1)}, u32[]{:S(2)}) copy-start(bf16[512,128]{1,0:T(8,128)(2,1)} %param.10) | copy-start | bytes 393220
  57.7 11.8 %collective-permute-start.1 = (bf16[32,2,8,1024]{3,2,1,0:T(8,128)(2,1)S(1)}, bf16[32,2,8,1024]{3,2,1,0:T(8,128)(2,1)S(1)}, u32[]{:S(2)}, u32[]{:S(2)}) collective-permute-start(bf16[32,2,8,1024]{3,2,1,0:T(8,128)(2,1)S(1)} %all-to-all-done), channel_id=1, source_target_pairs={{0,8},{8,0},{1,9},{9,1},{2,10},{10,2},{3,11},{11,3},{4,12},{12,4},... | collective-permute-start | bytes 3145736 | tf_op jit(solution)/shard_map/ppermute | solution.py:71
  73.2 5.6 %copy-start.4 = (f32[512]{0:T(512)S(1)}, f32[512]{0:T(512)}, u32[]{:S(2)}) copy-start(f32[512]{0:T(512)} %param.13) | copy-start | bytes 6148
  73.2 5.6 %copy-start.5 = (f32[512]{0:T(512)S(1)}, f32[512]{0:T(512)}, u32[]{:S(2)}) copy-start(f32[512]{0:T(512)} %param.12) | copy-start | bytes 6148
  74.8 30.8 %all-to-all-start.1 = ((f32[2,512,8,64]{1,3,0,2:T(8,128)}), f32[2,512,8,64]{1,3,0,2:T(8,128)S(1)}, u32[]{:S(2)}, u32[]{:S(2)}) async-start(f32[2,512,8,64]{1,3,0,2:T(8,128)} %copy.39), calls=%async_computation.1 | async-start | bytes 4194304 | tf_op jit(solution)/shard_map/all_to_all | solution.py:120
  106.9 12.5 %all-to-all-start.2 = ((bf16[8,512,64]{1,2,0:T(8,128)(2,1)}), bf16[8,512,64]{1,2,0:T(8,128)(2,1)S(1)}, u32[]{:S(2)}, u32[]{:S(2)}) async-start(bf16[8,512,64]{1,2,0:T(8,128)(2,1)} %broadcast_in_dim.46), calls=%async_computation.2 | async-start | bytes 1048576 | tf_op jit(solution)/shard_map/all_to_all | solution.py:91

commit v5 on v2

--- a/solution.py
+++ b/solution.py
@@ -79,10 +79,15 @@
     pair = jnp.where(first, jnp.stack([own, other], 1), jnp.stack([other, own], 1))
     mine = jnp.where(first, pair[0], pair[1])
     fetched = broadcast_gather(mine, CHIPS)
-    swapped = swap_cores(fetched)
-    query_rows = jnp.where(first, fetched, swapped)
-    output_rows = jnp.where(first, swapped, fetched)
-    return jnp.stack([query_rows, output_rows])
+    return fetched.reshape((-1,) + fetched.shape[3:])
+
+
+def partial_distance(rows, marks):
+    return (
+        squares_by_row(rows)[:, None]
+        + squares_by_row(marks)[None, :]
+        - 2.0 * inner_rows(rows, marks)
+    )
 
 
 def broadcast_gather(piece, axis_name):
@@ -102,19 +107,20 @@
     token_count = length * data_count
 
     own_rows = landmark_index % length
-    gathered = gather_marks(
+    first = lax.axis_index(CORE) == 0
+    fetched = gather_marks(
         jnp.take(queries, own_rows, axis=0),
         attend_rows(queries, key_rows, value_rows, own_rows),
     )
-    landmark_piece = gathered.reshape(2, landmarks, queries.shape[1])
+    swapped = swap_cores(fetched)
     attended = attend(queries, key_rows, value_rows)
-
-    row_norms = jnp.stack([squares_by_row(queries), squares_by_row(attended)])
-    mark_norms = squares_by_row(landmark_piece)
-    cross = jnp.stack(
-        [inner_rows(queries, landmark_piece[0]), inner_rows(attended, landmark_piece[1])]
-    )
-    distance_part = row_norms[:, :, None] + mark_norms[:, None, :] - 2.0 * cross
+    fetched_part = partial_distance(jnp.where(first, queries, attended), fetched)
+    swapped_part = partial_distance(jnp.where(first, attended, queries), swapped)
+    distance_part = jnp.where(
+        first,
+        jnp.stack([fetched_part, swapped_part]),
+        jnp.stack([swapped_part, fetched_part]),
+    )
     distance_part = distance_part.reshape(2, length, model_count, row_share)
     distance = jnp.sum(
         lax.all_to_all(distance_part, MODEL, 2, 2, tiled=True), axis=2

time: 147 us -> 151 us (1.027)
  other arithmetic: 6.67 us -> 9.72 us
    reduce_sum x2 -> x3, other arithmetic: 0.77 us -> 2.74 us  [squares_by_row(): return jnp.sum(jnp.square(matrix.astype(jnp.float32)), axis=-1)]
    sub x1 -> x0, local copies, waits for them, and re-layouts: 1.58 us -> none  [shards(): distance_part = row_norms[:, :, None] + mark_norms[:, None, :] - 2.0 * cross]
  transfers between devices with their start and end apart: 5 -> 5, of which waited for: 4 -> 4; matrix products, arithmetic and copies ran while one was open for 8% -> 10% of each run, Pallas kernels for 0% -> 0%
where the time goes in v5:
time: 151 us; the launch traced here: 150 us
  waiting for transfers between devices  60.4 us (40%)
  starting transfers between devices  31.7 us (21%)
  blocking collectives  22.4 us (15%)
  matrix products  15.5 us (10%)
  local copies, waits for them, and re-layouts  9.79 us (6%)
  other arithmetic  9.72 us (6%)
    all_to_all x2, waiting for transfers between devices, broadcast_gather(): return lax.all_to_all(spread, axis_name, 0, 0, tiled=True)  32.8 us
    all_to_all x1, waiting for transfers between devices, shards(): lax.all_to_all(distance_part, MODEL, 2, 2, tiled=True)  26.7 us
    all_to_all x1, blocking collectives, shards(): received = lax.all_to_all(packed, DATA, 0, 0, tiled=True)  22.4 us
    all_to_all x2, starting transfers between devices, broadcast_gather(): return lax.all_to_all(spread, axis_name, 0, 0, tiled=True)  14 us
    ppermute x2, starting transfers between devices, swap_cores(): return lax.ppermute(piece, CORE, [(0, 1), (1, 0)])  13.7 us
    dot_general x1, matrix products, attend(): jnp.einsum('kgts,skd->tkgd', weights, value_three, preferred_element_type...  6.69 us
    all_to_all x1, starting transfers between devices, shards(): lax.all_to_all(distance_part, MODEL, 2, 2, tiled=True)  3.99 us
    unnamed x17, local copies, waits for them, and re-layouts  3.56 us
  transfers between devices with their start and end apart: 5, of which 4 were waited for; matrix products, arithmetic and copies ran while one was open for 10% of the time, Pallas kernels for 0%

profile of v5, /device:TPU:1, one launch (start us, length us, event | category | flops | bytes accessed | tf_op | source)
XLA Modules:
  0.0 149.9 jit_solution(14472078237538742805)
XLA Ops:
  0.0 0.7 compare_and_fusion
  0.8 1.9 %gather_fusion = bf16[8,1024]{1,0:T(8,128)(2,1)S(1)} fusion(bf16[512,1024]{1,0:T(8,128)(2,1)} %param.8, s32[1024]{0:T(1024)S(1)} %pad_clamp_fusion), kind=kCustom, calls=%fused_computation.clone | custom fusion | bytes 32800 | tf_op jit(solution)/shard_map/jit(_take)/gather | solution.py:112
  2.7 0.1 fusion.35
  2.8 0.3 fusion.42
  3.1 0.2 fusion.27
  3.3 0.1 fusion.30
  3.4 1.1 fusion.11
  4.4 8.8 %collective-permute-start = (bf16[2,8,1024]{2,1,0:T(8,128)(2,1)S(1)}, bf16[2,8,1024]{2,1,0:T(8,128)(2,1)S(1)}, u32[]{:S(2)}, u32[]{:S(2)}) collective-permute-start(bf16[2,8,1024]{2,1,0:T(8,128)(2,1)S(1)} %get-tuple-element.19), channel_id=1, source_target_pairs={{0,8},{8,0},{1,9},{9,1},{2,10},{10,2},{3,11},{11,3},{4,12},{12,4},... | collective-permute-start | bytes 98312 | tf_op jit(solution)/shard_map/ppermute | solution.py:71
  13.2 0.8 collective-permute-done
  14.1 1.2 broadcast_in_dim.42
  15.3 10.3 %all-to-all-start = ((bf16[32,2,8,1024]{3,2,1,0:T(8,128)(2,1)}), bf16[32,2,8,1024]{3,2,1,0:T(8,128)(2,1)S(1)}, u32[]{:S(2)}, u32[]{:S(2)}) async-start(bf16[32,2,8,1024]{3,2,1,0:T(8,128)(2,1)} %broadcast_in_dim.42), calls=%async_computation | async-start | bytes 2097152 | tf_op jit(solution)/shard_map/all_to_all | solution.py:96
  25.6 0.1 iota_compare_fusion
  25.7 2.7 %fusion.1 = (f32[8,512]{1,0:T(8,128)S(1)}, f32[512,512,8]{1,0,2:T(8,128)S(1)}) fusion(pred[512,512]{0,1:T(8,128)(4,1)S(1)} %iota_compare_fusion, bf16[512,128]{1,0:T(8,128)(2,1)S(1)} %copy-done, bf16[512,1024]{1,0:T(8,128)(2,1)} %param.8), kind=kOutput, calls=%fused_computation.5 | convolution fusion | flops 543158272 | bytes 9846784 | tf_op jit(solution)/shard_map/tkgd,skd->kgts/dot_general | solution.py:27
  28.4 3.2 %copy-done.1 = f32[512,512,8]{1,0,2:T(8,128)} copy-done((f32[512,512,8]{1,0,2:T(8,128)}, f32[512,512,8]{1,0,2:T(8,128)S(1)}, u32[]{:S(2)}) %copy-start.1) | copy-done | bytes 8388632
  31.7 1.7 %fusion = f32[8,512]{1,0:T(8,128)S(1)} fusion(f32[512,512,8]{1,0,2:T(8,128)S(1)} %get-tuple-element.25, f32[8,512]{1,0:T(8,128)S(1)} %get-tuple-element.24, pred[512,512]{0,1:T(8,128)(4,1)S(1)} %iota_compare_fusion), kind=kLoop, calls=%fused_computation.4 | loop fusion | flops 8384512 | bytes 8683520 | tf_op jit(solution)/shard_map/reduce_sum | solution.py:33
  33.4 24.4 %all-to-all-done = bf16[32,2,8,1024]{3,2,1,0:T(8,128)(2,1)S(1)} async-done(((bf16[32,2,8,1024]{3,2,1,0:T(8,128)(2,1)}), bf16[32,2,8,1024]{3,2,1,0:T(8,128)(2,1)S(1)}, u32[]{:S(2)}, u32[]{:S(2)}) %all-to-all-start) | async-done | bytes 1048608 | tf_op jit(solution)/shard_map/all_to_all | solution.py:96
  57.8 5.0 %collective-permute-start.1 = (bf16[512,1024]{1,0:T(8,128)(2,1)S(1)}, bf16[512,1024]{1,0:T(8,128)(2,1)}, u32[]{:S(2)}, u32[]{:S(2)}) collective-permute-start(bf16[512,1024]{1,0:T(8,128)(2,1)S(1)} %bitcast.127), channel_id=1, source_target_pairs={{0,8},{8,0},{1,9},{9,1},{2,10},{10,2},{3,11},{11,3},{4,12},{12,4},... | collective-permute-start | bytes 3145736 | tf_op jit(solution)/shard_map/ppermute | solution.py:71
  62.7 6.7 %fusion.5 = bf16[8,512,128]{1,2,0:T(8,128)(2,1)} fusion(f32[8,512]{1,0:T(8,128)S(1)} %fusion, f32[8,512]{1,0:T(8,128)S(1)} %get-tuple-element.24, f32[512,512,8]{1,0,2:T(8,128)} %copy-done.1, pred[512,512]{0,1:T(8,128)(4,1)S(1)} %iota_compare_fusion, bf16[512,128]{1,0:T(8,128)(2,1)S(1)} %copy-done.3), kind=kOutput, calls=%fused_computation.14 | convolution fusion | flops 547880960 | bytes 9863168 | tf_op jit(solution)/shard_map/kgts,skd->tkgd/dot_general | solution.py:34
  69.4 1.5 copy.49
  70.9 0.9 multiply_reduce_fusion.3
  71.9 0.3 multiply_reduce_fusion.2
  72.2 0.1 add.79
  72.3 0.8 fusion.8
  73.1 1.5 %multiply_reduce_fusion = f32[512]{0:T(512)S(1)} fusion(bf16[512,1024]{1,0:T(8,128)(2,1)} %collective-permute-done.1), kind=kLoop, calls=%fused_computation.10 | loop fusion | flops 1572352 | bytes 1050624 | tf_op jit(solution)/shard_map/reduce_sum | solution.py:41
  74.6 2.0 %add_subtract_fusion = f32[512,512]{0,1:T(8,128)S(1)} fusion(f32[512]{0:T(512)S(1)} %multiply_reduce_fusion, f32[512]{0:T(512)S(1)} %get-tuple-element.7, bf16[512,1024]{1,0:T(8,128)(2,1)} %collective-permute-done.1, bf16[512,1024]{1,0:T(8,128)(2,1)S(1)} %copy.49, bf16[512,1024]{1,0:T(8,128)(2,1)S(1)} %copy-done.2, pred[]{:T(512)S(6)} %eq.6), kind=kOutput, calls=%fused_computation.33 | convolution fusion | flops 538181632 | bytes 4198401 | tf_op jit(solution)/shard_map/dot_general | solution.py:45
  76.5 1.6 %maximum_select_fusion = f32[2,512,8,64]{1,3,0,2:T(8,128)} fusion(f32[1,512,8,64]{1,3,0,2:T(8,128)S(1)} %bitcast.136, f32[1,512,8,64]{1,3,0,2:T(8,128)S(1)} %bitcast.135, pred[]{:T(512)S(6)} %eq.6), kind=kLoop, calls=%fused_computation.9 | loop fusion | flops 1572864 | bytes 4194305 | tf_op jit(solution)/shard_map/jit(_where)/select_n | solution.py:119
  78.1 4.0 %all-to-all-start.1 = ((f32[2,512,8,64]{1,3,0,2:T(8,128)}), f32[2,512,8,64]{1,3,0,2:T(8,128)S(1)}, u32[]{:S(2)}, u32[]{:S(2)}) async-start(f32[2,512,8,64]{1,3,0,2:T(8,128)} %maximum_select_fusion), calls=%async_computation.1 | async-start | bytes 4194304 | tf_op jit(solution)/shard_map/all_to_all | solution.py:126
  82.1 0.1 fusion.37
  82.2 26.7 %all-to-all-done.1 = f32[2,512,8,64]{1,3,0,2:T(8,128)S(1)} async-done(((f32[2,512,8,64]{1,3,0,2:T(8,128)}), f32[2,512,8,64]{1,3,0,2:T(8,128)S(1)}, u32[]{:S(2)}, u32[]{:S(2)}) %all-to-all-start.1) | async-done | bytes 2097184 | tf_op jit(solution)/shard_map/all_to_all | solution.py:126
  108.9 0.2 reduce_sum.179
  109.2 0.1 exponential_convert_fusion
  109.3 0.8 broadcast_in_dim.44
  110.1 3.7 %all-to-all-start.2 = ((bf16[8,512,64]{1,2,0:T(8,128)(2,1)}), bf16[8,512,64]{1,2,0:T(8,128)(2,1)S(1)}, u32[]{:S(2)}, u32[]{:S(2)}) async-start(bf16[8,512,64]{1,2,0:T(8,128)(2,1)} %broadcast_in_dim.44), calls=%async_computation.2 | async-start | bytes 1048576 | tf_op jit(solution)/shard_map/all_to_all | solution.py:96
  113.8 0.1 convert_reduce_fusion
  113.9 0.2 fusion.22
  114.1 8.5 %all-to-all-done.2 = bf16[8,512,64]{1,2,0:T(8,128)(2,1)S(1)} async-done(((bf16[8,512,64]{1,2,0:T(8,128)(2,1)}), bf16[8,512,64]{1,2,0:T(8,128)(2,1)S(1)}, u32[]{:S(2)}, u32[]{:S(2)}) %all-to-all-start.2) | async-done | bytes 524320 | tf_op jit(solution)/shard_map/all_to_all | solution.py:96
  122.6 0.1 bitcast_reduce_fusion
  122.9 0.3 fusion.16
  123.3 0.1 bitcast_subtract_fusion
  123.5 2.1 %convolution_bitcast_fusion = f32[64,64,8]{0,1,2:T(8,128)S(1)} fusion(f32[64,8,512]{2,1,0:T(8,128)S(1)} %bitcast.126, f32[64]{0:T(128)S(1)} %broadcast_multiply_fusion.3, bf16[2,512,64]{1,2,0:T(8,128)(2,1)S(1)} %exponential_convert_fusion), kind=kOutput, calls=%fused_computation.18 | convolution fusion | flops 201392128 | bytes 1245696 | tf_op jit(solution)/shard_map/dot_general | solution.py:144
  125.6 0.2 bitcast_dynamic-update-slice_fusion
  126.0 0.2 copy.61
  126.2 22.4 %all_to_all.27 = f32[64,1,656]{2,1,0:T(1,128)S(1)} all-to-all(f32[64,1,656]{2,1,0:T(1,128)S(1)} %copy.61), channel_id=1, replica_groups=mesh['z'=8,'y_hi'=4,'core'=2,'x'=4,'y_lo'=2] {'z','y_hi','core'}, dimensions={0} | all-to-all | bytes 335872 | tf_op jit(solution)/shard_map/all_to_all | solution.py:166
  148.6 0.1 slice_reduce_fusion.2
  148.7 0.1 slice_reduce_fusion.1
  148.9 0.1 reduce_sum.185
  149.1 0.1 multiply_reduce_fusion.4
  149.2 0.7 rsqrt_multiply_fusion
  (39 shorter events, 0.8 us)
Async XLA Ops:
  0.0 2.8 %copy-start = (bf16[512,128]{1,0:T(8,128)(2,1)S(1)}, bf16[512,128]{1,0:T(8,128)(2,1)}, u32[]{:S(2)}) copy-start(bf16[512,128]{1,0:T(8,128)(2,1)} %param.9) | copy-start | bytes 393220
  4.4 9.6 %collective-permute-start = (bf16[2,8,1024]{2,1,0:T(8,128)(2,1)S(1)}, bf16[2,8,1024]{2,1,0:T(8,128)(2,1)S(1)}, u32[]{:S(2)}, u32[]{:S(2)}) collective-permute-start(bf16[2,8,1024]{2,1,0:T(8,128)(2,1)S(1)} %get-tuple-element.19), channel_id=1, source_target_pairs={{0,8},{8,0},{1,9},{9,1},{2,10},{10,2},{3,11},{11,3},{4,12},{12,4},... | collective-permute-start | bytes 98312 | tf_op jit(solution)/shard_map/ppermute | solution.py:71
  15.3 42.5 %all-to-all-start = ((bf16[32,2,8,1024]{3,2,1,0:T(8,128)(2,1)}), bf16[32,2,8,1024]{3,2,1,0:T(8,128)(2,1)S(1)}, u32[]{:S(2)}, u32[]{:S(2)}) async-start(bf16[32,2,8,1024]{3,2,1,0:T(8,128)(2,1)} %broadcast_in_dim.42), calls=%async_computation | async-start | bytes 2097152 | tf_op jit(solution)/shard_map/all_to_all | solution.py:96
  25.7 37.0 %copy-start.3 = (bf16[512,128]{1,0:T(8,128)(2,1)S(1)}, bf16[512,128]{1,0:T(8,128)(2,1)}, u32[]{:S(2)}) copy-start(bf16[512,128]{1,0:T(8,128)(2,1)} %param.10) | copy-start | bytes 393220
  28.4 3.2 %copy-start.1 = (f32[512,512,8]{1,0,2:T(8,128)}, f32[512,512,8]{1,0,2:T(8,128)S(1)}, u32[]{:S(2)}) copy-start(f32[512,512,8]{1,0,2:T(8,128)S(1)} %get-tuple-element.25) | copy-start | bytes 25165828
  57.8 13.2 %copy-start.2 = (bf16[512,1024]{1,0:T(8,128)(2,1)S(1)}, bf16[512,1024]{1,0:T(8,128)(2,1)}, u32[]{:S(2)}) copy-start(bf16[512,1024]{1,0:T(8,128)(2,1)} %param.8) | copy-start | bytes 3145732
  57.8 15.3 %collective-permute-start.1 = (bf16[512,1024]{1,0:T(8,128)(2,1)S(1)}, bf16[512,1024]{1,0:T(8,128)(2,1)}, u32[]{:S(2)}, u32[]{:S(2)}) collective-permute-start(bf16[512,1024]{1,0:T(8,128)(2,1)S(1)} %bitcast.127), channel_id=1, source_target_pairs={{0,8},{8,0},{1,9},{9,1},{2,10},{10,2},{3,11},{11,3},{4,12},{12,4},... | collective-permute-start | bytes 3145736 | tf_op jit(solution)/shard_map/ppermute | solution.py:71
  73.0 9.1 %copy-start.4 = (f32[512]{0:T(512)S(1)}, f32[512]{0:T(512)}, u32[]{:S(2)}) copy-start(f32[512]{0:T(512)} %param.13) | copy-start | bytes 6148
  73.0 9.1 %copy-start.5 = (f32[512]{0:T(512)S(1)}, f32[512]{0:T(512)}, u32[]{:S(2)}) copy-start(f32[512]{0:T(512)} %param.12) | copy-start | bytes 6148
  78.1 30.8 %all-to-all-start.1 = ((f32[2,512,8,64]{1,3,0,2:T(8,128)}), f32[2,512,8,64]{1,3,0,2:T(8,128)S(1)}, u32[]{:S(2)}, u32[]{:S(2)}) async-start(f32[2,512,8,64]{1,3,0,2:T(8,128)} %maximum_select_fusion), calls=%async_computation.1 | async-start | bytes 4194304 | tf_op jit(solution)/shard_map/all_to_all | solution.py:126
  110.1 12.5 %all-to-all-start.2 = ((bf16[8,512,64]{1,2,0:T(8,128)(2,1)}), bf16[8,512,64]{1,2,0:T(8,128)(2,1)S(1)}, u32[]{:S(2)}, u32[]{:S(2)}) async-start(bf16[8,512,64]{1,2,0:T(8,128)(2,1)} %broadcast_in_dim.44), calls=%async_computation.2 | async-start | bytes 1048576 | tf_op jit(solution)/shard_map/all_to_all | solution.py:96

commit v6 on v2

--- a/solution.py
+++ b/solution.py
@@ -72,13 +72,13 @@
 
 
 def gather_marks(query_marks, output_marks):
-    core = lax.axis_index(CORE)
-    own = jnp.stack([query_marks, output_marks])
-    other = swap_cores(own)
-    first = core == 0
-    pair = jnp.where(first, jnp.stack([own, other], 1), jnp.stack([other, own], 1))
-    mine = jnp.where(first, pair[0], pair[1])
-    fetched = broadcast_gather(mine, CHIPS)
+    first = lax.axis_index(CORE) == 0
+    data_count = lax.axis_size(DATA)
+    kinds = jnp.stack([query_marks, output_marks])
+    spread = jnp.broadcast_to(kinds[None], (data_count // 2,) + kinds.shape)
+    fetched = lax.all_to_all(
+        spread.reshape((data_count,) + query_marks.shape), DATA, 0, 0, tiled=True
+    )
     swapped = swap_cores(fetched)
     query_rows = jnp.where(first, fetched, swapped)
     output_rows = jnp.where(first, swapped, fetched)

time: 147 us -> 146 us (level)
  starting transfers between devices: 31.8 us -> 27.8 us
    all_to_all x0 -> x1, waiting for transfers between devices: none -> 25.9 us  [gather_marks(): lax.all_to_all(spread.reshape((data_count,) + query_marks.shape), DATA, 0...]
    all_to_all x2 -> x1, waiting for transfers between devices: 33.4 us -> 9.07 us  [broadcast_gather(): return lax.all_to_all(spread, axis_name, 0, 0, tiled=True)]
    all_to_all x0 -> x1, starting transfers between devices: none -> 17.6 us  [gather_marks(): lax.all_to_all(spread.reshape((data_count,) + query_marks.shape), DATA, 0...]
    ppermute x2 -> x1, starting transfers between devices: 13.7 us -> 2.48 us  [swap_cores(): return lax.ppermute(piece, CORE, [(0, 1), (1, 0)])]
    all_to_all x2 -> x1, starting transfers between devices: 14 us -> 3.67 us  [broadcast_gather(): return lax.all_to_all(spread, axis_name, 0, 0, tiled=True)]
    unnamed x17 -> x19, local copies, waits for them, and re-layouts: 3.55 us -> 4.54 us
  transfers between devices with their start and end apart: 5 -> 4, of which waited for: 4 -> 3; matrix products, arithmetic and copies ran while one was open for 8% -> 8% of each run, Pallas kernels for 0% -> 0%
where the time goes in v6:
time: 146 us; the launch traced here: 145 us
  waiting for transfers between devices  61.6 us (42%)
  starting transfers between devices  27.8 us (19%)
  blocking collectives  22.1 us (15%)
  matrix products  15.9 us (11%)
  local copies, waits for them, and re-layouts  10.8 us (7%)
  other arithmetic  6.65 us (5%)
    all_to_all x1, waiting for transfers between devices, shards(): lax.all_to_all(distance_part, MODEL, 2, 2, tiled=True)  26.7 us
    all_to_all x1, waiting for transfers between devices, gather_marks(): lax.all_to_all(spread.reshape((data_count,) + query_marks.shape), DATA, 0...  25.9 us
    all_to_all x1, blocking collectives, shards(): received = lax.all_to_all(packed, DATA, 0, 0, tiled=True)  22.1 us
    all_to_all x1, starting transfers between devices, gather_marks(): lax.all_to_all(spread.reshape((data_count,) + query_marks.shape), DATA, 0...  17.6 us
    all_to_all x1, waiting for transfers between devices, broadcast_gather(): return lax.all_to_all(spread, axis_name, 0, 0, tiled=True)  9.07 us
    dot_general x1, matrix products, attend(): jnp.einsum('kgts,skd->tkgd', weights, value_three, preferred_element_type...  6.86 us
    unnamed x19, local copies, waits for them, and re-layouts  4.54 us
    all_to_all x1, starting transfers between devices, shards(): lax.all_to_all(distance_part, MODEL, 2, 2, tiled=True)  4.01 us
  transfers between devices with their start and end apart: 4, of which 3 were waited for; matrix products, arithmetic and copies ran while one was open for 8% of the time, Pallas kernels for 0%

profile of v6, /device:TPU:1, one launch (start us, length us, event | category | flops | bytes accessed | tf_op | source)
XLA Modules:
  0.0 145.2 jit_solution(15625212965437867110)
XLA Ops:
  0.0 0.8 compare_and_fusion
  0.9 1.9 %gather_fusion = bf16[8,1024]{1,0:T(8,128)(2,1)S(1)} fusion(bf16[512,1024]{1,0:T(8,128)(2,1)} %param.8, s32[1024]{0:T(1024)S(1)} %pad_clamp_fusion), kind=kCustom, calls=%fused_computation.clone | custom fusion | bytes 32800 | tf_op jit(solution)/shard_map/jit(_take)/gather | solution.py:106
  2.8 0.1 fusion.37
  2.9 0.3 fusion.43
  3.1 0.2 fusion.30
  3.3 0.1 fusion.33
  3.4 1.1 fusion.11
  4.5 1.2 broadcast_in_dim.39
  5.7 17.6 %all-to-all-start = ((bf16[64,8,1024]{2,1,0:T(8,128)(2,1)}), bf16[64,8,1024]{2,1,0:T(8,128)(2,1)S(1)}, u32[]{:S(2)}, u32[]{:S(2)}) async-start(bf16[64,8,1024]{2,1,0:T(8,128)(2,1)} %bitcast.21), calls=%async_computation | async-start | bytes 2097152 | tf_op jit(solution)/shard_map/all_to_all | solution.py:79
  23.3 0.1 iota_compare_fusion
  23.4 0.3 multiply_reduce_fusion.2
  23.7 1.7 %fusion.1 = (f32[8,512]{1,0:T(8,128)S(1)}, f32[512,512,8]{1,0,2:T(8,128)S(1)}) fusion(pred[512,512]{0,1:T(8,128)(4,1)S(1)} %iota_compare_fusion, bf16[512,128]{1,0:T(8,128)(2,1)S(1)} %copy-done, bf16[512,1024]{1,0:T(8,128)(2,1)S(1)} %copy-done.2), kind=kOutput, calls=%fused_computation.5 | convolution fusion | flops 543158272 | bytes 9846784 | tf_op jit(solution)/shard_map/tkgd,skd->kgts/dot_general | solution.py:27
  25.4 3.2 %copy-done.1 = f32[512,512,8]{1,0,2:T(8,128)} copy-done((f32[512,512,8]{1,0,2:T(8,128)}, f32[512,512,8]{1,0,2:T(8,128)S(1)}, u32[]{:S(2)}) %copy-start.1) | copy-done | bytes 8388632
  28.6 1.7 %fusion = f32[8,512]{1,0:T(8,128)S(1)} fusion(f32[512,512,8]{1,0,2:T(8,128)S(1)} %get-tuple-element.21, f32[8,512]{1,0:T(8,128)S(1)} %get-tuple-element.20, pred[512,512]{0,1:T(8,128)(4,1)S(1)} %iota_compare_fusion), kind=kLoop, calls=%fused_computation.4 | loop fusion | flops 8384512 | bytes 8683520 | tf_op jit(solution)/shard_map/reduce_sum | solution.py:33
  30.4 25.9 %all-to-all-done = bf16[64,8,1024]{2,1,0:T(8,128)(2,1)S(1)} async-done(((bf16[64,8,1024]{2,1,0:T(8,128)(2,1)}), bf16[64,8,1024]{2,1,0:T(8,128)(2,1)S(1)}, u32[]{:S(2)}, u32[]{:S(2)}) %all-to-all-start) | async-done | bytes 1048608 | tf_op jit(solution)/shard_map/all_to_all | solution.py:79
  56.2 2.5 %collective-permute-start = (bf16[64,8,1024]{2,1,0:T(8,128)(2,1)S(1)}, bf16[64,8,1024]{2,1,0:T(8,128)(2,1)S(1)}, u32[]{:S(2)}, u32[]{:S(2)}) collective-permute-start(bf16[64,8,1024]{2,1,0:T(8,128)(2,1)S(1)} %all-to-all-done), channel_id=1, source_target_pairs={{0,8},{8,0},{1,9},{9,1},{2,10},{10,2},{3,11},{11,3},{4,12},{12,4},... | collective-permute-start | bytes 3145736 | tf_op jit(solution)/shard_map/ppermute | solution.py:71
  58.7 6.9 %multiply_reduce_fusion.1 = (f32[512]{0:T(512)S(1)}, bf16[8,512,128]{1,2,0:T(8,128)(2,1)}) fusion(bf16[512,128]{1,0:T(8,128)(2,1)S(1)} %copy-done.4, f32[8,512]{1,0:T(8,128)S(1)} %fusion, f32[8,512]{1,0:T(8,128)S(1)} %get-tuple-element.20, f32[512,512,8]{1,0,2:T(8,128)} %copy-done.1, pred[512,512]{0,1:T(8,128)(4,1)S(1)} %iota_compare_fusion), kind=kOutput, calls=%fused_computation.12 | convolution fusion | flops 549453312 | bytes 9865216 | tf_op jit(solution)/shard_map/kgts,skd->tkgd/dot_general | solution.py:34
  65.6 1.0 copy-done.3
  66.6 0.1 fusion.20
  66.8 0.5 multiply_reduce_fusion
  67.2 0.1 add.67
  67.3 1.9 %convolution_bitcast_fusion = f32[1,512,8,64]{1,3,2,0:T(8,128)S(1)} fusion(bf16[512,1024,1]{0,1,2:T(8,128)(2,1)} %bitcast.151, bf16[8,64,1024]{2,1,0:T(8,128)(2,1)S(1)} %bitcast.138), kind=kOutput, calls=%fused_computation.15 | convolution fusion | flops 536870912 | bytes 3145728 | tf_op jit(solution)/shard_map/dot_general | solution.py:45
  69.3 2.0 %fusion.17 = f32[512,512]{1,0:T(8,128)S(1)} fusion(bf16[512,1024]{1,0:T(8,128)(2,1)S(1)} %copy-done.2, bf16[64,8,1024]{2,1,0:T(8,128)(2,1)S(1)} %all-to-all-done, bf16[64,8,1024]{2,1,0:T(8,128)(2,1)} %copy-done.3, pred[]{:T(512)S(6)} %eq.5), kind=kOutput, calls=%fused_computation.30 | convolution fusion | flops 537395200 | bytes 4194305 | tf_op jit(solution)/shard_map/dot_general | solution.py:45
  71.3 0.3 fusion.5
  71.6 1.6 %copy.46 = f32[2,512,8,64]{1,3,0,2:T(8,128)} copy(f32[2,512,8,64]{1,3,2,0:T(8,128)S(1)} %fusion.5) | data formatting | bytes 4194304 | tf_op jit(solution)/shard_map/sub | solution.py:117
  73.2 4.0 %all-to-all-start.1 = ((f32[2,512,8,64]{1,3,0,2:T(8,128)}), f32[2,512,8,64]{1,3,0,2:T(8,128)S(1)}, u32[]{:S(2)}, u32[]{:S(2)}) async-start(f32[2,512,8,64]{1,3,0,2:T(8,128)} %copy.46), calls=%async_computation.1 | async-start | bytes 4194304 | tf_op jit(solution)/shard_map/all_to_all | solution.py:120
  77.2 0.1 fusion.39
  77.3 26.7 %all-to-all-done.1 = f32[2,512,8,64]{1,3,0,2:T(8,128)S(1)} async-done(((f32[2,512,8,64]{1,3,0,2:T(8,128)}), f32[2,512,8,64]{1,3,0,2:T(8,128)S(1)}, u32[]{:S(2)}, u32[]{:S(2)}) %all-to-all-start.1) | async-done | bytes 2097184 | tf_op jit(solution)/shard_map/all_to_all | solution.py:120
  103.9 0.2 reduce_sum.169
  104.2 0.1 exponential_convert_fusion
  104.3 0.8 broadcast_in_dim.41
  105.1 3.7 %all-to-all-start.2 = ((bf16[8,512,64]{1,2,0:T(8,128)(2,1)}), bf16[8,512,64]{1,2,0:T(8,128)(2,1)S(1)}, u32[]{:S(2)}, u32[]{:S(2)}) async-start(bf16[8,512,64]{1,2,0:T(8,128)(2,1)} %broadcast_in_dim.41), calls=%async_computation.2 | async-start | bytes 1048576 | tf_op jit(solution)/shard_map/all_to_all | solution.py:91
  108.8 0.1 convert_reduce_fusion
  108.9 0.2 fusion.25
  109.1 9.1 %all-to-all-done.2 = bf16[8,512,64]{1,2,0:T(8,128)(2,1)S(1)} async-done(((bf16[8,512,64]{1,2,0:T(8,128)(2,1)}), bf16[8,512,64]{1,2,0:T(8,128)(2,1)S(1)}, u32[]{:S(2)}, u32[]{:S(2)}) %all-to-all-start.2) | async-done | bytes 524320 | tf_op jit(solution)/shard_map/all_to_all | solution.py:91
  118.2 0.1 bitcast_reduce_fusion
  118.4 0.1 div.104
  118.5 0.1 bitcast_subtract_fusion
  118.7 2.1 %convolution_bitcast_fusion.1 = f32[64,64,8]{0,1,2:T(8,128)S(1)} fusion(f32[64,8,512]{2,1,0:T(8,128)S(1)} %bitcast.139, f32[64]{0:T(128)S(1)} %broadcast_multiply_fusion.3, bf16[2,512,64]{1,2,0:T(8,128)(2,1)S(1)} %exponential_convert_fusion), kind=kOutput, calls=%fused_computation.16 | convolution fusion | flops 201392128 | bytes 1245696 | tf_op jit(solution)/shard_map/dot_general | solution.py:138
  120.8 0.2 bitcast_dynamic-update-slice_fusion
  121.1 0.3 fusion.16
  121.6 0.2 copy.51
  121.8 22.1 %all_to_all.27 = f32[64,1,656]{2,1,0:T(1,128)S(1)} all-to-all(f32[64,1,656]{2,1,0:T(1,128)S(1)} %copy.51), channel_id=1, replica_groups=mesh['z'=8,'y_hi'=4,'core'=2,'x'=4,'y_lo'=2] {'z','y_hi','core'}, dimensions={0} | all-to-all | bytes 335872 | tf_op jit(solution)/shard_map/all_to_all | solution.py:160
  144.0 0.1 slice_reduce_fusion.1
  144.1 0.1 slice_reduce_fusion.2
  144.2 0.1 reduce_sum.175
  144.4 0.1 multiply_reduce_fusion.3
  144.5 0.7 rsqrt_multiply_fusion
  (38 shorter events, 0.7 us)
Async XLA Ops:
  0.0 2.9 %copy-start = (bf16[512,128]{1,0:T(8,128)(2,1)S(1)}, bf16[512,128]{1,0:T(8,128)(2,1)}, u32[]{:S(2)}) copy-start(bf16[512,128]{1,0:T(8,128)(2,1)} %param.9) | copy-start | bytes 393220
  0.0 23.4 %copy-start.2 = (bf16[512,1024]{1,0:T(8,128)(2,1)S(1)}, bf16[512,1024]{1,0:T(8,128)(2,1)}, u32[]{:S(2)}) copy-start(bf16[512,1024]{1,0:T(8,128)(2,1)} %param.8) | copy-start | bytes 3145732
  5.7 50.5 %all-to-all-start = ((bf16[64,8,1024]{2,1,0:T(8,128)(2,1)}), bf16[64,8,1024]{2,1,0:T(8,128)(2,1)S(1)}, u32[]{:S(2)}, u32[]{:S(2)}) async-start(bf16[64,8,1024]{2,1,0:T(8,128)(2,1)} %bitcast.21), calls=%async_computation | async-start | bytes 2097152 | tf_op jit(solution)/shard_map/all_to_all | solution.py:79
  25.4 3.2 %copy-start.1 = (f32[512,512,8]{1,0,2:T(8,128)}, f32[512,512,8]{1,0,2:T(8,128)S(1)}, u32[]{:S(2)}) copy-start(f32[512,512,8]{1,0,2:T(8,128)S(1)} %get-tuple-element.21) | copy-start | bytes 25165828
  28.6 30.1 %copy-start.4 = (bf16[512,128]{1,0:T(8,128)(2,1)S(1)}, bf16[512,128]{1,0:T(8,128)(2,1)}, u32[]{:S(2)}) copy-start(bf16[512,128]{1,0:T(8,128)(2,1)} %param.10) | copy-start | bytes 393220
  56.2 9.4 %collective-permute-start = (bf16[64,8,1024]{2,1,0:T(8,128)(2,1)S(1)}, bf16[64,8,1024]{2,1,0:T(8,128)(2,1)S(1)}, u32[]{:S(2)}, u32[]{:S(2)}) collective-permute-start(bf16[64,8,1024]{2,1,0:T(8,128)(2,1)S(1)} %all-to-all-done), channel_id=1, source_target_pairs={{0,8},{8,0},{1,9},{9,1},{2,10},{10,2},{3,11},{11,3},{4,12},{12,4},... | collective-permute-start | bytes 3145736 | tf_op jit(solution)/shard_map/ppermute | solution.py:71
  65.6 1.0 copy-start.3
  71.5 5.6 %copy-start.5 = (f32[512]{0:T(512)S(1)}, f32[512]{0:T(512)}, u32[]{:S(2)}) copy-start(f32[512]{0:T(512)} %param.13) | copy-start | bytes 6148
  71.6 5.6 %copy-start.6 = (f32[512]{0:T(512)S(1)}, f32[512]{0:T(512)}, u32[]{:S(2)}) copy-start(f32[512]{0:T(512)} %param.12) | copy-start | bytes 6148
  73.2 30.8 %all-to-all-start.1 = ((f32[2,512,8,64]{1,3,0,2:T(8,128)}), f32[2,512,8,64]{1,3,0,2:T(8,128)S(1)}, u32[]{:S(2)}, u32[]{:S(2)}) async-start(f32[2,512,8,64]{1,3,0,2:T(8,128)} %copy.46), calls=%async_computation.1 | async-start | bytes 4194304 | tf_op jit(solution)/shard_map/all_to_all | solution.py:120
  105.1 13.1 %all-to-all-start.2 = ((bf16[8,512,64]{1,2,0:T(8,128)(2,1)}), bf16[8,512,64]{1,2,0:T(8,128)(2,1)S(1)}, u32[]{:S(2)}, u32[]{:S(2)}) async-start(bf16[8,512,64]{1,2,0:T(8,128)(2,1)} %broadcast_in_dim.41), calls=%async_computation.2 | async-start | bytes 1048576 | tf_op jit(solution)/shard_map/all_to_all | solution.py:91

commit v7 on v6

--- a/solution.py
+++ b/solution.py
@@ -51,7 +51,7 @@
     length = queries.shape[0]
     kv_heads = key_rows.shape[1] // HEAD_DIM
     group_size = queries.shape[1] // HEAD_DIM // kv_heads
-    picked = jnp.take(queries, rows, axis=0)
+    picked = pick_rows(queries, rows)
     query_four = picked.reshape(rows.shape[0], kv_heads, group_size, HEAD_DIM)
     key_three = key_rows.reshape(length, kv_heads, HEAD_DIM)
     value_three = value_rows.reshape(length, kv_heads, HEAD_DIM)
@@ -67,6 +67,13 @@
     return mixture.astype(jnp.bfloat16).reshape(rows.shape[0], queries.shape[1])
 
 
+def pick_rows(matrix, rows):
+    hits = rows[:, None] == lax.broadcasted_iota(jnp.int32, (rows.shape[0], matrix.shape[0]), 1)
+    return jnp.dot(
+        hits.astype(matrix.dtype), matrix, preferred_element_type=jnp.float32
+    ).astype(matrix.dtype)
+
+
 def swap_cores(piece):
     return lax.ppermute(piece, CORE, [(0, 1), (1, 0)])
 
@@ -103,7 +110,7 @@
 
     own_rows = landmark_index % length
     gathered = gather_marks(
-        jnp.take(queries, own_rows, axis=0),
+        pick_rows(queries, own_rows),
         attend_rows(queries, key_rows, value_rows, own_rows),
     )
     landmark_piece = gathered.reshape(2, landmarks, queries.shape[1])
@@ -112,38 +119,38 @@
     row_norms = jnp.stack([squares_by_row(queries), squares_by_row(attended)])
     mark_norms = squares_by_row(landmark_piece)
     cross = jnp.stack(
-        [inner_rows(queries, landmark_piece[0]), inner_rows(attended, landmark_piece[1])]
-    )
-    distance_part = row_norms[:, :, None] + mark_norms[:, None, :] - 2.0 * cross
-    distance_part = distance_part.reshape(2, length, model_count, row_share)
+        [inner_rows(landmark_piece[0], queries), inner_rows(landmark_piece[1], attended)]
+    )
+    distance_part = mark_norms[:, :, None] + row_norms[:, None, :] - 2.0 * cross
+    distance_part = jnp.transpose(
+        distance_part.reshape(2, model_count, row_share, length), (1, 0, 2, 3)
+    )
     distance = jnp.sum(
-        lax.all_to_all(distance_part, MODEL, 2, 2, tiled=True), axis=2
+        lax.all_to_all(distance_part, MODEL, 0, 0, tiled=True), axis=0
     )
 
     widths = lax.dynamic_slice_in_dim(
         jnp.stack([radius_in, radius_out]), model_index * row_share, row_share, 1
     )
-    features = jnp.exp(-distance / (D * widths[:, None, :])).astype(jnp.bfloat16)
+    features = jnp.exp(-distance / (D * widths[:, :, None])).astype(jnp.bfloat16)
     row_features = features[0]
-    column_features = jnp.transpose(
-        broadcast_gather(features[1], MODEL), (1, 0, 2)
-    ).reshape(length, landmarks)
+    column_features = broadcast_gather(features[1], MODEL).reshape(landmarks, length)
 
     rows32 = row_features.astype(jnp.float32)
     columns32 = column_features.astype(jnp.float32)
-    row_mean = jnp.mean(rows32, axis=0)
-    column_mean = jnp.mean(columns32, axis=0)
-    rows_centered = rows32 - row_mean[None, :]
-    columns_centered = columns32 - column_mean[None, :]
+    row_mean = jnp.mean(rows32, axis=1)
+    column_mean = jnp.mean(columns32, axis=1)
+    rows_centered = rows32 - row_mean[:, None]
+    columns_centered = columns32 - column_mean[:, None]
     second = lax.dot_general(
         rows_centered,
         columns_centered,
-        (((0,), (0,)), ((), ())),
+        (((1,), (1,)), ((), ())),
         precision=lax.Precision.HIGHEST,
         preferred_element_type=jnp.float32,
     )
-    row_square = jnp.sum(jnp.square(rows_centered), axis=0)
-    column_square = jnp.sum(jnp.square(columns_centered), axis=0)
+    row_square = jnp.sum(jnp.square(rows_centered), axis=1)
+    column_square = jnp.sum(jnp.square(columns_centered), axis=1)
 
     packed = jnp.concatenate(
         [

time: 146 us -> 142 us (0.973)
  local copies, waits for them, and re-layouts: 10.8 us -> 7.86 us
    gather x1 -> x0, local copies, waits for them, and re-layouts: 1.94 us -> none  [shards(): jnp.take(queries, own_rows, axis=0)]
    sub x1 -> x0, local copies, waits for them, and re-layouts: 1.58 us -> none  [shards(): distance_part = row_norms[:, :, None] + mark_norms[:, None, :] - 2.0 * cross]
    transpose x0 -> x1, local copies, waits for them, and re-layouts: none -> 1.58 us  [shards(): jnp.transpose(distance_part.reshape(2, model_count, row_share, length), (...]
    dot_general x1 -> x2, matrix products: 2.11 us -> 3.61 us  [the longest x1 2.11 us: shards(): lax.dot_general(rows_centered, columns_centered, (((1,), (1,)), ((), ()))...]
    unnamed x19 -> x17, local copies, waits for them, and re-layouts: 4.54 us -> 3.55 us
where the time goes in v7:
time: 142 us
  waiting for transfers between devices  61.1 us (43%)
  starting transfers between devices  27.8 us (20%)
  blocking collectives  22.2 us (16%)
  matrix products  16.2 us (11%)
  local copies, waits for them, and re-layouts  7.86 us (6%)
  other arithmetic  6.41 us (5%)
    all_to_all x1, waiting for transfers between devices, shards(): lax.all_to_all(distance_part, MODEL, 0, 0, tiled=True)  26.7 us
    all_to_all x1, waiting for transfers between devices, gather_marks(): lax.all_to_all(spread.reshape((data_count,) + query_marks.shape), DATA, 0...  25.9 us
    all_to_all x1, blocking collectives, shards(): received = lax.all_to_all(packed, DATA, 0, 0, tiled=True)  22.2 us
    all_to_all x1, starting transfers between devices, gather_marks(): lax.all_to_all(spread.reshape((data_count,) + query_marks.shape), DATA, 0...  17.6 us
    all_to_all x1, waiting for transfers between devices, broadcast_gather(): return lax.all_to_all(spread, axis_name, 0, 0, tiled=True)  8.46 us
    dot_general x1, matrix products, attend(): jnp.einsum('kgts,skd->tkgd', weights, value_three, preferred_element_type...  6.86 us
    all_to_all x1, starting transfers between devices, shards(): lax.all_to_all(distance_part, MODEL, 0, 0, tiled=True)  4.02 us
    all_to_all x1, starting transfers between devices, broadcast_gather(): return lax.all_to_all(spread, axis_name, 0, 0, tiled=True)  3.67 us
  transfers between devices with their start and end apart: 4, of which 3 were waited for; matrix products, arithmetic and copies ran while one was open for 8% of the time, Pallas kernels for 0%

profile of v7, /device:TPU:1, one launch (start us, length us, event | category | flops | bytes accessed | tf_op | source)
XLA Modules:
  0.0 141.7 jit_solution(4668530162877877967)
XLA Ops:
  0.0 0.8 and_select_fusion
  0.8 0.1 iota_compare_fusion.1
  0.8 1.5 %convolution_convert_fusion.1 = bf16[8,1024]{1,0:T(8,128)(2,1)S(1)} fusion(bf16[512,1024]{1,0:T(8,128)(2,1)} %param.6, s32[8]{0:T(128)S(1)} %and_select_fusion), kind=kOutput, calls=%fused_computation.24 | convolution fusion | flops 8400896 | bytes 1064992 | tf_op jit(solution)/shard_map/dot_general | solution.py:72
  2.3 0.3 fusion.39
  2.6 0.2 fusion.27
  2.8 0.1 fusion.30
  2.9 1.1 fusion.12
  4.0 1.2 broadcast_in_dim.28
  5.2 17.6 %all-to-all-start = ((bf16[64,8,1024]{2,1,0:T(8,128)(2,1)}), bf16[64,8,1024]{2,1,0:T(8,128)(2,1)S(1)}, u32[]{:S(2)}, u32[]{:S(2)}) async-start(bf16[64,8,1024]{2,1,0:T(8,128)(2,1)} %bitcast.12), calls=%async_computation | async-start | bytes 2097152 | tf_op jit(solution)/shard_map/all_to_all | solution.py:86
  22.8 0.1 iota_compare_fusion
  22.9 0.3 multiply_reduce_fusion.2
  23.2 1.7 %fusion.1 = (f32[8,512]{1,0:T(8,128)S(1)}, f32[512,512,8]{1,0,2:T(8,128)S(1)}) fusion(pred[512,512]{0,1:T(8,128)(4,1)S(1)} %iota_compare_fusion, bf16[512,128]{1,0:T(8,128)(2,1)S(1)} %copy-done, bf16[512,1024]{1,0:T(8,128)(2,1)S(1)} %copy-done.2), kind=kOutput, calls=%fused_computation.4 | convolution fusion | flops 543158272 | bytes 9846784 | tf_op jit(solution)/shard_map/tkgd,skd->kgts/dot_general | solution.py:27
  24.9 3.2 %copy-done.1 = f32[512,512,8]{1,0,2:T(8,128)} copy-done((f32[512,512,8]{1,0,2:T(8,128)}, f32[512,512,8]{1,0,2:T(8,128)S(1)}, u32[]{:S(2)}) %copy-start.1) | copy-done | bytes 8388632
  28.1 1.7 %fusion = f32[8,512]{1,0:T(8,128)S(1)} fusion(f32[512,512,8]{1,0,2:T(8,128)S(1)} %get-tuple-element.20, f32[8,512]{1,0:T(8,128)S(1)} %get-tuple-element.19, pred[512,512]{0,1:T(8,128)(4,1)S(1)} %iota_compare_fusion), kind=kLoop, calls=%fused_computation.3 | loop fusion | flops 8384512 | bytes 8683520 | tf_op jit(solution)/shard_map/reduce_sum | solution.py:33
  29.8 25.9 %all-to-all-done = bf16[64,8,1024]{2,1,0:T(8,128)(2,1)S(1)} async-done(((bf16[64,8,1024]{2,1,0:T(8,128)(2,1)}), bf16[64,8,1024]{2,1,0:T(8,128)(2,1)S(1)}, u32[]{:S(2)}, u32[]{:S(2)}) %all-to-all-start) | async-done | bytes 1048608 | tf_op jit(solution)/shard_map/all_to_all | solution.py:86
  55.7 2.5 %collective-permute-start = (bf16[64,8,1024]{2,1,0:T(8,128)(2,1)S(1)}, bf16[64,8,1024]{2,1,0:T(8,128)(2,1)S(1)}, u32[]{:S(2)}, u32[]{:S(2)}) collective-permute-start(bf16[64,8,1024]{2,1,0:T(8,128)(2,1)S(1)} %all-to-all-done), channel_id=1, source_target_pairs={{0,8},{8,0},{1,9},{9,1},{2,10},{10,2},{3,11},{11,3},{4,12},{12,4},... | collective-permute-start | bytes 3145736 | tf_op jit(solution)/shard_map/ppermute | solution.py:78
  58.2 6.9 %multiply_reduce_fusion.1 = (f32[512]{0:T(512)S(1)}, bf16[8,512,128]{1,2,0:T(8,128)(2,1)}) fusion(bf16[512,128]{1,0:T(8,128)(2,1)S(1)} %copy-done.3, f32[8,512]{1,0:T(8,128)S(1)} %fusion, f32[8,512]{1,0:T(8,128)S(1)} %get-tuple-element.19, f32[512,512,8]{1,0,2:T(8,128)} %copy-done.1, pred[512,512]{0,1:T(8,128)(4,1)S(1)} %iota_compare_fusion), kind=kOutput, calls=%fused_computation.12 | convolution fusion | flops 549453312 | bytes 9865216 | tf_op jit(solution)/shard_map/kgts,skd->tkgd/dot_general | solution.py:34
  65.1 0.1 broadcast_select_fusion.1
  65.3 0.7 convolution_bitcast_fusion.1
  66.0 0.5 multiply_reduce_fusion
  66.5 0.1 add.63
  66.6 1.9 %convolution_bitcast_fusion = f32[1,8,64,512]{3,2,1,0:T(8,128)S(1)} fusion(bf16[8,64,1024]{2,1,0:T(8,128)(2,1)S(1)} %bitcast.126, bf16[512,1024,1]{0,1,2:T(8,128)(2,1)} %bitcast.142), kind=kOutput, calls=%fused_computation.15 | convolution fusion | flops 536870912 | bytes 3145728 | tf_op jit(solution)/shard_map/dot_general | solution.py:45
  68.5 0.3 fusion.6
  68.8 1.6 %copy.45 = f32[8,2,64,512]{3,2,1,0:T(8,128)} copy(f32[8,2,64,512]{3,2,0,1:T(8,128)S(1)} %fusion.6) | data formatting | bytes 4194304 | tf_op jit(solution)/shard_map/transpose | solution.py:125
  70.4 4.0 %all-to-all-start.1 = ((f32[8,2,64,512]{3,2,1,0:T(8,128)}), f32[8,2,64,512]{3,2,1,0:T(8,128)S(1)}, u32[]{:S(2)}, u32[]{:S(2)}) async-start(f32[8,2,64,512]{3,2,1,0:T(8,128)} %copy.45), calls=%async_computation.1 | async-start | bytes 4194304 | tf_op jit(solution)/shard_map/all_to_all | solution.py:129
  74.4 0.1 fusion.35
  74.5 26.7 %all-to-all-done.1 = f32[8,2,64,512]{3,2,1,0:T(8,128)S(1)} async-done(((f32[8,2,64,512]{3,2,1,0:T(8,128)}), f32[8,2,64,512]{3,2,1,0:T(8,128)S(1)}, u32[]{:S(2)}, u32[]{:S(2)}) %all-to-all-start.1) | async-done | bytes 2097184 | tf_op jit(solution)/shard_map/all_to_all | solution.py:129
  101.2 0.2 reduce_sum.169
  101.5 0.1 exponential_convert_fusion
  101.6 0.8 broadcast_in_dim.32
  102.4 3.7 %all-to-all-start.2 = ((bf16[8,64,512]{2,1,0:T(8,128)(2,1)}), bf16[8,64,512]{2,1,0:T(8,128)(2,1)S(1)}, u32[]{:S(2)}, u32[]{:S(2)}) async-start(bf16[8,64,512]{2,1,0:T(8,128)(2,1)} %broadcast_in_dim.32), calls=%async_computation.2 | async-start | bytes 1048576 | tf_op jit(solution)/shard_map/all_to_all | solution.py:98
  106.1 0.1 convert_reduce_fusion.1
  106.2 0.2 fusion.22
  106.4 8.5 %all-to-all-done.2 = bf16[8,64,512]{2,1,0:T(8,128)(2,1)S(1)} async-done(((bf16[8,64,512]{2,1,0:T(8,128)(2,1)}), bf16[8,64,512]{2,1,0:T(8,128)(2,1)S(1)}, u32[]{:S(2)}, u32[]{:S(2)}) %all-to-all-start.2) | async-done | bytes 524320 | tf_op jit(solution)/shard_map/all_to_all | solution.py:98
  114.9 0.1 convert_reduce_fusion
  115.1 0.1 div.102
  115.1 0.3 multiply_reduce_fusion.3
  115.4 2.1 %convolution_bitcast_fusion.2 = f32[64,64,8]{0,1,2:T(8,128)S(1)} fusion(f32[64,8,512]{2,1,0:T(8,128)S(1)} %bitcast.129, f32[64]{0:T(128)S(1)} %broadcast_multiply_fusion.3, bf16[2,64,512]{2,1,0:T(8,128)(2,1)S(1)} %exponential_convert_fusion), kind=kOutput, calls=%fused_computation.19 | convolution fusion | flops 201392128 | bytes 1245696 | tf_op jit(solution)/shard_map/dot_general | solution.py:145
  117.5 0.2 bitcast_dynamic-update-slice_fusion
  117.7 0.1 broadcast_dynamic-update-slice_fusion.1
  117.9 0.1 copy.49
  118.1 0.2 copy.50
  118.3 22.2 %all_to_all.27 = f32[64,1,656]{2,1,0:T(1,128)S(1)} all-to-all(f32[64,1,656]{2,1,0:T(1,128)S(1)} %copy.50), channel_id=1, replica_groups=mesh['z'=8,'y_hi'=4,'core'=2,'x'=4,'y_lo'=2] {'z','y_hi','core'}, dimensions={0} | all-to-all | bytes 335872 | tf_op jit(solution)/shard_map/all_to_all | solution.py:167
  140.5 0.1 slice_reduce_fusion.1
  140.6 0.1 slice_reduce_fusion.2
  140.7 0.1 reduce_sum.175
  140.9 0.1 multiply_reduce_fusion.4
  141.1 0.7 rsqrt_multiply_fusion
  (31 shorter events, 0.4 us)
Async XLA Ops:
  0.0 2.3 %copy-start = (bf16[512,128]{1,0:T(8,128)(2,1)S(1)}, bf16[512,128]{1,0:T(8,128)(2,1)}, u32[]{:S(2)}) copy-start(bf16[512,128]{1,0:T(8,128)(2,1)} %param.7) | copy-start | bytes 393220
  0.0 22.9 %copy-start.2 = (bf16[512,1024]{1,0:T(8,128)(2,1)S(1)}, bf16[512,1024]{1,0:T(8,128)(2,1)}, u32[]{:S(2)}) copy-start(bf16[512,1024]{1,0:T(8,128)(2,1)} %param.6) | copy-start | bytes 3145732
  5.2 50.6 %all-to-all-start = ((bf16[64,8,1024]{2,1,0:T(8,128)(2,1)}), bf16[64,8,1024]{2,1,0:T(8,128)(2,1)S(1)}, u32[]{:S(2)}, u32[]{:S(2)}) async-start(bf16[64,8,1024]{2,1,0:T(8,128)(2,1)} %bitcast.12), calls=%async_computation | async-start | bytes 2097152 | tf_op jit(solution)/shard_map/all_to_all | solution.py:86
  24.9 3.2 %copy-start.1 = (f32[512,512,8]{1,0,2:T(8,128)}, f32[512,512,8]{1,0,2:T(8,128)S(1)}, u32[]{:S(2)}) copy-start(f32[512,512,8]{1,0,2:T(8,128)S(1)} %get-tuple-element.20) | copy-start | bytes 25165828
  28.1 30.1 %copy-start.3 = (bf16[512,128]{1,0:T(8,128)(2,1)S(1)}, bf16[512,128]{1,0:T(8,128)(2,1)}, u32[]{:S(2)}) copy-start(bf16[512,128]{1,0:T(8,128)(2,1)} %param.8) | copy-start | bytes 393220
  55.7 9.4 %collective-permute-start = (bf16[64,8,1024]{2,1,0:T(8,128)(2,1)S(1)}, bf16[64,8,1024]{2,1,0:T(8,128)(2,1)S(1)}, u32[]{:S(2)}, u32[]{:S(2)}) collective-permute-start(bf16[64,8,1024]{2,1,0:T(8,128)(2,1)S(1)} %all-to-all-done), channel_id=1, source_target_pairs={{0,8},{8,0},{1,9},{9,1},{2,10},{10,2},{3,11},{11,3},{4,12},{12,4},... | collective-permute-start | bytes 3145736 | tf_op jit(solution)/shard_map/ppermute | solution.py:78
  68.8 5.6 %copy-start.4 = (f32[512]{0:T(512)S(1)}, f32[512]{0:T(512)}, u32[]{:S(2)}) copy-start(f32[512]{0:T(512)} %param.11) | copy-start | bytes 6148
  68.8 5.6 %copy-start.5 = (f32[512]{0:T(512)S(1)}, f32[512]{0:T(512)}, u32[]{:S(2)}) copy-start(f32[512]{0:T(512)} %param.10) | copy-start | bytes 6148
  70.4 30.8 %all-to-all-start.1 = ((f32[8,2,64,512]{3,2,1,0:T(8,128)}), f32[8,2,64,512]{3,2,1,0:T(8,128)S(1)}, u32[]{:S(2)}, u32[]{:S(2)}) async-start(f32[8,2,64,512]{3,2,1,0:T(8,128)} %copy.45), calls=%async_computation.1 | async-start | bytes 4194304 | tf_op jit(solution)/shard_map/all_to_all | solution.py:129
  102.4 12.5 %all-to-all-start.2 = ((bf16[8,64,512]{2,1,0:T(8,128)(2,1)}), bf16[8,64,512]{2,1,0:T(8,128)(2,1)S(1)}, u32[]{:S(2)}, u32[]{:S(2)}) async-start(bf16[8,64,512]{2,1,0:T(8,128)(2,1)} %broadcast_in_dim.32), calls=%async_computation.2 | async-start | bytes 1048576 | tf_op jit(solution)/shard_map/all_to_all | solution.py:98

commit v8 on v7

--- a/solution.py
+++ b/solution.py
@@ -79,17 +79,12 @@
 
 
 def gather_marks(query_marks, output_marks):
-    first = lax.axis_index(CORE) == 0
     data_count = lax.axis_size(DATA)
     kinds = jnp.stack([query_marks, output_marks])
     spread = jnp.broadcast_to(kinds[None], (data_count // 2,) + kinds.shape)
-    fetched = lax.all_to_all(
+    return lax.all_to_all(
         spread.reshape((data_count,) + query_marks.shape), DATA, 0, 0, tiled=True
     )
-    swapped = swap_cores(fetched)
-    query_rows = jnp.where(first, fetched, swapped)
-    output_rows = jnp.where(first, swapped, fetched)
-    return jnp.stack([query_rows, output_rows])
 
 
 def broadcast_gather(piece, axis_name):
@@ -109,19 +104,20 @@
     token_count = length * data_count
 
     own_rows = landmark_index % length
-    gathered = gather_marks(
+    first = lax.axis_index(CORE) == 0
+    marks = gather_marks(
         pick_rows(queries, own_rows),
         attend_rows(queries, key_rows, value_rows, own_rows),
-    )
-    landmark_piece = gathered.reshape(2, landmarks, queries.shape[1])
+    ).reshape(landmarks, queries.shape[1])
     attended = attend(queries, key_rows, value_rows)
+    own_side = jnp.where(first, queries, attended)
+    other_side = swap_cores(jnp.where(first, attended, queries))
+    tokens = jnp.stack([own_side, other_side])
 
-    row_norms = jnp.stack([squares_by_row(queries), squares_by_row(attended)])
-    mark_norms = squares_by_row(landmark_piece)
-    cross = jnp.stack(
-        [inner_rows(landmark_piece[0], queries), inner_rows(landmark_piece[1], attended)]
-    )
-    distance_part = mark_norms[:, :, None] + row_norms[:, None, :] - 2.0 * cross
+    row_norms = squares_by_row(tokens)
+    mark_norms = squares_by_row(marks)
+    cross = jnp.stack([inner_rows(marks, tokens[0]), inner_rows(marks, tokens[1])])
+    distance_part = mark_norms[None, :, None] + row_norms[:, None, :] - 2.0 * cross
     distance_part = jnp.transpose(
         distance_part.reshape(2, model_count, row_share, length), (1, 0, 2, 3)
     )
@@ -129,12 +125,13 @@
         lax.all_to_all(distance_part, MODEL, 0, 0, tiled=True), axis=0
     )
 
-    widths = lax.dynamic_slice_in_dim(
-        jnp.stack([radius_in, radius_out]), model_index * row_share, row_share, 1
-    )
-    features = jnp.exp(-distance / (D * widths[:, :, None])).astype(jnp.bfloat16)
-    row_features = features[0]
-    column_features = broadcast_gather(features[1], MODEL).reshape(landmarks, length)
+    radius = jnp.where(first, radius_in, radius_out)
+    widths = lax.dynamic_slice_in_dim(radius, model_index * row_share, row_share, 0)
+    side = jnp.exp(-distance / (D * widths[None, :, None])).astype(jnp.bfloat16)
+    handed = swap_cores(side[1])
+    row_features = jnp.where(first, side[0], handed)
+    own_columns = jnp.where(first, handed, side[0])
+    column_features = broadcast_gather(own_columns, MODEL).reshape(landmarks, length)
 
     rows32 = row_features.astype(jnp.float32)
     columns32 = column_features.astype(jnp.float32)

time: 142 us -> 139 us (0.979)
  waiting for transfers between devices: 61.1 us -> 55.4 us
  starting transfers between devices: 27.8 us -> 31.4 us
  matrix products: 16.2 us -> 14.7 us
    all_to_all x1, waiting for transfers between devices: 25.9 us -> 17.2 us  [gather_marks(): lax.all_to_all(spread.reshape((data_count,) + query_marks.shape), DATA, 0...]
    ppermute x1 -> x2, starting transfers between devices: 2.48 us -> 6.05 us  [swap_cores(): return lax.ppermute(piece, CORE, [(0, 1), (1, 0)])]
    dot_general x1, matrix products: 6.86 us -> 3.33 us  [attend(): jnp.einsum('kgts,skd->tkgd', weights, value_three, preferred_element_type...]
    ppermute x1 -> x2, waiting for transfers between devices: 0.01 us -> 3.14 us  [swap_cores(): return lax.ppermute(piece, CORE, [(0, 1), (1, 0)])]
    unnamed x17, local copies, waits for them, and re-layouts: 3.55 us -> 1.37 us
    reshape x0 -> x1, local copies, waits for them, and re-layouts: none -> 1.48 us  [attend(): return mixture.astype(jnp.bfloat16).reshape(length, queries.shape[1])]
  transfers between devices with their start and end apart: 4 -> 5, of which waited for: 3 -> 5; matrix products, arithmetic and copies ran while one was open for 8% -> 7% of each run, Pallas kernels for 0% -> 0%
where the time goes in v8:
time: 139 us
  waiting for transfers between devices  55.4 us (40%)
  starting transfers between devices  31.4 us (23%)
  blocking collectives  22.3 us (16%)
  matrix products  14.7 us (11%)
  other arithmetic  7.72 us (6%)
  local copies, waits for them, and re-layouts  7.06 us (5%)
    all_to_all x1, waiting for transfers between devices, shards(): lax.all_to_all(distance_part, MODEL, 0, 0, tiled=True)  26 us
    all_to_all x1, blocking collectives, shards(): received = lax.all_to_all(packed, DATA, 0, 0, tiled=True)  22.3 us
    all_to_all x1, starting transfers between devices, gather_marks(): lax.all_to_all(spread.reshape((data_count,) + query_marks.shape), DATA, 0...  17.6 us
    all_to_all x1, waiting for transfers between devices, gather_marks(): lax.all_to_all(spread.reshape((data_count,) + query_marks.shape), DATA, 0...  17.2 us
    all_to_all x1, waiting for transfers between devices, broadcast_gather(): return lax.all_to_all(spread, axis_name, 0, 0, tiled=True)  9 us
    ppermute x2, starting transfers between devices, swap_cores(): return lax.ppermute(piece, CORE, [(0, 1), (1, 0)])  6.05 us
    all_to_all x1, starting transfers between devices, shards(): lax.all_to_all(distance_part, MODEL, 0, 0, tiled=True)  4.01 us
    dot_general x2, matrix products, inner_rows(): lax.dot_general(left, right, (((1,), (1,)), ((), ())), preferred_element_...  3.71 us
  transfers between devices with their start and end apart: 5, of which 5 were waited for; matrix products, arithmetic and copies ran while one was open for 7% of the time, Pallas kernels for 0%

profile of v8, /device:TPU:1, one launch (start us, length us, event | category | flops | bytes accessed | tf_op | source)
XLA Modules:
  0.0 138.8 jit_solution(4815169562554544886)
XLA Ops:
  0.0 0.7 and_select_fusion
  0.8 1.5 %convolution_convert_fusion.1 = bf16[8,1024]{1,0:T(8,128)(2,1)S(1)} fusion(bf16[512,1024]{1,0:T(8,128)(2,1)} %param.6, s32[8]{0:T(128)S(1)} %and_select_fusion), kind=kOutput, calls=%fused_computation.21 | convolution fusion | flops 8400896 | bytes 1064992 | tf_op jit(solution)/shard_map/dot_general | solution.py:72
  2.3 0.3 fusion.37
  2.5 0.2 fusion.28
  2.7 0.1 fusion.31
  2.8 1.1 fusion.12
  3.9 1.1 broadcast_in_dim.26
  5.0 17.6 %all-to-all-start = ((bf16[64,8,1024]{2,1,0:T(8,128)(2,1)}), bf16[64,8,1024]{2,1,0:T(8,128)(2,1)S(1)}, u32[]{:S(2)}, u32[]{:S(2)}) async-start(bf16[64,8,1024]{2,1,0:T(8,128)(2,1)} %bitcast.12), calls=%async_computation | async-start | bytes 2097152 | tf_op jit(solution)/shard_map/all_to_all | solution.py:85
  22.7 0.1 iota_compare_fusion
  22.8 2.7 %fusion.1 = (f32[8,512]{1,0:T(8,128)S(1)}, f32[512,512,8]{1,0,2:T(8,128)S(1)}) fusion(pred[512,512]{0,1:T(8,128)(4,1)S(1)} %iota_compare_fusion, bf16[512,128]{1,0:T(8,128)(2,1)S(1)} %copy-done, bf16[512,1024]{1,0:T(8,128)(2,1)} %param.6), kind=kOutput, calls=%fused_computation.4 | convolution fusion | flops 543158272 | bytes 9846784 | tf_op jit(solution)/shard_map/tkgd,skd->kgts/dot_general | solution.py:27
  25.5 1.7 %fusion = f32[8,512]{1,0:T(8,128)S(1)} fusion(f32[512,512,8]{1,0,2:T(8,128)S(1)} %get-tuple-element.20, f32[8,512]{1,0:T(8,128)S(1)} %get-tuple-element.19, pred[512,512]{0,1:T(8,128)(4,1)S(1)} %iota_compare_fusion), kind=kLoop, calls=%fused_computation.3 | loop fusion | flops 8384512 | bytes 8683520 | tf_op jit(solution)/shard_map/reduce_sum | solution.py:33
  27.2 3.3 %fusion.7 = bf16[8,512,128]{1,2,0:T(8,128)(2,1)} fusion(f32[8,512]{1,0:T(8,128)S(1)} %fusion, f32[8,512]{1,0:T(8,128)S(1)} %get-tuple-element.19, f32[512,512,8]{1,0,2:T(8,128)S(1)} %get-tuple-element.20, pred[512,512]{0,1:T(8,128)(4,1)S(1)} %iota_compare_fusion, bf16[512,128]{1,0:T(8,128)(2,1)S(1)} %copy-done.3), kind=kOutput, calls=%fused_computation.13 | convolution fusion | flops 547880960 | bytes 9863168 | tf_op jit(solution)/shard_map/kgts,skd->tkgd/dot_general | solution.py:34
  30.6 1.5 %copy.48 = bf16[512,1024]{1,0:T(8,128)(2,1)S(1)} copy(bf16[512,1024]{0,1:T(8,128)(2,1)} %bitcast.123) | data formatting | bytes 2097152 | tf_op jit(solution)/shard_map/reshape | solution.py:37
  32.1 0.1 fusion.19
  32.2 2.4 %collective-permute-start = (bf16[512,1024]{1,0:T(8,128)(2,1)S(1)}, bf16[512,1024]{1,0:T(8,128)(2,1)S(1)}, u32[]{:S(2)}, u32[]{:S(2)}) collective-permute-start(bf16[512,1024]{1,0:T(8,128)(2,1)S(1)} %get-tuple-element.16), channel_id=1, source_target_pairs={{0,8},{8,0},{1,9},{9,1},{2,10},{10,2},{3,11},{11,3},{4,12},{12,4},... | collective-permute-start | bytes 3145736 | tf_op jit(solution)/shard_map/ppermute | solution.py:78
  34.6 2.3 %collective-permute-done = bf16[512,1024]{1,0:T(8,128)(2,1)S(1)} collective-permute-done((bf16[512,1024]{1,0:T(8,128)(2,1)S(1)}, bf16[512,1024]{1,0:T(8,128)(2,1)S(1)}, u32[]{:S(2)}, u32[]{:S(2)}) %collective-permute-start) | collective-permute-done | bytes 1048608 | tf_op jit(solution)/shard_map/ppermute | solution.py:78
  36.9 1.0 copy-done.2
  37.9 0.5 multiply_reduce_fusion
  38.4 17.2 %all-to-all-done = bf16[64,8,1024]{2,1,0:T(8,128)(2,1)S(1)} async-done(((bf16[64,8,1024]{2,1,0:T(8,128)(2,1)}), bf16[64,8,1024]{2,1,0:T(8,128)(2,1)S(1)}, u32[]{:S(2)}, u32[]{:S(2)}) %all-to-all-start) | async-done | bytes 1048608 | tf_op jit(solution)/shard_map/all_to_all | solution.py:85
  55.6 1.7 %convolution_bitcast_fusion.1 = f32[1,8,64,512]{3,2,1,0:T(8,128)} fusion(bf16[8,64,1024]{2,1,0:T(8,128)(2,1)S(1)} %bitcast.114, bf16[512,1024]{1,0:T(8,128)(2,1)S(1)} %copy-done.1, bf16[512,1024]{1,0:T(8,128)(2,1)S(1)} %copy.48, pred[]{:T(512)S(6)} %eq.8), kind=kOutput, calls=%fused_computation.15 | convolution fusion | flops 537395200 | bytes 4194305 | tf_op jit(solution)/shard_map/dot_general | solution.py:45
  57.3 0.3 multiply_reduce_fusion.1
  57.7 2.0 %convolution_bitcast_fusion = f32[1,8,64,512]{3,2,1,0:T(8,128)S(1)} fusion(bf16[8,64,1024]{2,1,0:T(8,128)(2,1)S(1)} %bitcast.115, bf16[512,1024]{1,0:T(8,128)(2,1)} %copy-done.2), kind=kOutput, calls=%fused_computation.14 | convolution fusion | flops 536870912 | bytes 3145728 | tf_op jit(solution)/shard_map/dot_general | solution.py:45
  59.6 1.5 %fusion.6 = f32[8,2,64,512]{3,2,0,1:T(8,128)S(1)} fusion(f32[1,8,64,512]{3,2,1,0:T(8,128)S(1)} %convolution_bitcast_fusion, f32[1,8,64,512]{3,2,1,0:T(8,128)} %convolution_bitcast_fusion.1, f32[2,512]{1,0:T(2,128)S(1)} %multiply_reduce_fusion, f32[8,64]{1,0:T(8,128)S(1)} %add.63), kind=kLoop, calls=%fused_computation.11 | loop fusion | flops 2097152 | bytes 4200448 | tf_op jit(solution)/shard_map/transpose | solution.py:121
  61.2 1.6 %copy.50 = f32[8,2,64,512]{3,2,1,0:T(8,128)} copy(f32[8,2,64,512]{3,2,0,1:T(8,128)S(1)} %fusion.6) | data formatting | bytes 4194304 | tf_op jit(solution)/shard_map/transpose | solution.py:121
  62.7 4.0 %all-to-all-start.1 = ((f32[8,2,64,512]{3,2,1,0:T(8,128)}), f32[8,2,64,512]{3,2,1,0:T(8,128)S(1)}, u32[]{:S(2)}, u32[]{:S(2)}) async-start(f32[8,2,64,512]{3,2,1,0:T(8,128)} %copy.50), calls=%async_computation.1 | async-start | bytes 4194304 | tf_op jit(solution)/shard_map/all_to_all | solution.py:125
  66.8 0.1 dynamic-slice_multiply_fusion
  66.9 26.0 %all-to-all-done.1 = f32[8,2,64,512]{3,2,1,0:T(8,128)S(1)} async-done(((f32[8,2,64,512]{3,2,1,0:T(8,128)}), f32[8,2,64,512]{3,2,1,0:T(8,128)S(1)}, u32[]{:S(2)}, u32[]{:S(2)}) %all-to-all-start.1) | async-done | bytes 2097184 | tf_op jit(solution)/shard_map/all_to_all | solution.py:125
  92.9 0.2 reduce_sum.159
  93.1 0.1 exponential_convert_fusion
  93.3 3.7 %collective-permute-start.1 = (bf16[64,512]{1,0:T(8,128)(2,1)S(1)}, bf16[64,512]{1,0:T(8,128)(2,1)S(1)}, u32[]{:S(2)}, u32[]{:S(2)}) collective-permute-start(bf16[64,512]{1,0:T(8,128)(2,1)S(1)} %slice_bitcast_fusion), channel_id=1, source_target_pairs={{0,8},{8,0},{1,9},{9,1},{2,10},{10,2},{3,11},{11,3},{4,12},{12,4},... | collective-permute-start | bytes 196616 | tf_op jit(solution)/shard_map/ppermute | solution.py:78
  97.0 0.9 collective-permute-done.1
  97.9 0.8 broadcast_in_dim.29
  98.7 3.7 %all-to-all-start.2 = ((bf16[8,64,512]{2,1,0:T(8,128)(2,1)}), bf16[8,64,512]{2,1,0:T(8,128)(2,1)S(1)}, u32[]{:S(2)}, u32[]{:S(2)}) async-start(bf16[8,64,512]{2,1,0:T(8,128)(2,1)} %broadcast_in_dim.29), calls=%async_computation.2 | async-start | bytes 1048576 | tf_op jit(solution)/shard_map/all_to_all | solution.py:93
  102.4 0.1 convert_reduce_fusion.1
  102.5 0.2 fusion.23
  102.7 9.0 %all-to-all-done.2 = bf16[8,64,512]{2,1,0:T(8,128)(2,1)S(1)} async-done(((bf16[8,64,512]{2,1,0:T(8,128)(2,1)}), bf16[8,64,512]{2,1,0:T(8,128)(2,1)S(1)}, u32[]{:S(2)}, u32[]{:S(2)}) %all-to-all-start.2) | async-done | bytes 524320 | tf_op jit(solution)/shard_map/all_to_all | solution.py:93
  111.7 0.1 convert_reduce_fusion
  111.9 0.3 multiply_reduce_fusion.2
  112.4 0.2 broadcast_subtract_fusion
  112.6 2.1 %convolution_bitcast_fusion.2 = f32[64,64,8]{0,1,2:T(8,128)S(1)} fusion(f32[64,8,512]{2,1,0:T(8,128)S(1)} %broadcast_subtract_fusion, bf16[64,512]{1,0:T(8,128)(2,1)S(1)} %get-tuple-element.14, f32[64]{0:T(128)S(1)} %broadcast_multiply_fusion.3), kind=kOutput, calls=%fused_computation.16 | convolution fusion | flops 201392128 | bytes 1245440 | tf_op jit(solution)/shard_map/dot_general | solution.py:142
  114.7 0.2 bitcast_dynamic-update-slice_fusion
  115.0 0.2 copy.55
  115.2 22.3 %all_to_all.27 = f32[64,1,656]{2,1,0:T(1,128)S(1)} all-to-all(f32[64,1,656]{2,1,0:T(1,128)S(1)} %copy.55), channel_id=1, replica_groups=mesh['z'=8,'y_hi'=4,'core'=2,'x'=4,'y_lo'=2] {'z','y_hi','core'}, dimensions={0} | all-to-all | bytes 335872 | tf_op jit(solution)/shard_map/all_to_all | solution.py:164
  137.5 0.1 slice_reduce_fusion.2
  137.6 0.1 slice_reduce_fusion.1
  137.8 0.1 reduce_sum.165
  137.9 0.1 multiply_reduce_fusion.3
  138.1 0.7 rsqrt_multiply_fusion
  (36 shorter events, 0.8 us)
Async XLA Ops:
  0.0 2.3 %copy-start = (bf16[512,128]{1,0:T(8,128)(2,1)S(1)}, bf16[512,128]{1,0:T(8,128)(2,1)}, u32[]{:S(2)}) copy-start(bf16[512,128]{1,0:T(8,128)(2,1)} %param.7) | copy-start | bytes 393220
  5.0 50.6 %all-to-all-start = ((bf16[64,8,1024]{2,1,0:T(8,128)(2,1)}), bf16[64,8,1024]{2,1,0:T(8,128)(2,1)S(1)}, u32[]{:S(2)}, u32[]{:S(2)}) async-start(bf16[64,8,1024]{2,1,0:T(8,128)(2,1)} %bitcast.12), calls=%async_computation | async-start | bytes 2097152 | tf_op jit(solution)/shard_map/all_to_all | solution.py:85
  22.8 4.5 %copy-start.3 = (bf16[512,128]{1,0:T(8,128)(2,1)S(1)}, bf16[512,128]{1,0:T(8,128)(2,1)}, u32[]{:S(2)}) copy-start(bf16[512,128]{1,0:T(8,128)(2,1)} %param.8) | copy-start | bytes 393220
  27.2 4.8 %copy-start.1 = (bf16[512,1024]{1,0:T(8,128)(2,1)S(1)}, bf16[512,1024]{1,0:T(8,128)(2,1)}, u32[]{:S(2)}) copy-start(bf16[512,1024]{1,0:T(8,128)(2,1)} %param.6) | copy-start | bytes 3145732
  32.2 4.6 %collective-permute-start = (bf16[512,1024]{1,0:T(8,128)(2,1)S(1)}, bf16[512,1024]{1,0:T(8,128)(2,1)S(1)}, u32[]{:S(2)}, u32[]{:S(2)}) collective-permute-start(bf16[512,1024]{1,0:T(8,128)(2,1)S(1)} %get-tuple-element.16), channel_id=1, source_target_pairs={{0,8},{8,0},{1,9},{9,1},{2,10},{10,2},{3,11},{11,3},{4,12},{12,4},... | collective-permute-start | bytes 3145736 | tf_op jit(solution)/shard_map/ppermute | solution.py:78
  36.9 1.0 copy-start.2
  57.3 9.4 %copy-start.4 = (f32[512]{0:T(512)S(1)}, f32[512]{0:T(512)}, u32[]{:S(2)}) copy-start(f32[512]{0:T(512)} %param.10) | copy-start | bytes 6148
  57.3 9.4 %copy-start.5 = (f32[512]{0:T(512)S(1)}, f32[512]{0:T(512)}, u32[]{:S(2)}) copy-start(f32[512]{0:T(512)} %param.11) | copy-start | bytes 6148
  62.7 30.2 %all-to-all-start.1 = ((f32[8,2,64,512]{3,2,1,0:T(8,128)}), f32[8,2,64,512]{3,2,1,0:T(8,128)S(1)}, u32[]{:S(2)}, u32[]{:S(2)}) async-start(f32[8,2,64,512]{3,2,1,0:T(8,128)} %copy.50), calls=%async_computation.1 | async-start | bytes 4194304 | tf_op jit(solution)/shard_map/all_to_all | solution.py:125
  93.3 4.6 %collective-permute-start.1 = (bf16[64,512]{1,0:T(8,128)(2,1)S(1)}, bf16[64,512]{1,0:T(8,128)(2,1)S(1)}, u32[]{:S(2)}, u32[]{:S(2)}) collective-permute-start(bf16[64,512]{1,0:T(8,128)(2,1)S(1)} %slice_bitcast_fusion), channel_id=1, source_target_pairs={{0,8},{8,0},{1,9},{9,1},{2,10},{10,2},{3,11},{11,3},{4,12},{12,4},... | collective-permute-start | bytes 196616 | tf_op jit(solution)/shard_map/ppermute | solution.py:78
  98.7 13.0 %all-to-all-start.2 = ((bf16[8,64,512]{2,1,0:T(8,128)(2,1)}), bf16[8,64,512]{2,1,0:T(8,128)(2,1)S(1)}, u32[]{:S(2)}, u32[]{:S(2)}) async-start(bf16[8,64,512]{2,1,0:T(8,128)(2,1)} %broadcast_in_dim.29), calls=%async_computation.2 | async-start | bytes 1048576 | tf_op jit(solution)/shard_map/all_to_all | solution.py:93

commit v9 on v8

--- a/solution.py
+++ b/solution.py
@@ -103,7 +103,7 @@
     column_share = landmarks // data_count
     token_count = length * data_count
 
-    own_rows = landmark_index % length
+    own_rows = lax.rem(landmark_index, length)
     first = lax.axis_index(CORE) == 0
     marks = gather_marks(
         pick_rows(queries, own_rows),
@@ -114,16 +114,15 @@
     other_side = swap_cores(jnp.where(first, attended, queries))
     tokens = jnp.stack([own_side, other_side])
 
-    row_norms = squares_by_row(tokens)
-    mark_norms = squares_by_row(marks)
-    cross = jnp.stack([inner_rows(marks, tokens[0]), inner_rows(marks, tokens[1])])
-    distance_part = mark_norms[None, :, None] + row_norms[:, None, :] - 2.0 * cross
-    distance_part = jnp.transpose(
-        distance_part.reshape(2, model_count, row_share, length), (1, 0, 2, 3)
-    )
+    tokens = tokens.reshape(2 * length, queries.shape[1])
+    cross = inner_rows(marks, tokens)
+    distance_part = (
+        squares_by_row(marks)[:, None] + squares_by_row(tokens)[None, :] - 2.0 * cross
+    ).reshape(model_count, row_share, 2, length)
     distance = jnp.sum(
         lax.all_to_all(distance_part, MODEL, 0, 0, tiled=True), axis=0
     )
+    distance = jnp.transpose(distance, (1, 0, 2))
 
     radius = jnp.where(first, radius_in, radius_out)
     widths = lax.dynamic_slice_in_dim(radius, model_index * row_share, row_share, 0)
@@ -143,7 +142,7 @@
         rows_centered,
         columns_centered,
         (((1,), (1,)), ((), ())),
-        precision=lax.Precision.HIGHEST,
+        precision=lax.Precision.HIGH,
         preferred_element_type=jnp.float32,
     )
     row_square = jnp.sum(jnp.square(rows_centered), axis=1)

time: 139 us -> 139 us (level)
  matrix products: 14.7 us -> 11.8 us
  waiting for transfers between devices: 55.4 us -> 57.3 us
  local copies, waits for them, and re-layouts: 7.06 us -> 8.48 us
    reshape x0 -> x1, local copies, waits for them, and re-layouts: none -> 4.02 us  [shards(): distance_part = (squares_by_row(marks)[:, None] + squares_by_row(tokens)[...]
    all_to_all x1, waiting for transfers between devices: 17.2 us -> 19.1 us  [gather_marks(): lax.all_to_all(spread.reshape((data_count,) + query_marks.shape), DATA, 0...]
    transpose x1 -> x0, local copies, waits for them, and re-layouts: 1.58 us -> none  [shards(): jnp.transpose(distance_part.reshape(2, model_count, row_share, length), (...]
    transpose x1 -> x0, other arithmetic: 1.51 us -> none  [shards(): jnp.transpose(distance_part.reshape(2, model_count, row_share, length), (...]
    dot_general x2 -> x1, matrix products: 3.71 us -> 2.64 us  [inner_rows(): lax.dot_general(left, right, (((1,), (1,)), ((), ())), preferred_element_...]
where the time goes in v9:
time: 139 us
  waiting for transfers between devices  57.3 us (41%)
  starting transfers between devices  31.3 us (23%)
  blocking collectives  22.2 us (16%)
  matrix products  11.8 us (8%)
  local copies, waits for them, and re-layouts  8.48 us (6%)
  other arithmetic  7.21 us (5%)
    all_to_all x1, waiting for transfers between devices, shards(): lax.all_to_all(distance_part, MODEL, 0, 0, tiled=True)  26.1 us
    all_to_all x1, blocking collectives, shards(): received = lax.all_to_all(packed, DATA, 0, 0, tiled=True)  22.2 us
    all_to_all x1, waiting for transfers between devices, gather_marks(): lax.all_to_all(spread.reshape((data_count,) + query_marks.shape), DATA, 0...  19.1 us
    all_to_all x1, starting transfers between devices, gather_marks(): lax.all_to_all(spread.reshape((data_count,) + query_marks.shape), DATA, 0...  17.6 us
    all_to_all x1, waiting for transfers between devices, broadcast_gather(): return lax.all_to_all(spread, axis_name, 0, 0, tiled=True)  9 us
    ppermute x2, starting transfers between devices, swap_cores(): return lax.ppermute(piece, CORE, [(0, 1), (1, 0)])  6.03 us
    reshape x1, local copies, waits for them, and re-layouts, shards(): distance_part = (squares_by_row(marks)[:, None] + squares_by_row(tokens)[...  4.02 us
    all_to_all x1, starting transfers between devices, shards(): lax.all_to_all(distance_part, MODEL, 0, 0, tiled=True)  4 us
  transfers between devices with their start and end apart: 5, of which 5 were waited for; matrix products, arithmetic and copies ran while one was open for 7% of the time, Pallas kernels for 0%

profile of v9, /device:TPU:1, one launch (start us, length us, event | category | flops | bytes accessed | tf_op | source)
XLA Modules:
  0.0 138.6 jit_solution(5497003893763757778)
XLA Ops:
  0.0 0.8 compare_select_fusion
  0.8 0.1 iota_compare_fusion.1
  0.8 1.5 %convolution_convert_fusion.1 = bf16[8,1024]{1,0:T(8,128)(2,1)S(1)} fusion(bf16[512,1024]{1,0:T(8,128)(2,1)} %param.6, s32[8]{0:T(128)S(1)} %compare_select_fusion), kind=kOutput, calls=%fused_computation.18 | convolution fusion | flops 8400896 | bytes 1064992 | tf_op jit(solution)/shard_map/dot_general | solution.py:72
  2.3 0.3 fusion.37
  2.6 0.2 fusion.28
  2.8 0.1 fusion.31
  2.9 1.1 fusion.10
  4.0 1.1 broadcast_in_dim.26
  5.1 17.6 %all-to-all-start = ((bf16[64,8,1024]{2,1,0:T(8,128)(2,1)}), bf16[64,8,1024]{2,1,0:T(8,128)(2,1)S(1)}, u32[]{:S(2)}, u32[]{:S(2)}) async-start(bf16[64,8,1024]{2,1,0:T(8,128)(2,1)} %bitcast.12), calls=%async_computation | async-start | bytes 2097152 | tf_op jit(solution)/shard_map/all_to_all | solution.py:85
  22.7 0.1 iota_compare_fusion
  22.8 1.7 %fusion.1 = (f32[8,512]{1,0:T(8,128)S(1)}, f32[512,512,8]{1,0,2:T(8,128)S(1)}) fusion(pred[512,512]{0,1:T(8,128)(4,1)S(1)} %iota_compare_fusion, bf16[512,128]{1,0:T(8,128)(2,1)S(1)} %copy-done, bf16[512,1024]{1,0:T(8,128)(2,1)S(1)} %copy-done.1), kind=kOutput, calls=%fused_computation.4 | convolution fusion | flops 543158272 | bytes 9846784 | tf_op jit(solution)/shard_map/tkgd,skd->kgts/dot_general | solution.py:27
  24.5 1.7 %fusion = f32[8,512]{1,0:T(8,128)S(1)} fusion(f32[512,512,8]{1,0,2:T(8,128)S(1)} %get-tuple-element.18, f32[8,512]{1,0:T(8,128)S(1)} %get-tuple-element.17, pred[512,512]{0,1:T(8,128)(4,1)S(1)} %iota_compare_fusion), kind=kLoop, calls=%fused_computation.3 | loop fusion | flops 8384512 | bytes 8683520 | tf_op jit(solution)/shard_map/reduce_sum | solution.py:33
  26.3 3.3 %fusion.5 = bf16[8,512,128]{1,2,0:T(8,128)(2,1)} fusion(f32[8,512]{1,0:T(8,128)S(1)} %fusion, f32[8,512]{1,0:T(8,128)S(1)} %get-tuple-element.17, f32[512,512,8]{1,0,2:T(8,128)S(1)} %get-tuple-element.18, pred[512,512]{0,1:T(8,128)(4,1)S(1)} %iota_compare_fusion, bf16[512,128]{1,0:T(8,128)(2,1)S(1)} %copy-done.2), kind=kOutput, calls=%fused_computation.12 | convolution fusion | flops 547880960 | bytes 9863168 | tf_op jit(solution)/shard_map/kgts,skd->tkgd/dot_general | solution.py:34
  29.6 1.5 %copy.87 = bf16[512,1024]{1,0:T(8,128)(2,1)S(1)} copy(bf16[512,1024]{0,1:T(8,128)(2,1)} %bitcast.117) | data formatting | bytes 2097152 | tf_op jit(solution)/shard_map/reshape | solution.py:37
  31.1 0.1 select_bitcast_fusion
  31.3 2.4 %collective-permute-start = (bf16[512,1024]{1,0:T(8,128)(2,1)S(1)}, bf16[512,1024]{1,0:T(8,128)(2,1)S(1)}, u32[]{:S(2)}, u32[]{:S(2)}) collective-permute-start(bf16[512,1024]{1,0:T(8,128)(2,1)S(1)} %get-tuple-element.16), channel_id=1, source_target_pairs={{0,8},{8,0},{1,9},{9,1},{2,10},{10,2},{3,11},{11,3},{4,12},{12,4},... | collective-permute-start | bytes 3145736 | tf_op jit(solution)/shard_map/ppermute | solution.py:78
  33.6 2.3 %collective-permute-done = bf16[512,1024]{1,0:T(8,128)(2,1)S(1)} collective-permute-done((bf16[512,1024]{1,0:T(8,128)(2,1)S(1)}, bf16[512,1024]{1,0:T(8,128)(2,1)S(1)}, u32[]{:S(2)}, u32[]{:S(2)}) %collective-permute-start) | collective-permute-done | bytes 1048608 | tf_op jit(solution)/shard_map/ppermute | solution.py:78
  35.9 0.5 multiply_reduce_fusion
  36.4 0.2 pad_maximum_fusion
  36.6 19.1 %all-to-all-done = bf16[64,8,1024]{2,1,0:T(8,128)(2,1)S(1)} async-done(((bf16[64,8,1024]{2,1,0:T(8,128)(2,1)}), bf16[64,8,1024]{2,1,0:T(8,128)(2,1)S(1)}, u32[]{:S(2)}, u32[]{:S(2)}) %all-to-all-start) | async-done | bytes 1048608 | tf_op jit(solution)/shard_map/all_to_all | solution.py:85
  55.6 0.3 multiply_reduce_fusion.1
  55.9 0.1 add.57
  56.0 2.6 %multiply_subtract_fusion = f32[512,1024]{1,0:T(8,128)} fusion(bf16[1024,1024]{1,0:T(8,128)(2,1)S(1)} %bitcast.110, bf16[64,8,1024]{2,1,0:T(8,128)(2,1)S(1)} %all-to-all-done, f32[1024]{0:T(1024)S(1)} %bitcast.121, f32[512]{0:T(512)S(1)} %add.57), kind=kOutput, calls=%fused_computation.10 | convolution fusion | flops 1075314688 | bytes 5249024 | tf_op jit(solution)/shard_map/dot_general | solution.py:45
  58.7 4.0 %reshape.163 = f32[8,64,2,512]{3,2,1,0:T(2,128)} reshape(f32[512,1024]{1,0:T(8,128)} %multiply_subtract_fusion) | data formatting | bytes 4194304 | tf_op jit(solution)/shard_map/reshape | solution.py:121
  62.7 4.0 %all-to-all-start.1 = ((f32[8,64,2,512]{3,2,1,0:T(2,128)}), f32[8,64,2,512]{3,2,1,0:T(2,128)S(1)}, u32[]{:S(2)}, u32[]{:S(2)}) async-start(f32[8,64,2,512]{3,2,1,0:T(2,128)} %reshape.163), calls=%async_computation.1 | async-start | bytes 4194304 | tf_op jit(solution)/shard_map/all_to_all | solution.py:123
  66.7 0.1 dynamic-slice_multiply_fusion
  66.8 26.1 %all-to-all-done.1 = f32[8,64,2,512]{3,2,1,0:T(2,128)S(1)} async-done(((f32[8,64,2,512]{3,2,1,0:T(2,128)}), f32[8,64,2,512]{3,2,1,0:T(2,128)S(1)}, u32[]{:S(2)}, u32[]{:S(2)}) %all-to-all-start.1) | async-done | bytes 2097184 | tf_op jit(solution)/shard_map/all_to_all | solution.py:123
  92.8 1.0 reduce_sum.159
  93.8 0.1 fusion.27
  93.9 3.7 %collective-permute-start.1 = (bf16[64,512]{1,0:T(8,128)(2,1)S(1)}, bf16[64,512]{1,0:T(8,128)(2,1)S(1)}, u32[]{:S(2)}, u32[]{:S(2)}) collective-permute-start(bf16[64,512]{1,0:T(8,128)(2,1)S(1)} %slice_bitcast_fusion), channel_id=1, source_target_pairs={{0,8},{8,0},{1,9},{9,1},{2,10},{10,2},{3,11},{11,3},{4,12},{12,4},... | collective-permute-start | bytes 196616 | tf_op jit(solution)/shard_map/ppermute | solution.py:78
  97.6 0.9 collective-permute-done.1
  98.5 0.8 broadcast_in_dim.29
  99.3 3.7 %all-to-all-start.2 = ((bf16[8,64,512]{2,1,0:T(8,128)(2,1)}), bf16[8,64,512]{2,1,0:T(8,128)(2,1)S(1)}, u32[]{:S(2)}, u32[]{:S(2)}) async-start(bf16[8,64,512]{2,1,0:T(8,128)(2,1)} %broadcast_in_dim.29), calls=%async_computation.2 | async-start | bytes 1048576 | tf_op jit(solution)/shard_map/all_to_all | solution.py:93
  103.0 0.1 convert_reduce_fusion.1
  103.2 0.2 fusion.22
  103.3 9.0 %all-to-all-done.2 = bf16[8,64,512]{2,1,0:T(8,128)(2,1)S(1)} async-done(((bf16[8,64,512]{2,1,0:T(8,128)(2,1)}), bf16[8,64,512]{2,1,0:T(8,128)(2,1)S(1)}, u32[]{:S(2)}, u32[]{:S(2)}) %all-to-all-start.2) | async-done | bytes 524320 | tf_op jit(solution)/shard_map/all_to_all | solution.py:93
  112.3 0.1 convert_reduce_fusion
  112.6 0.3 multiply_reduce_fusion.2
  113.1 0.2 broadcast_subtract_fusion
  113.2 1.3 convolution_bitcast_fusion
  114.6 0.2 bitcast_dynamic-update-slice_fusion
  114.9 0.2 copy.94
  115.1 22.2 %all_to_all.27 = f32[64,1,656]{2,1,0:T(1,128)S(1)} all-to-all(f32[64,1,656]{2,1,0:T(1,128)S(1)} %copy.94), channel_id=1, replica_groups=mesh['z'=8,'y_hi'=4,'core'=2,'x'=4,'y_lo'=2] {'z','y_hi','core'}, dimensions={0} | all-to-all | bytes 335872 | tf_op jit(solution)/shard_map/all_to_all | solution.py:163
  137.3 0.1 slice_reduce_fusion.2
  137.4 0.1 slice_reduce_fusion.1
  137.6 0.1 reduce_sum.165
  137.8 0.1 multiply_reduce_fusion.3
  137.9 0.7 rsqrt_multiply_fusion
  (34 shorter events, 0.6 us)
Async XLA Ops:
  0.0 2.3 %copy-start = (bf16[512,128]{1,0:T(8,128)(2,1)S(1)}, bf16[512,128]{1,0:T(8,128)(2,1)}, u32[]{:S(2)}) copy-start(bf16[512,128]{1,0:T(8,128)(2,1)} %param.7) | copy-start | bytes 393220
  0.0 22.8 %copy-start.1 = (bf16[512,1024]{1,0:T(8,128)(2,1)S(1)}, bf16[512,1024]{1,0:T(8,128)(2,1)}, u32[]{:S(2)}) copy-start(bf16[512,1024]{1,0:T(8,128)(2,1)} %param.6) | copy-start | bytes 3145732
  5.1 50.6 %all-to-all-start = ((bf16[64,8,1024]{2,1,0:T(8,128)(2,1)}), bf16[64,8,1024]{2,1,0:T(8,128)(2,1)S(1)}, u32[]{:S(2)}, u32[]{:S(2)}) async-start(bf16[64,8,1024]{2,1,0:T(8,128)(2,1)} %bitcast.12), calls=%async_computation | async-start | bytes 2097152 | tf_op jit(solution)/shard_map/all_to_all | solution.py:85
  24.5 1.8 %copy-start.2 = (bf16[512,128]{1,0:T(8,128)(2,1)S(1)}, bf16[512,128]{1,0:T(8,128)(2,1)}, u32[]{:S(2)}) copy-start(bf16[512,128]{1,0:T(8,128)(2,1)} %param.8) | copy-start | bytes 393220
  31.3 4.6 %collective-permute-start = (bf16[512,1024]{1,0:T(8,128)(2,1)S(1)}, bf16[512,1024]{1,0:T(8,128)(2,1)S(1)}, u32[]{:S(2)}, u32[]{:S(2)}) collective-permute-start(bf16[512,1024]{1,0:T(8,128)(2,1)S(1)} %get-tuple-element.16), channel_id=1, source_target_pairs={{0,8},{8,0},{1,9},{9,1},{2,10},{10,2},{3,11},{11,3},{4,12},{12,4},... | collective-permute-start | bytes 3145736 | tf_op jit(solution)/shard_map/ppermute | solution.py:78
  58.6 8.0 %copy-start.3 = (f32[512]{0:T(512)S(1)}, f32[512]{0:T(512)}, u32[]{:S(2)}) copy-start(f32[512]{0:T(512)} %param.10) | copy-start | bytes 6148
  58.6 8.0 %copy-start.4 = (f32[512]{0:T(512)S(1)}, f32[512]{0:T(512)}, u32[]{:S(2)}) copy-start(f32[512]{0:T(512)} %param.11) | copy-start | bytes 6148
  62.7 30.2 %all-to-all-start.1 = ((f32[8,64,2,512]{3,2,1,0:T(2,128)}), f32[8,64,2,512]{3,2,1,0:T(2,128)S(1)}, u32[]{:S(2)}, u32[]{:S(2)}) async-start(f32[8,64,2,512]{3,2,1,0:T(2,128)} %reshape.163), calls=%async_computation.1 | async-start | bytes 4194304 | tf_op jit(solution)/shard_map/all_to_all | solution.py:123
  93.9 4.6 %collective-permute-start.1 = (bf16[64,512]{1,0:T(8,128)(2,1)S(1)}, bf16[64,512]{1,0:T(8,128)(2,1)S(1)}, u32[]{:S(2)}, u32[]{:S(2)}) collective-permute-start(bf16[64,512]{1,0:T(8,128)(2,1)S(1)} %slice_bitcast_fusion), channel_id=1, source_target_pairs={{0,8},{8,0},{1,9},{9,1},{2,10},{10,2},{3,11},{11,3},{4,12},{12,4},... | collective-permute-start | bytes 196616 | tf_op jit(solution)/shard_map/ppermute | solution.py:78
  99.3 13.0 %all-to-all-start.2 = ((bf16[8,64,512]{2,1,0:T(8,128)(2,1)}), bf16[8,64,512]{2,1,0:T(8,128)(2,1)S(1)}, u32[]{:S(2)}, u32[]{:S(2)}) async-start(bf16[8,64,512]{2,1,0:T(8,128)(2,1)} %broadcast_in_dim.29), calls=%async_computation.2 | async-start | bytes 1048576 | tf_op jit(solution)/shard_map/all_to_all | solution.py:93

commit v10 on v9

--- a/solution.py
+++ b/solution.py
@@ -118,18 +118,17 @@
     cross = inner_rows(marks, tokens)
     distance_part = (
         squares_by_row(marks)[:, None] + squares_by_row(tokens)[None, :] - 2.0 * cross
-    ).reshape(model_count, row_share, 2, length)
+    ).reshape(model_count, row_share, 2 * length)
     distance = jnp.sum(
         lax.all_to_all(distance_part, MODEL, 0, 0, tiled=True), axis=0
     )
-    distance = jnp.transpose(distance, (1, 0, 2))
 
     radius = jnp.where(first, radius_in, radius_out)
     widths = lax.dynamic_slice_in_dim(radius, model_index * row_share, row_share, 0)
-    side = jnp.exp(-distance / (D * widths[None, :, None])).astype(jnp.bfloat16)
-    handed = swap_cores(side[1])
-    row_features = jnp.where(first, side[0], handed)
-    own_columns = jnp.where(first, handed, side[0])
+    side = jnp.exp(-distance / (D * widths[:, None])).astype(jnp.bfloat16)
+    handed = swap_cores(side[:, length:])
+    row_features = jnp.where(first, side[:, :length], handed)
+    own_columns = jnp.where(first, handed, side[:, :length])
     column_features = broadcast_gather(own_columns, MODEL).reshape(landmarks, length)
 
     rows32 = row_features.astype(jnp.float32)

time: 139 us -> 136 us (0.978)
  local copies, waits for them, and re-layouts: 8.48 us -> 4.45 us
  matrix products: 11.8 us -> 13.4 us
    reshape x1 -> x0, local copies, waits for them, and re-layouts: 4.02 us -> none  [shards(): distance_part = (squares_by_row(marks)[:, None] + squares_by_row(tokens)[...]
    dot_general x1, matrix products: 2.64 us -> 4.18 us  [inner_rows(): lax.dot_general(left, right, (((1,), (1,)), ((), ())), preferred_element_...]
  transfers between devices with their start and end apart: 5 -> 5, of which waited for: 5 -> 5; matrix products, arithmetic and copies ran while one was open for 7% -> 8% of each run, Pallas kernels for 0% -> 0%
where the time goes in v10:
time: 136 us; the launch traced here: 135 us
  waiting for transfers between devices  56.1 us (41%)
  starting transfers between devices  31.3 us (23%)
  blocking collectives  22.3 us (16%)
  matrix products  13.4 us (10%)
  other arithmetic  7.73 us (6%)
  local copies, waits for them, and re-layouts  4.45 us (3%)
    all_to_all x1, waiting for transfers between devices, shards(): lax.all_to_all(distance_part, MODEL, 0, 0, tiled=True)  26.1 us
    all_to_all x1, blocking collectives, shards(): received = lax.all_to_all(packed, DATA, 0, 0, tiled=True)  22.3 us
    all_to_all x1, waiting for transfers between devices, gather_marks(): lax.all_to_all(spread.reshape((data_count,) + query_marks.shape), DATA, 0...  17.7 us
    all_to_all x1, starting transfers between devices, gather_marks(): lax.all_to_all(spread.reshape((data_count,) + query_marks.shape), DATA, 0...  17.6 us
    all_to_all x1, waiting for transfers between devices, broadcast_gather(): return lax.all_to_all(spread, axis_name, 0, 0, tiled=True)  9.18 us
    ppermute x2, starting transfers between devices, swap_cores(): return lax.ppermute(piece, CORE, [(0, 1), (1, 0)])  6.04 us
    dot_general x1, matrix products, inner_rows(): lax.dot_general(left, right, (((1,), (1,)), ((), ())), preferred_element_...  4.18 us
    all_to_all x1, starting transfers between devices, shards(): lax.all_to_all(distance_part, MODEL, 0, 0, tiled=True)  4.17 us
  transfers between devices with their start and end apart: 5, of which 5 were waited for; matrix products, arithmetic and copies ran while one was open for 8% of the time, Pallas kernels for 0%

profile of v10, /device:TPU:1, one launch (start us, length us, event | category | flops | bytes accessed | tf_op | source)
XLA Modules:
  0.0 135.5 jit_solution(11022688485679655601)
XLA Ops:
  0.0 0.8 compare_select_fusion
  0.8 0.1 iota_compare_fusion.1
  0.8 1.5 %convolution_convert_fusion.1 = bf16[8,1024]{1,0:T(8,128)(2,1)S(1)} fusion(bf16[512,1024]{1,0:T(8,128)(2,1)} %param.6, s32[8]{0:T(128)S(1)} %compare_select_fusion), kind=kOutput, calls=%fused_computation.18 | convolution fusion | flops 8400896 | bytes 1064992 | tf_op jit(solution)/shard_map/dot_general | solution.py:72
  2.3 0.3 fusion.33
  2.6 0.2 fusion.24
  2.8 0.1 fusion.27
  2.9 1.1 fusion.10
  4.0 1.1 broadcast_in_dim.26
  5.1 17.6 %all-to-all-start = ((bf16[64,8,1024]{2,1,0:T(8,128)(2,1)}), bf16[64,8,1024]{2,1,0:T(8,128)(2,1)S(1)}, u32[]{:S(2)}, u32[]{:S(2)}) async-start(bf16[64,8,1024]{2,1,0:T(8,128)(2,1)} %bitcast.12), calls=%async_computation | async-start | bytes 2097152 | tf_op jit(solution)/shard_map/all_to_all | solution.py:85
  22.7 0.1 iota_compare_fusion
  22.8 1.7 %fusion.1 = (f32[8,512]{1,0:T(8,128)S(1)}, f32[512,512,8]{1,0,2:T(8,128)S(1)}) fusion(pred[512,512]{0,1:T(8,128)(4,1)S(1)} %iota_compare_fusion, bf16[512,128]{1,0:T(8,128)(2,1)S(1)} %copy-done, bf16[512,1024]{1,0:T(8,128)(2,1)S(1)} %copy-done.1), kind=kOutput, calls=%fused_computation.4 | convolution fusion | flops 543158272 | bytes 9846784 | tf_op jit(solution)/shard_map/tkgd,skd->kgts/dot_general | solution.py:27
  24.5 1.7 %fusion = f32[8,512]{1,0:T(8,128)S(1)} fusion(f32[512,512,8]{1,0,2:T(8,128)S(1)} %get-tuple-element.18, f32[8,512]{1,0:T(8,128)S(1)} %get-tuple-element.17, pred[512,512]{0,1:T(8,128)(4,1)S(1)} %iota_compare_fusion), kind=kLoop, calls=%fused_computation.3 | loop fusion | flops 8384512 | bytes 8683520 | tf_op jit(solution)/shard_map/reduce_sum | solution.py:33
  26.3 3.4 %fusion.5 = bf16[8,512,128]{1,2,0:T(8,128)(2,1)} fusion(f32[8,512]{1,0:T(8,128)S(1)} %fusion, f32[8,512]{1,0:T(8,128)S(1)} %get-tuple-element.17, f32[512,512,8]{1,0,2:T(8,128)S(1)} %get-tuple-element.18, pred[512,512]{0,1:T(8,128)(4,1)S(1)} %iota_compare_fusion, bf16[512,128]{1,0:T(8,128)(2,1)S(1)} %copy-done.2), kind=kOutput, calls=%fused_computation.12 | convolution fusion | flops 547880960 | bytes 9863168 | tf_op jit(solution)/shard_map/kgts,skd->tkgd/dot_general | solution.py:34
  29.6 1.5 %copy.47 = bf16[512,1024]{1,0:T(8,128)(2,1)S(1)} copy(bf16[512,1024]{0,1:T(8,128)(2,1)} %bitcast.108) | data formatting | bytes 2097152 | tf_op jit(solution)/shard_map/reshape | solution.py:37
  31.1 0.1 select_bitcast_fusion
  31.3 2.4 %collective-permute-start = (bf16[512,1024]{1,0:T(8,128)(2,1)S(1)}, bf16[512,1024]{1,0:T(8,128)(2,1)S(1)}, u32[]{:S(2)}, u32[]{:S(2)}) collective-permute-start(bf16[512,1024]{1,0:T(8,128)(2,1)S(1)} %get-tuple-element.16), channel_id=1, source_target_pairs={{0,8},{8,0},{1,9},{9,1},{2,10},{10,2},{3,11},{11,3},{4,12},{12,4},... | collective-permute-start | bytes 3145736 | tf_op jit(solution)/shard_map/ppermute | solution.py:78
  33.6 2.3 %collective-permute-done = bf16[512,1024]{1,0:T(8,128)(2,1)S(1)} collective-permute-done((bf16[512,1024]{1,0:T(8,128)(2,1)S(1)}, bf16[512,1024]{1,0:T(8,128)(2,1)S(1)}, u32[]{:S(2)}, u32[]{:S(2)}) %collective-permute-start) | collective-permute-done | bytes 1048608 | tf_op jit(solution)/shard_map/ppermute | solution.py:78
  35.9 0.5 multiply_reduce_fusion
  36.4 1.5 %pad_maximum_fusion = bf16[2,512,1024]{2,1,0:T(8,128)(2,1)} fusion(bf16[1,512,1024]{2,1,0:T(8,128)(2,1)S(1)} %bitcast.99, bf16[1,512,1024]{2,1,0:T(8,128)(2,1)S(1)} %get-tuple-element.15), kind=kLoop, calls=%fused_computation.9 | loop fusion | flops 1048576 | bytes 4194304 | tf_op jit(solution)/shard_map/stack | solution.py:115
  37.9 17.7 %all-to-all-done = bf16[64,8,1024]{2,1,0:T(8,128)(2,1)S(1)} async-done(((bf16[64,8,1024]{2,1,0:T(8,128)(2,1)}), bf16[64,8,1024]{2,1,0:T(8,128)(2,1)S(1)}, u32[]{:S(2)}, u32[]{:S(2)}) %all-to-all-start) | async-done | bytes 1048608 | tf_op jit(solution)/shard_map/all_to_all | solution.py:85
  55.6 0.3 multiply_reduce_fusion.1
  55.9 0.1 add.57
  56.0 4.2 %multiply_subtract_fusion = f32[512,1024]{1,0:T(8,128)} fusion(bf16[1024,1024]{1,0:T(8,128)(2,1)} %bitcast.101, bf16[64,8,1024]{2,1,0:T(8,128)(2,1)S(1)} %all-to-all-done, f32[1024]{0:T(1024)S(1)} %bitcast.112, f32[512]{0:T(512)S(1)} %add.57), kind=kOutput, calls=%fused_computation.10 | convolution fusion | flops 1075314688 | bytes 5249024 | tf_op jit(solution)/shard_map/dot_general | solution.py:45
  60.2 4.2 %all-to-all-start.1 = ((f32[8,64,1024]{2,1,0:T(8,128)}), f32[8,64,1024]{2,1,0:T(8,128)S(1)}, u32[]{:S(2)}, u32[]{:S(2)}) async-start(f32[8,64,1024]{2,1,0:T(8,128)} %bitcast.100), calls=%async_computation.1 | async-start | bytes 4194304 | tf_op jit(solution)/shard_map/all_to_all | solution.py:123
  64.4 0.1 dynamic-slice_multiply_fusion
  64.4 26.1 %all-to-all-done.1 = f32[8,64,1024]{2,1,0:T(8,128)S(1)} async-done(((f32[8,64,1024]{2,1,0:T(8,128)}), f32[8,64,1024]{2,1,0:T(8,128)S(1)}, u32[]{:S(2)}, u32[]{:S(2)}) %all-to-all-start.1) | async-done | bytes 2097184 | tf_op jit(solution)/shard_map/all_to_all | solution.py:123
  90.5 0.1 reduce_sum.159
  90.6 0.1 exponential_convert_fusion
  90.8 3.7 %collective-permute-start.1 = (bf16[64,512]{1,0:T(8,128)(2,1)S(1)}, bf16[64,512]{1,0:T(8,128)(2,1)S(1)}, u32[]{:S(2)}, u32[]{:S(2)}) collective-permute-start(bf16[64,512]{1,0:T(8,128)(2,1)S(1)} %slice.30), channel_id=1, source_target_pairs={{0,8},{8,0},{1,9},{9,1},{2,10},{10,2},{3,11},{11,3},{4,12},{12,4},... | collective-permute-start | bytes 196616 | tf_op jit(solution)/shard_map/ppermute | solution.py:78
  94.5 0.9 collective-permute-done.1
  95.4 0.8 broadcast_in_dim.29
  96.2 3.5 %all-to-all-start.2 = ((bf16[8,64,512]{2,1,0:T(8,128)(2,1)}), bf16[8,64,512]{2,1,0:T(8,128)(2,1)S(1)}, u32[]{:S(2)}, u32[]{:S(2)}) async-start(bf16[8,64,512]{2,1,0:T(8,128)(2,1)} %broadcast_in_dim.29), calls=%async_computation.2 | async-start | bytes 1048576 | tf_op jit(solution)/shard_map/all_to_all | solution.py:93
  99.7 0.1 convert_reduce_fusion.1
  99.8 0.2 fusion.19
  100.0 9.2 %all-to-all-done.2 = bf16[8,64,512]{2,1,0:T(8,128)(2,1)S(1)} async-done(((bf16[8,64,512]{2,1,0:T(8,128)(2,1)}), bf16[8,64,512]{2,1,0:T(8,128)(2,1)S(1)}, u32[]{:S(2)}, u32[]{:S(2)}) %all-to-all-start.2) | async-done | bytes 524320 | tf_op jit(solution)/shard_map/all_to_all | solution.py:93
  109.2 0.1 convert_reduce_fusion
  109.4 0.3 multiply_reduce_fusion.2
  109.7 0.1 reshape.165
  109.9 0.2 broadcast_subtract_fusion
  110.1 1.3 convolution_bitcast_fusion
  111.4 0.2 bitcast_dynamic-update-slice_fusion
  111.7 0.2 copy.53
  111.9 22.3 %all_to_all.27 = f32[64,1,656]{2,1,0:T(1,128)S(1)} all-to-all(f32[64,1,656]{2,1,0:T(1,128)S(1)} %copy.53), channel_id=1, replica_groups=mesh['z'=8,'y_hi'=4,'core'=2,'x'=4,'y_lo'=2] {'z','y_hi','core'}, dimensions={0} | all-to-all | bytes 335872 | tf_op jit(solution)/shard_map/all_to_all | solution.py:162
  134.2 0.1 slice_reduce_fusion.2
  134.3 0.1 slice_reduce_fusion.1
  134.5 0.1 reduce_sum.165
  134.7 0.1 multiply_reduce_fusion.3
  134.8 0.7 rsqrt_multiply_fusion
  (33 shorter events, 0.6 us)
Async XLA Ops:
  0.0 2.3 %copy-start = (bf16[512,128]{1,0:T(8,128)(2,1)S(1)}, bf16[512,128]{1,0:T(8,128)(2,1)}, u32[]{:S(2)}) copy-start(bf16[512,128]{1,0:T(8,128)(2,1)} %param.7) | copy-start | bytes 393220
  0.0 22.8 %copy-start.1 = (bf16[512,1024]{1,0:T(8,128)(2,1)S(1)}, bf16[512,1024]{1,0:T(8,128)(2,1)}, u32[]{:S(2)}) copy-start(bf16[512,1024]{1,0:T(8,128)(2,1)} %param.6) | copy-start | bytes 3145732
  5.1 50.5 %all-to-all-start = ((bf16[64,8,1024]{2,1,0:T(8,128)(2,1)}), bf16[64,8,1024]{2,1,0:T(8,128)(2,1)S(1)}, u32[]{:S(2)}, u32[]{:S(2)}) async-start(bf16[64,8,1024]{2,1,0:T(8,128)(2,1)} %bitcast.12), calls=%async_computation | async-start | bytes 2097152 | tf_op jit(solution)/shard_map/all_to_all | solution.py:85
  24.5 1.7 %copy-start.2 = (bf16[512,128]{1,0:T(8,128)(2,1)S(1)}, bf16[512,128]{1,0:T(8,128)(2,1)}, u32[]{:S(2)}) copy-start(bf16[512,128]{1,0:T(8,128)(2,1)} %param.8) | copy-start | bytes 393220
  31.3 4.6 %collective-permute-start = (bf16[512,1024]{1,0:T(8,128)(2,1)S(1)}, bf16[512,1024]{1,0:T(8,128)(2,1)S(1)}, u32[]{:S(2)}, u32[]{:S(2)}) collective-permute-start(bf16[512,1024]{1,0:T(8,128)(2,1)S(1)} %get-tuple-element.16), channel_id=1, source_target_pairs={{0,8},{8,0},{1,9},{9,1},{2,10},{10,2},{3,11},{11,3},{4,12},{12,4},... | collective-permute-start | bytes 3145736 | tf_op jit(solution)/shard_map/ppermute | solution.py:78
  60.2 4.2 %copy-start.3 = (f32[512]{0:T(512)S(1)}, f32[512]{0:T(512)}, u32[]{:S(2)}) copy-start(f32[512]{0:T(512)} %param.10) | copy-start | bytes 6148
  60.2 4.2 %copy-start.4 = (f32[512]{0:T(512)S(1)}, f32[512]{0:T(512)}, u32[]{:S(2)}) copy-start(f32[512]{0:T(512)} %param.11) | copy-start | bytes 6148
  60.2 30.3 %all-to-all-start.1 = ((f32[8,64,1024]{2,1,0:T(8,128)}), f32[8,64,1024]{2,1,0:T(8,128)S(1)}, u32[]{:S(2)}, u32[]{:S(2)}) async-start(f32[8,64,1024]{2,1,0:T(8,128)} %bitcast.100), calls=%async_computation.1 | async-start | bytes 4194304 | tf_op jit(solution)/shard_map/all_to_all | solution.py:123
  90.8 4.6 %collective-permute-start.1 = (bf16[64,512]{1,0:T(8,128)(2,1)S(1)}, bf16[64,512]{1,0:T(8,128)(2,1)S(1)}, u32[]{:S(2)}, u32[]{:S(2)}) collective-permute-start(bf16[64,512]{1,0:T(8,128)(2,1)S(1)} %slice.30), channel_id=1, source_target_pairs={{0,8},{8,0},{1,9},{9,1},{2,10},{10,2},{3,11},{11,3},{4,12},{12,4},... | collective-permute-start | bytes 196616 | tf_op jit(solution)/shard_map/ppermute | solution.py:78
  96.2 13.0 %all-to-all-start.2 = ((bf16[8,64,512]{2,1,0:T(8,128)(2,1)}), bf16[8,64,512]{2,1,0:T(8,128)(2,1)S(1)}, u32[]{:S(2)}, u32[]{:S(2)}) async-start(bf16[8,64,512]{2,1,0:T(8,128)(2,1)} %broadcast_in_dim.29), calls=%async_computation.2 | async-start | bytes 1048576 | tf_op jit(solution)/shard_map/all_to_all | solution.py:93

commit v11 on v10

--- a/solution.py
+++ b/solution.py
@@ -15,6 +15,7 @@
 CORE = "core"
 DATA = CHIPS + (CORE,)
 MODEL = ("x", "y_lo")
+PAIR = (CORE,) + MODEL
 
 
 def attend(queries, key_rows, value_rows):
@@ -110,25 +111,29 @@
         attend_rows(queries, key_rows, value_rows, own_rows),
     ).reshape(landmarks, queries.shape[1])
     attended = attend(queries, key_rows, value_rows)
-    own_side = jnp.where(first, queries, attended)
-    other_side = swap_cores(jnp.where(first, attended, queries))
-    tokens = jnp.stack([own_side, other_side])
-
-    tokens = tokens.reshape(2 * length, queries.shape[1])
-    cross = inner_rows(marks, tokens)
-    distance_part = (
-        squares_by_row(marks)[:, None] + squares_by_row(tokens)[None, :] - 2.0 * cross
-    ).reshape(model_count, row_share, 2 * length)
-    distance = jnp.sum(
-        lax.all_to_all(distance_part, MODEL, 0, 0, tiled=True), axis=0
-    )
-
-    radius = jnp.where(first, radius_in, radius_out)
-    widths = lax.dynamic_slice_in_dim(radius, model_index * row_share, row_share, 0)
-    side = jnp.exp(-distance / (D * widths[:, None])).astype(jnp.bfloat16)
-    handed = swap_cores(side[:, length:])
-    row_features = jnp.where(first, side[:, :length], handed)
-    own_columns = jnp.where(first, handed, side[:, :length])
+    swapped = swap_cores(jnp.where(first, attended, queries))
+    tokens = [jnp.where(first, queries, swapped), jnp.where(first, swapped, attended)]
+
+    mark_norms = squares_by_row(marks)
+    distance_part = jnp.stack(
+        [
+            (
+                mark_norms[:, None]
+                + squares_by_row(rows)[None, :]
+                - 2.0 * inner_rows(marks, rows)
+            ).reshape(model_count, row_share, length)
+            for rows in tokens
+        ]
+    ).reshape(2 * model_count, row_share, length)
+    received = lax.all_to_all(distance_part, PAIR, 0, 0, tiled=True)
+    distance = jnp.sum(received.reshape(2, model_count, row_share, length), axis=1)
+
+    widths = lax.dynamic_slice_in_dim(
+        jnp.stack([radius_in, radius_out]), model_index * row_share, row_share, 1
+    )
+    features = jnp.exp(-distance / (D * widths[:, :, None])).astype(jnp.bfloat16)
+    row_features = features[0]
+    own_columns = features[1]
     column_features = broadcast_gather(own_columns, MODEL).reshape(landmarks, length)
 
     rows32 = row_features.astype(jnp.float32)

time: 136 us -> 133 us (0.978)
  starting transfers between devices: 31.3 us -> 28.9 us
  waiting for transfers between devices: 56.1 us -> 54.6 us
    ppermute x2 -> x1, starting transfers between devices: 6.04 us -> 2.36 us  [swap_cores(): return lax.ppermute(piece, CORE, [(0, 1), (1, 0)])]
    dot_general x1 -> x2, matrix products: 4.18 us -> 2.74 us  [inner_rows(): lax.dot_general(left, right, (((1,), (1,)), ((), ())), preferred_element_...]
    ppermute x2 -> x1, waiting for transfers between devices: 3.14 us -> 2.26 us  [swap_cores(): return lax.ppermute(piece, CORE, [(0, 1), (1, 0)])]
  transfers between devices with their start and end apart: 5 -> 4, of which waited for: 5 -> 4; matrix products, arithmetic and copies ran while one was open for 8% -> 8% of each run, Pallas kernels for 0% -> 0%
where the time goes in v11:
time: 133 us
  waiting for transfers between devices  54.6 us (41%)
  starting transfers between devices  28.9 us (22%)
  blocking collectives  22.5 us (17%)
  matrix products  12.9 us (10%)
  other arithmetic  8.02 us (6%)
  local copies, waits for them, and re-layouts  5.52 us (4%)
    all_to_all x1, waiting for transfers between devices, shards(): received = lax.all_to_all(distance_part, PAIR, 0, 0, tiled=True)  26.9 us
    all_to_all x1, blocking collectives, shards(): received = lax.all_to_all(packed, DATA, 0, 0, tiled=True)  22.5 us
    all_to_all x1, starting transfers between devices, gather_marks(): lax.all_to_all(spread.reshape((data_count,) + query_marks.shape), DATA, 0...  17.6 us
    all_to_all x1, waiting for transfers between devices, gather_marks(): lax.all_to_all(spread.reshape((data_count,) + query_marks.shape), DATA, 0...  16.8 us
    all_to_all x1, waiting for transfers between devices, broadcast_gather(): return lax.all_to_all(spread, axis_name, 0, 0, tiled=True)  8.66 us
    all_to_all x1, starting transfers between devices, shards(): received = lax.all_to_all(distance_part, PAIR, 0, 0, tiled=True)  4.9 us
    all_to_all x1, starting transfers between devices, broadcast_gather(): return lax.all_to_all(spread, axis_name, 0, 0, tiled=True)  3.97 us
    dot_general x1, matrix products, attend(): jnp.einsum('kgts,skd->tkgd', weights, value_three, preferred_element_type...  3.33 us
  transfers between devices with their start and end apart: 4, of which 4 were waited for; matrix products, arithmetic and copies ran while one was open for 8% of the time, Pallas kernels for 0%

profile of v11, /device:TPU:1, one launch (start us, length us, event | category | flops | bytes accessed | tf_op | source)
XLA Modules:
  0.0 132.8 jit_solution(3913128310135351144)
XLA Ops:
  0.0 0.7 compare_select_fusion
  0.7 0.1 iota_compare_fusion.1
  0.8 1.5 %convolution_convert_fusion.1 = bf16[8,1024]{1,0:T(8,128)(2,1)S(1)} fusion(bf16[512,1024]{1,0:T(8,128)(2,1)} %param.6, s32[8]{0:T(128)S(1)} %compare_select_fusion), kind=kOutput, calls=%fused_computation.23 | convolution fusion | flops 8400896 | bytes 1064992 | tf_op jit(solution)/shard_map/dot_general | solution.py:73
  2.3 0.3 fusion.42
  2.5 0.2 fusion.30
  2.7 0.1 fusion.33
  2.8 1.1 fusion.10
  3.9 1.1 broadcast_in_dim.28
  5.0 17.6 %all-to-all-start = ((bf16[64,8,1024]{2,1,0:T(8,128)(2,1)}), bf16[64,8,1024]{2,1,0:T(8,128)(2,1)S(1)}, u32[]{:S(2)}, u32[]{:S(2)}) async-start(bf16[64,8,1024]{2,1,0:T(8,128)(2,1)} %bitcast.12), calls=%async_computation | async-start | bytes 2097152 | tf_op jit(solution)/shard_map/all_to_all | solution.py:86
  22.7 0.1 iota_compare_fusion
  22.8 2.7 %fusion.1 = (f32[8,512]{1,0:T(8,128)S(1)}, f32[512,512,8]{1,0,2:T(8,128)S(1)}) fusion(pred[512,512]{0,1:T(8,128)(4,1)S(1)} %iota_compare_fusion, bf16[512,128]{1,0:T(8,128)(2,1)S(1)} %copy-done, bf16[512,1024]{1,0:T(8,128)(2,1)} %param.6), kind=kOutput, calls=%fused_computation.4 | convolution fusion | flops 543158272 | bytes 9846784 | tf_op jit(solution)/shard_map/tkgd,skd->kgts/dot_general | solution.py:28
  25.5 1.7 %fusion = f32[8,512]{1,0:T(8,128)S(1)} fusion(f32[512,512,8]{1,0,2:T(8,128)S(1)} %get-tuple-element.18, f32[8,512]{1,0:T(8,128)S(1)} %get-tuple-element.17, pred[512,512]{0,1:T(8,128)(4,1)S(1)} %iota_compare_fusion), kind=kLoop, calls=%fused_computation.3 | loop fusion | flops 8384512 | bytes 8683520 | tf_op jit(solution)/shard_map/reduce_sum | solution.py:34
  27.2 3.3 %fusion.5 = bf16[8,512,128]{1,2,0:T(8,128)(2,1)} fusion(f32[8,512]{1,0:T(8,128)S(1)} %fusion, f32[8,512]{1,0:T(8,128)S(1)} %get-tuple-element.17, f32[512,512,8]{1,0,2:T(8,128)S(1)} %get-tuple-element.18, pred[512,512]{0,1:T(8,128)(4,1)S(1)} %iota_compare_fusion, bf16[512,128]{1,0:T(8,128)(2,1)S(1)} %copy-done.3), kind=kOutput, calls=%fused_computation.13 | convolution fusion | flops 547880960 | bytes 9863168 | tf_op jit(solution)/shard_map/kgts,skd->tkgd/dot_general | solution.py:35
  30.6 1.5 %copy.46 = bf16[512,1024]{1,0:T(8,128)(2,1)S(1)} copy(bf16[512,1024]{0,1:T(8,128)(2,1)} %bitcast.120) | data formatting | bytes 2097152 | tf_op jit(solution)/shard_map/reshape | solution.py:38
  32.1 0.1 broadcast_select_fusion.2
  32.2 2.4 %collective-permute-start = (bf16[512,1024]{1,0:T(8,128)(2,1)S(1)}, bf16[512,1024]{1,0:T(8,128)(2,1)S(1)}, u32[]{:S(2)}, u32[]{:S(2)}) collective-permute-start(bf16[512,1024]{1,0:T(8,128)(2,1)S(1)} %broadcast_select_fusion.2), channel_id=1, source_target_pairs={{0,8},{8,0},{1,9},{9,1},{2,10},{10,2},{3,11},{11,3},{4,12},{12,4},... | collective-permute-start | bytes 3145736 | tf_op jit(solution)/shard_map/ppermute | solution.py:79
  34.6 2.3 %collective-permute-done = bf16[512,1024]{1,0:T(8,128)(2,1)S(1)} collective-permute-done((bf16[512,1024]{1,0:T(8,128)(2,1)S(1)}, bf16[512,1024]{1,0:T(8,128)(2,1)S(1)}, u32[]{:S(2)}, u32[]{:S(2)}) %collective-permute-start) | collective-permute-done | bytes 1048608 | tf_op jit(solution)/shard_map/ppermute | solution.py:79
  36.8 1.0 copy-done.2
  37.9 0.9 multiply_reduce_fusion.1
  38.8 16.8 %all-to-all-done = bf16[64,8,1024]{2,1,0:T(8,128)(2,1)S(1)} async-done(((bf16[64,8,1024]{2,1,0:T(8,128)(2,1)}), bf16[64,8,1024]{2,1,0:T(8,128)(2,1)S(1)}, u32[]{:S(2)}, u32[]{:S(2)}) %all-to-all-start) | async-done | bytes 1048608 | tf_op jit(solution)/shard_map/all_to_all | solution.py:86
  55.6 0.3 multiply_reduce_fusion.2
  55.9 0.1 add.66
  56.0 2.0 %add_subtract_fusion.1 = f32[512,512]{1,0:T(8,128)S(1)} fusion(bf16[64,8,1024]{2,1,0:T(8,128)(2,1)S(1)} %all-to-all-done, f32[512]{0:T(512)S(1)} %get-tuple-element.5, f32[512]{0:T(512)S(1)} %add.66, bf16[512,1024]{1,0:T(8,128)(2,1)S(1)} %copy-done.1, bf16[512,1024]{1,0:T(8,128)(2,1)} %copy-done.2, pred[]{:T(512)S(6)} %eq.8), kind=kOutput, calls=%fused_computation.33 | convolution fusion | flops 538181632 | bytes 4198401 | tf_op jit(solution)/shard_map/dot_general | solution.py:46
  58.0 0.8 add_subtract_fusion
  58.7 1.6 %pad_maximum_fusion = f32[2,8,64,512]{3,2,1,0:T(8,128)} fusion(f32[1,8,64,512]{3,2,1,0:T(8,128)S(1)} %bitcast.122, f32[1,8,64,512]{3,2,1,0:T(8,128)S(1)} %bitcast.121), kind=kLoop, calls=%fused_computation.8 | loop fusion | flops 524288 | bytes 4194304 | tf_op jit(solution)/shard_map/stack | solution.py:118
  60.3 4.9 %all-to-all-start.1 = ((f32[16,64,512]{2,1,0:T(8,128)}), f32[16,64,512]{2,1,0:T(8,128)S(1)}, u32[]{:S(2)}, u32[]{:S(2)}) async-start(f32[16,64,512]{2,1,0:T(8,128)} %bitcast.112), calls=%async_computation.1 | async-start | bytes 4194304 | tf_op jit(solution)/shard_map/all_to_all | solution.py:128
  65.2 0.1 fusion.38
  65.3 26.9 %all-to-all-done.1 = f32[16,64,512]{2,1,0:T(8,128)S(1)} async-done(((f32[16,64,512]{2,1,0:T(8,128)}), f32[16,64,512]{2,1,0:T(8,128)S(1)}, u32[]{:S(2)}, u32[]{:S(2)}) %all-to-all-start.1) | async-done | bytes 2097184 | tf_op jit(solution)/shard_map/all_to_all | solution.py:128
  92.2 0.2 bitcast_reduce_fusion
  92.5 0.1 exponential_convert_fusion
  92.6 0.8 broadcast_in_dim.32
  93.4 4.0 %all-to-all-start.2 = ((bf16[8,64,512]{2,1,0:T(8,128)(2,1)}), bf16[8,64,512]{2,1,0:T(8,128)(2,1)S(1)}, u32[]{:S(2)}, u32[]{:S(2)}) async-start(bf16[8,64,512]{2,1,0:T(8,128)(2,1)} %broadcast_in_dim.32), calls=%async_computation.2 | async-start | bytes 1048576 | tf_op jit(solution)/shard_map/all_to_all | solution.py:94
  97.4 0.1 convert_reduce_fusion.1
  97.5 0.2 fusion.25
  97.7 8.7 %all-to-all-done.2 = bf16[8,64,512]{2,1,0:T(8,128)(2,1)S(1)} async-done(((bf16[8,64,512]{2,1,0:T(8,128)(2,1)}), bf16[8,64,512]{2,1,0:T(8,128)(2,1)S(1)}, u32[]{:S(2)}, u32[]{:S(2)}) %all-to-all-start.2) | async-done | bytes 524320 | tf_op jit(solution)/shard_map/all_to_all | solution.py:94
  106.4 0.1 convert_reduce_fusion
  106.5 0.1 div.102
  106.6 0.3 multiply_reduce_fusion.3
  106.9 1.3 convolution_bitcast_fusion
  108.2 0.2 bitcast_dynamic-update-slice_fusion
  108.6 0.1 copy.51
  108.7 0.2 copy.52
  108.9 22.5 %all_to_all.27 = f32[64,1,656]{2,1,0:T(1,128)S(1)} all-to-all(f32[64,1,656]{2,1,0:T(1,128)S(1)} %copy.52), channel_id=1, replica_groups=mesh['z'=8,'y_hi'=4,'core'=2,'x'=4,'y_lo'=2] {'z','y_hi','core'}, dimensions={0} | all-to-all | bytes 335872 | tf_op jit(solution)/shard_map/all_to_all | solution.py:167
  131.5 0.1 slice_reduce_fusion.2
  131.6 0.1 slice_reduce_fusion.1
  131.8 0.1 reduce_sum.175
  131.9 0.1 multiply_reduce_fusion.4
  132.1 0.7 rsqrt_multiply_fusion
  (30 shorter events, 0.5 us)
Async XLA Ops:
  0.0 2.3 %copy-start = (bf16[512,128]{1,0:T(8,128)(2,1)S(1)}, bf16[512,128]{1,0:T(8,128)(2,1)}, u32[]{:S(2)}) copy-start(bf16[512,128]{1,0:T(8,128)(2,1)} %param.7) | copy-start | bytes 393220
  5.0 50.6 %all-to-all-start = ((bf16[64,8,1024]{2,1,0:T(8,128)(2,1)}), bf16[64,8,1024]{2,1,0:T(8,128)(2,1)S(1)}, u32[]{:S(2)}, u32[]{:S(2)}) async-start(bf16[64,8,1024]{2,1,0:T(8,128)(2,1)} %bitcast.12), calls=%async_computation | async-start | bytes 2097152 | tf_op jit(solution)/shard_map/all_to_all | solution.py:86
  22.8 4.5 %copy-start.3 = (bf16[512,128]{1,0:T(8,128)(2,1)S(1)}, bf16[512,128]{1,0:T(8,128)(2,1)}, u32[]{:S(2)}) copy-start(bf16[512,128]{1,0:T(8,128)(2,1)} %param.8) | copy-start | bytes 393220
  27.2 4.8 %copy-start.1 = (bf16[512,1024]{1,0:T(8,128)(2,1)S(1)}, bf16[512,1024]{1,0:T(8,128)(2,1)}, u32[]{:S(2)}) copy-start(bf16[512,1024]{1,0:T(8,128)(2,1)} %param.6) | copy-start | bytes 3145732
  32.2 4.6 %collective-permute-start = (bf16[512,1024]{1,0:T(8,128)(2,1)S(1)}, bf16[512,1024]{1,0:T(8,128)(2,1)S(1)}, u32[]{:S(2)}, u32[]{:S(2)}) collective-permute-start(bf16[512,1024]{1,0:T(8,128)(2,1)S(1)} %broadcast_select_fusion.2), channel_id=1, source_target_pairs={{0,8},{8,0},{1,9},{9,1},{2,10},{10,2},{3,11},{11,3},{4,12},{12,4},... | collective-permute-start | bytes 3145736 | tf_op jit(solution)/shard_map/ppermute | solution.py:79
  36.8 1.0 copy-start.2
  55.9 9.3 %copy-start.4 = (f32[512]{0:T(512)S(1)}, f32[512]{0:T(512)}, u32[]{:S(2)}) copy-start(f32[512]{0:T(512)} %param.11) | copy-start | bytes 6148
  56.0 9.3 %copy-start.5 = (f32[512]{0:T(512)S(1)}, f32[512]{0:T(512)}, u32[]{:S(2)}) copy-start(f32[512]{0:T(512)} %param.10) | copy-start | bytes 6148
  60.3 31.9 %all-to-all-start.1 = ((f32[16,64,512]{2,1,0:T(8,128)}), f32[16,64,512]{2,1,0:T(8,128)S(1)}, u32[]{:S(2)}, u32[]{:S(2)}) async-start(f32[16,64,512]{2,1,0:T(8,128)} %bitcast.112), calls=%async_computation.1 | async-start | bytes 4194304 | tf_op jit(solution)/shard_map/all_to_all | solution.py:128
  93.4 12.9 %all-to-all-start.2 = ((bf16[8,64,512]{2,1,0:T(8,128)(2,1)}), bf16[8,64,512]{2,1,0:T(8,128)(2,1)S(1)}, u32[]{:S(2)}, u32[]{:S(2)}) async-start(bf16[8,64,512]{2,1,0:T(8,128)(2,1)} %broadcast_in_dim.32), calls=%async_computation.2 | async-start | bytes 1048576 | tf_op jit(solution)/shard_map/all_to_all | solution.py:94

commit v12 on v11

--- a/solution.py
+++ b/solution.py
@@ -112,18 +112,15 @@
     ).reshape(landmarks, queries.shape[1])
     attended = attend(queries, key_rows, value_rows)
     swapped = swap_cores(jnp.where(first, attended, queries))
-    tokens = [jnp.where(first, queries, swapped), jnp.where(first, swapped, attended)]
+    tokens = jnp.stack(
+        [jnp.where(first, queries, swapped), jnp.where(first, swapped, attended)]
+    )
 
-    mark_norms = squares_by_row(marks)
-    distance_part = jnp.stack(
-        [
-            (
-                mark_norms[:, None]
-                + squares_by_row(rows)[None, :]
-                - 2.0 * inner_rows(marks, rows)
-            ).reshape(model_count, row_share, length)
-            for rows in tokens
-        ]
+    cross = jnp.einsum("mc,ktc->kmt", marks, tokens, preferred_element_type=jnp.float32)
+    distance_part = (
+        squares_by_row(marks)[None, :, None]
+        + squares_by_row(tokens)[:, None, :]
+        - 2.0 * cross
     ).reshape(2 * model_count, row_share, length)
     received = lax.all_to_all(distance_part, PAIR, 0, 0, tiled=True)
     distance = jnp.sum(received.reshape(2, model_count, row_share, length), axis=1)

time: 133 us -> 133 us (level)
  other arithmetic: 8.02 us -> 6.22 us
    dot_general x2 -> x1, matrix products: 2.74 us -> 4.18 us  [shards(): jnp.einsum('mc,ktc->kmt', marks, tokens, preferred_element_type=jnp.float32)]
    another operation x2, other arithmetic: 1.7 us -> 0.27 us  [the longest x1 0.17 us: shards(): jnp.stack([jnp.where(first, queries, swapped), jnp.where(first, swapped,...]
  transfers between devices with their start and end apart: 4 -> 4, of which waited for: 4 -> 4; matrix products, arithmetic and copies ran while one was open for 8% -> 7% of each run, Pallas kernels for 0% -> 0%
where the time goes in v12:
time: 133 us
  waiting for transfers between devices  55.6 us (42%)
  starting transfers between devices  29 us (22%)
  blocking collectives  22.5 us (17%)
  matrix products  13.4 us (10%)
  other arithmetic  6.22 us (5%)
  local copies, waits for them, and re-layouts  5.76 us (4%)
    all_to_all x1, waiting for transfers between devices, shards(): received = lax.all_to_all(distance_part, PAIR, 0, 0, tiled=True)  26.9 us
    all_to_all x1, blocking collectives, shards(): received = lax.all_to_all(packed, DATA, 0, 0, tiled=True)  22.5 us
    all_to_all x1, waiting for transfers between devices, gather_marks(): lax.all_to_all(spread.reshape((data_count,) + query_marks.shape), DATA, 0...  17.8 us
    all_to_all x1, starting transfers between devices, gather_marks(): lax.all_to_all(spread.reshape((data_count,) + query_marks.shape), DATA, 0...  17.6 us
    all_to_all x1, waiting for transfers between devices, broadcast_gather(): return lax.all_to_all(spread, axis_name, 0, 0, tiled=True)  8.66 us
    all_to_all x1, starting transfers between devices, shards(): received = lax.all_to_all(distance_part, PAIR, 0, 0, tiled=True)  5.05 us
    dot_general x1, matrix products, shards(): jnp.einsum('mc,ktc->kmt', marks, tokens, preferred_element_type=jnp.float32)  4.18 us
    all_to_all x1, starting transfers between devices, broadcast_gather(): return lax.all_to_all(spread, axis_name, 0, 0, tiled=True)  3.97 us
  transfers between devices with their start and end apart: 4, of which 4 were waited for; matrix products, arithmetic and copies ran while one was open for 7% of the time, Pallas kernels for 0%

profile of v12, /device:TPU:1, one launch (start us, length us, event | category | flops | bytes accessed | tf_op | source)
XLA Modules:
  0.0 132.8 jit_solution(6781365223956742435)
XLA Ops:
  0.0 0.8 compare_select_fusion
  0.8 0.1 iota_compare_fusion.1
  0.8 1.5 %convolution_convert_fusion.1 = bf16[8,1024]{1,0:T(8,128)(2,1)S(1)} fusion(bf16[512,1024]{1,0:T(8,128)(2,1)} %param.6, s32[8]{0:T(128)S(1)} %compare_select_fusion), kind=kOutput, calls=%fused_computation.21 | convolution fusion | flops 8400896 | bytes 1064992 | tf_op jit(solution)/shard_map/dot_general | solution.py:73
  2.3 0.3 fusion.38
  2.6 0.2 fusion.25
  2.8 0.1 fusion.28
  2.9 1.1 fusion.10
  4.0 1.1 broadcast_in_dim.28
  5.1 17.6 %all-to-all-start = ((bf16[64,8,1024]{2,1,0:T(8,128)(2,1)}), bf16[64,8,1024]{2,1,0:T(8,128)(2,1)S(1)}, u32[]{:S(2)}, u32[]{:S(2)}) async-start(bf16[64,8,1024]{2,1,0:T(8,128)(2,1)} %bitcast.12), calls=%async_computation | async-start | bytes 2097152 | tf_op jit(solution)/shard_map/all_to_all | solution.py:86
  22.7 0.1 iota_compare_fusion
  22.8 1.7 %fusion.1 = (f32[8,512]{1,0:T(8,128)S(1)}, f32[512,512,8]{1,0,2:T(8,128)S(1)}) fusion(pred[512,512]{0,1:T(8,128)(4,1)S(1)} %iota_compare_fusion, bf16[512,128]{1,0:T(8,128)(2,1)S(1)} %copy-done, bf16[512,1024]{1,0:T(8,128)(2,1)S(1)} %copy-done.1), kind=kOutput, calls=%fused_computation.4 | convolution fusion | flops 543158272 | bytes 9846784 | tf_op jit(solution)/shard_map/tkgd,skd->kgts/dot_general | solution.py:28
  24.5 1.7 %fusion = f32[8,512]{1,0:T(8,128)S(1)} fusion(f32[512,512,8]{1,0,2:T(8,128)S(1)} %get-tuple-element.18, f32[8,512]{1,0:T(8,128)S(1)} %get-tuple-element.17, pred[512,512]{0,1:T(8,128)(4,1)S(1)} %iota_compare_fusion), kind=kLoop, calls=%fused_computation.3 | loop fusion | flops 8384512 | bytes 8683520 | tf_op jit(solution)/shard_map/reduce_sum | solution.py:34
  26.3 3.3 %fusion.5 = bf16[8,512,128]{1,2,0:T(8,128)(2,1)} fusion(f32[8,512]{1,0:T(8,128)S(1)} %fusion, f32[8,512]{1,0:T(8,128)S(1)} %get-tuple-element.17, f32[512,512,8]{1,0,2:T(8,128)S(1)} %get-tuple-element.18, pred[512,512]{0,1:T(8,128)(4,1)S(1)} %iota_compare_fusion, bf16[512,128]{1,0:T(8,128)(2,1)S(1)} %copy-done.4), kind=kOutput, calls=%fused_computation.13 | convolution fusion | flops 547880960 | bytes 9863168 | tf_op jit(solution)/shard_map/kgts,skd->tkgd/dot_general | solution.py:35
  29.6 1.5 %copy.46 = bf16[512,1024]{1,0:T(8,128)(2,1)S(1)} copy(bf16[512,1024]{0,1:T(8,128)(2,1)} %bitcast.120) | data formatting | bytes 2097152 | tf_op jit(solution)/shard_map/reshape | solution.py:38
  31.1 0.1 broadcast_select_fusion
  31.2 2.4 %collective-permute-start = (bf16[512,1024]{1,0:T(8,128)(2,1)S(1)}, bf16[512,1024]{1,0:T(8,128)(2,1)S(1)}, u32[]{:S(2)}, u32[]{:S(2)}) collective-permute-start(bf16[512,1024]{1,0:T(8,128)(2,1)S(1)} %broadcast_select_fusion), channel_id=1, source_target_pairs={{0,8},{8,0},{1,9},{9,1},{2,10},{10,2},{3,11},{11,3},{4,12},{12,4},... | collective-permute-start | bytes 3145736 | tf_op jit(solution)/shard_map/ppermute | solution.py:79
  33.6 2.3 %collective-permute-done = bf16[512,1024]{1,0:T(8,128)(2,1)S(1)} collective-permute-done((bf16[512,1024]{1,0:T(8,128)(2,1)S(1)}, bf16[512,1024]{1,0:T(8,128)(2,1)S(1)}, u32[]{:S(2)}, u32[]{:S(2)}) %collective-permute-start) | collective-permute-done | bytes 1048608 | tf_op jit(solution)/shard_map/ppermute | solution.py:79
  35.9 0.2 select_bitcast_fusion.1
  36.1 1.0 copy-done.2
  37.0 0.3 copy-done.3
  37.3 0.5 multiply_reduce_fusion
  37.8 17.8 %all-to-all-done = bf16[64,8,1024]{2,1,0:T(8,128)(2,1)S(1)} async-done(((bf16[64,8,1024]{2,1,0:T(8,128)(2,1)}), bf16[64,8,1024]{2,1,0:T(8,128)(2,1)S(1)}, u32[]{:S(2)}, u32[]{:S(2)}) %all-to-all-start) | async-done | bytes 1048608 | tf_op jit(solution)/shard_map/all_to_all | solution.py:86
  55.6 0.3 multiply_reduce_fusion.1
  55.9 0.1 add.55
  56.0 4.2 %bitcast_subtract_fusion = f32[2,512,512]{2,1,0:T(8,128)} fusion(bf16[1,512,1024]{2,1,0:T(8,128)(2,1)} %copy-done.3, bf16[1,512,1024]{2,1,0:T(8,128)(2,1)} %copy-done.2, bf16[64,8,1024]{2,1,0:T(8,128)(2,1)S(1)} %all-to-all-done, f32[2,512]{1,0:T(2,128)S(1)} %multiply_reduce_fusion, f32[512]{0:T(512)S(1)} %add.55), kind=kOutput, calls=%fused_computation.11 | convolution fusion | flops 1076363264 | bytes 5249024 | tf_op jit(solution)/shard_map/mc,ktc->kmt/dot_general | solution.py:119
  60.2 5.0 %all-to-all-start.1 = ((f32[16,64,512]{2,1,0:T(8,128)}), f32[16,64,512]{2,1,0:T(8,128)S(1)}, u32[]{:S(2)}, u32[]{:S(2)}) async-start(f32[16,64,512]{2,1,0:T(8,128)} %bitcast.113), calls=%async_computation.1 | async-start | bytes 4194304 | tf_op jit(solution)/shard_map/all_to_all | solution.py:125
  65.2 0.1 fusion.33
  65.3 26.9 %all-to-all-done.1 = f32[16,64,512]{2,1,0:T(8,128)S(1)} async-done(((f32[16,64,512]{2,1,0:T(8,128)}), f32[16,64,512]{2,1,0:T(8,128)S(1)}, u32[]{:S(2)}, u32[]{:S(2)}) %all-to-all-start.1) | async-done | bytes 2097184 | tf_op jit(solution)/shard_map/all_to_all | solution.py:125
  92.2 0.2 bitcast_reduce_fusion
  92.5 0.1 exponential_convert_fusion
  92.6 0.8 broadcast_in_dim.32
  93.4 4.0 %all-to-all-start.2 = ((bf16[8,64,512]{2,1,0:T(8,128)(2,1)}), bf16[8,64,512]{2,1,0:T(8,128)(2,1)S(1)}, u32[]{:S(2)}, u32[]{:S(2)}) async-start(bf16[8,64,512]{2,1,0:T(8,128)(2,1)} %broadcast_in_dim.32), calls=%async_computation.2 | async-start | bytes 1048576 | tf_op jit(solution)/shard_map/all_to_all | solution.py:94
  97.4 0.1 convert_reduce_fusion.1
  97.5 0.2 fusion.20
  97.7 8.7 %all-to-all-done.2 = bf16[8,64,512]{2,1,0:T(8,128)(2,1)S(1)} async-done(((bf16[8,64,512]{2,1,0:T(8,128)(2,1)}), bf16[8,64,512]{2,1,0:T(8,128)(2,1)S(1)}, u32[]{:S(2)}, u32[]{:S(2)}) %all-to-all-start.2) | async-done | bytes 524320 | tf_op jit(solution)/shard_map/all_to_all | solution.py:94
  106.4 0.1 convert_reduce_fusion
  106.5 0.1 div.102
  106.6 0.3 multiply_reduce_fusion.2
  106.9 1.3 convolution_bitcast_fusion
  108.2 0.2 bitcast_dynamic-update-slice_fusion
  108.6 0.1 copy.51
  108.7 0.2 copy.52
  108.9 22.5 %all_to_all.27 = f32[64,1,656]{2,1,0:T(1,128)S(1)} all-to-all(f32[64,1,656]{2,1,0:T(1,128)S(1)} %copy.52), channel_id=1, replica_groups=mesh['z'=8,'y_hi'=4,'core'=2,'x'=4,'y_lo'=2] {'z','y_hi','core'}, dimensions={0} | all-to-all | bytes 335872 | tf_op jit(solution)/shard_map/all_to_all | solution.py:164
  131.5 0.1 slice_reduce_fusion.2
  131.6 0.1 slice_reduce_fusion.1
  131.8 0.1 reduce_sum.165
  131.9 0.1 multiply_reduce_fusion.3
  132.1 0.7 rsqrt_multiply_fusion
  (31 shorter events, 0.5 us)
Async XLA Ops:
  0.0 2.3 %copy-start = (bf16[512,128]{1,0:T(8,128)(2,1)S(1)}, bf16[512,128]{1,0:T(8,128)(2,1)}, u32[]{:S(2)}) copy-start(bf16[512,128]{1,0:T(8,128)(2,1)} %param.7) | copy-start | bytes 393220
  0.0 22.8 %copy-start.1 = (bf16[512,1024]{1,0:T(8,128)(2,1)S(1)}, bf16[512,1024]{1,0:T(8,128)(2,1)}, u32[]{:S(2)}) copy-start(bf16[512,1024]{1,0:T(8,128)(2,1)} %param.6) | copy-start | bytes 3145732
  5.1 50.5 %all-to-all-start = ((bf16[64,8,1024]{2,1,0:T(8,128)(2,1)}), bf16[64,8,1024]{2,1,0:T(8,128)(2,1)S(1)}, u32[]{:S(2)}, u32[]{:S(2)}) async-start(bf16[64,8,1024]{2,1,0:T(8,128)(2,1)} %bitcast.12), calls=%async_computation | async-start | bytes 2097152 | tf_op jit(solution)/shard_map/all_to_all | solution.py:86
  24.5 1.7 %copy-start.4 = (bf16[512,128]{1,0:T(8,128)(2,1)S(1)}, bf16[512,128]{1,0:T(8,128)(2,1)}, u32[]{:S(2)}) copy-start(bf16[512,128]{1,0:T(8,128)(2,1)} %param.8) | copy-start | bytes 393220
  31.2 4.6 %collective-permute-start = (bf16[512,1024]{1,0:T(8,128)(2,1)S(1)}, bf16[512,1024]{1,0:T(8,128)(2,1)S(1)}, u32[]{:S(2)}, u32[]{:S(2)}) collective-permute-start(bf16[512,1024]{1,0:T(8,128)(2,1)S(1)} %broadcast_select_fusion), channel_id=1, source_target_pairs={{0,8},{8,0},{1,9},{9,1},{2,10},{10,2},{3,11},{11,3},{4,12},{12,4},... | collective-permute-start | bytes 3145736 | tf_op jit(solution)/shard_map/ppermute | solution.py:79
  36.0 1.0 copy-start.2
  36.0 1.3 copy-start.3
  60.2 5.1 %copy-start.5 = (f32[512]{0:T(512)S(1)}, f32[512]{0:T(512)}, u32[]{:S(2)}) copy-start(f32[512]{0:T(512)} %param.11) | copy-start | bytes 6148
  60.2 5.1 %copy-start.6 = (f32[512]{0:T(512)S(1)}, f32[512]{0:T(512)}, u32[]{:S(2)}) copy-start(f32[512]{0:T(512)} %param.10) | copy-start | bytes 6148
  60.2 32.1 %all-to-all-start.1 = ((f32[16,64,512]{2,1,0:T(8,128)}), f32[16,64,512]{2,1,0:T(8,128)S(1)}, u32[]{:S(2)}, u32[]{:S(2)}) async-start(f32[16,64,512]{2,1,0:T(8,128)} %bitcast.113), calls=%async_computation.1 | async-start | bytes 4194304 | tf_op jit(solution)/shard_map/all_to_all | solution.py:125
  93.4 12.9 %all-to-all-start.2 = ((bf16[8,64,512]{2,1,0:T(8,128)(2,1)}), bf16[8,64,512]{2,1,0:T(8,128)(2,1)S(1)}, u32[]{:S(2)}, u32[]{:S(2)}) async-start(bf16[8,64,512]{2,1,0:T(8,128)(2,1)} %broadcast_in_dim.32), calls=%async_computation.2 | async-start | bytes 1048576 | tf_op jit(solution)/shard_map/all_to_all | solution.py:94

commit v13 on v11

--- a/solution.py
+++ b/solution.py
@@ -69,10 +69,9 @@
 
 
 def pick_rows(matrix, rows):
-    hits = rows[:, None] == lax.broadcasted_iota(jnp.int32, (rows.shape[0], matrix.shape[0]), 1)
-    return jnp.dot(
-        hits.astype(matrix.dtype), matrix, preferred_element_type=jnp.float32
-    ).astype(matrix.dtype)
+    return jnp.concatenate(
+        [lax.dynamic_slice_in_dim(matrix, rows[i], 1, 0) for i in range(rows.shape[0])]
+    )
 
 
 def swap_cores(piece):

time: 133 us -> 148 us (1.11)
  between operations: 0.27 us -> 15.1 us
  local copies, waits for them, and re-layouts: 5.52 us -> 7.15 us
  matrix products: 12.9 us -> 11.4 us
    dot_general x1 -> x0, matrix products: 1.5 us -> none  [pick_rows(): jnp.dot(hits.astype(matrix.dtype), matrix, preferred_element_type=jnp.flo...]
  transfers between devices with their start and end apart: 4 -> 4, of which waited for: 4 -> 4; matrix products, arithmetic and copies ran while one was open for 8% -> 7% of each run, Pallas kernels for 0% -> 0%
where the time goes in v13:
time: 148 us
  waiting for transfers between devices  54.6 us (37%)
  starting transfers between devices  28.9 us (20%)
  blocking collectives  22.5 us (15%)
  between operations  15.1 us (10%)
  matrix products  11.4 us (8%)
  other arithmetic  8 us (5%)
  local copies, waits for them, and re-layouts  7.15 us (5%)
    all_to_all x1, waiting for transfers between devices, shards(): received = lax.all_to_all(distance_part, PAIR, 0, 0, tiled=True)  26.9 us
    all_to_all x1, blocking collectives, shards(): received = lax.all_to_all(packed, DATA, 0, 0, tiled=True)  22.5 us
    all_to_all x1, starting transfers between devices, gather_marks(): lax.all_to_all(spread.reshape((data_count,) + query_marks.shape), DATA, 0...  17.6 us
    all_to_all x1, waiting for transfers between devices, gather_marks(): lax.all_to_all(spread.reshape((data_count,) + query_marks.shape), DATA, 0...  16.8 us
    all_to_all x1, waiting for transfers between devices, broadcast_gather(): return lax.all_to_all(spread, axis_name, 0, 0, tiled=True)  8.66 us
    all_to_all x1, starting transfers between devices, shards(): received = lax.all_to_all(distance_part, PAIR, 0, 0, tiled=True)  4.89 us
    all_to_all x1, starting transfers between devices, broadcast_gather(): return lax.all_to_all(spread, axis_name, 0, 0, tiled=True)  3.97 us
    dot_general x1, matrix products, attend(): jnp.einsum('kgts,skd->tkgd', weights, value_three, preferred_element_type...  3.33 us
  transfers between devices with their start and end apart: 4, of which 4 were waited for; matrix products, arithmetic and copies ran while one was open for 7% of the time, Pallas kernels for 0%

profile of v13, /device:TPU:1, one launch (start us, length us, event | category | flops | bytes accessed | tf_op | source)
XLA Modules:
  0.0 147.7 jit_solution(15051684365974725189)
XLA Ops:
  0.0 0.7 compare_select_fusion
  0.7 0.7 fusion.42
  11.3 0.1 iota_compare_fusion.1
  16.3 0.9 constant_dynamic-slice_fusion
  17.3 0.3 fusion.43
  17.5 0.2 fusion.30
  17.7 0.1 fusion.33
  17.8 1.1 fusion.10
  18.9 1.1 broadcast_in_dim.28
  20.0 17.6 %all-to-all-start = ((bf16[64,8,1024]{2,1,0:T(8,128)(2,1)}), bf16[64,8,1024]{2,1,0:T(8,128)(2,1)S(1)}, u32[]{:S(2)}, u32[]{:S(2)}) async-start(bf16[64,8,1024]{2,1,0:T(8,128)(2,1)} %bitcast.19), calls=%async_computation | async-start | bytes 2097152 | tf_op jit(solution)/shard_map/all_to_all | solution.py:85
  37.6 0.1 iota_compare_fusion
  37.7 2.7 %fusion.1 = (f32[8,512]{1,0:T(8,128)S(1)}, f32[512,512,8]{1,0,2:T(8,128)S(1)}) fusion(pred[512,512]{0,1:T(8,128)(4,1)S(1)} %iota_compare_fusion, bf16[512,128]{1,0:T(8,128)(2,1)S(1)} %copy-done, bf16[512,1024]{1,0:T(8,128)(2,1)} %param.6), kind=kOutput, calls=%fused_computation.4 | convolution fusion | flops 543158272 | bytes 9846784 | tf_op jit(solution)/shard_map/tkgd,skd->kgts/dot_general | solution.py:28
  40.5 1.7 %fusion = f32[8,512]{1,0:T(8,128)S(1)} fusion(f32[512,512,8]{1,0,2:T(8,128)S(1)} %get-tuple-element.34, f32[8,512]{1,0:T(8,128)S(1)} %get-tuple-element.33, pred[512,512]{0,1:T(8,128)(4,1)S(1)} %iota_compare_fusion), kind=kLoop, calls=%fused_computation.3 | loop fusion | flops 8384512 | bytes 8683520 | tf_op jit(solution)/shard_map/reduce_sum | solution.py:34
  42.2 3.3 %fusion.5 = bf16[8,512,128]{1,2,0:T(8,128)(2,1)} fusion(f32[8,512]{1,0:T(8,128)S(1)} %fusion, f32[8,512]{1,0:T(8,128)S(1)} %get-tuple-element.33, f32[512,512,8]{1,0,2:T(8,128)S(1)} %get-tuple-element.34, pred[512,512]{0,1:T(8,128)(4,1)S(1)} %iota_compare_fusion, bf16[512,128]{1,0:T(8,128)(2,1)S(1)} %copy-done.3), kind=kOutput, calls=%fused_computation.13 | convolution fusion | flops 547880960 | bytes 9863168 | tf_op jit(solution)/shard_map/kgts,skd->tkgd/dot_general | solution.py:35
  45.5 1.5 %copy.42 = bf16[512,1024]{1,0:T(8,128)(2,1)S(1)} copy(bf16[512,1024]{0,1:T(8,128)(2,1)} %bitcast.132) | data formatting | bytes 2097152 | tf_op jit(solution)/shard_map/reshape | solution.py:38
  47.0 0.1 broadcast_select_fusion.2
  47.2 2.4 %collective-permute-start = (bf16[512,1024]{1,0:T(8,128)(2,1)S(1)}, bf16[512,1024]{1,0:T(8,128)(2,1)S(1)}, u32[]{:S(2)}, u32[]{:S(2)}) collective-permute-start(bf16[512,1024]{1,0:T(8,128)(2,1)S(1)} %broadcast_select_fusion.2), channel_id=1, source_target_pairs={{0,8},{8,0},{1,9},{9,1},{2,10},{10,2},{3,11},{11,3},{4,12},{12,4},... | collective-permute-start | bytes 3145736 | tf_op jit(solution)/shard_map/ppermute | solution.py:78
  49.5 2.3 %collective-permute-done = bf16[512,1024]{1,0:T(8,128)(2,1)S(1)} collective-permute-done((bf16[512,1024]{1,0:T(8,128)(2,1)S(1)}, bf16[512,1024]{1,0:T(8,128)(2,1)S(1)}, u32[]{:S(2)}, u32[]{:S(2)}) %collective-permute-start) | collective-permute-done | bytes 1048608 | tf_op jit(solution)/shard_map/ppermute | solution.py:78
  51.8 1.0 copy-done.2
  52.8 0.9 multiply_reduce_fusion.1
  53.8 16.8 %all-to-all-done = bf16[64,8,1024]{2,1,0:T(8,128)(2,1)S(1)} async-done(((bf16[64,8,1024]{2,1,0:T(8,128)(2,1)}), bf16[64,8,1024]{2,1,0:T(8,128)(2,1)S(1)}, u32[]{:S(2)}, u32[]{:S(2)}) %all-to-all-start) | async-done | bytes 1048608 | tf_op jit(solution)/shard_map/all_to_all | solution.py:85
  70.6 0.3 multiply_reduce_fusion.2
  70.8 0.1 add.106
  70.9 0.8 add_subtract_fusion
  71.7 2.0 %add_subtract_fusion.1 = f32[512,512]{1,0:T(8,128)S(1)} fusion(bf16[64,8,1024]{2,1,0:T(8,128)(2,1)S(1)} %all-to-all-done, f32[512]{0:T(512)S(1)} %get-tuple-element.5, f32[512]{0:T(512)S(1)} %add.106, bf16[512,1024]{1,0:T(8,128)(2,1)S(1)} %copy-done.1, bf16[512,1024]{1,0:T(8,128)(2,1)} %copy-done.2, pred[]{:T(512)S(6)} %eq.3), kind=kOutput, calls=%fused_computation.32 | convolution fusion | flops 538181632 | bytes 4198401 | tf_op jit(solution)/shard_map/dot_general | solution.py:46
  73.7 1.6 %pad_maximum_fusion = f32[2,8,64,512]{3,2,1,0:T(8,128)} fusion(f32[1,8,64,512]{3,2,1,0:T(8,128)S(1)} %bitcast.133, f32[1,8,64,512]{3,2,1,0:T(8,128)S(1)} %bitcast.134), kind=kLoop, calls=%fused_computation.8 | loop fusion | flops 524288 | bytes 4194304 | tf_op jit(solution)/shard_map/stack | solution.py:117
  75.3 4.9 %all-to-all-start.1 = ((f32[16,64,512]{2,1,0:T(8,128)}), f32[16,64,512]{2,1,0:T(8,128)S(1)}, u32[]{:S(2)}, u32[]{:S(2)}) async-start(f32[16,64,512]{2,1,0:T(8,128)} %bitcast.124), calls=%async_computation.1 | async-start | bytes 4194304 | tf_op jit(solution)/shard_map/all_to_all | solution.py:127
  80.2 0.1 fusion.38
  80.3 26.9 %all-to-all-done.1 = f32[16,64,512]{2,1,0:T(8,128)S(1)} async-done(((f32[16,64,512]{2,1,0:T(8,128)}), f32[16,64,512]{2,1,0:T(8,128)S(1)}, u32[]{:S(2)}, u32[]{:S(2)}) %all-to-all-start.1) | async-done | bytes 2097184 | tf_op jit(solution)/shard_map/all_to_all | solution.py:127
  107.2 0.2 bitcast_reduce_fusion
  107.4 0.1 exponential_convert_fusion
  107.5 0.8 broadcast_in_dim.32
  108.4 4.0 %all-to-all-start.2 = ((bf16[8,64,512]{2,1,0:T(8,128)(2,1)}), bf16[8,64,512]{2,1,0:T(8,128)(2,1)S(1)}, u32[]{:S(2)}, u32[]{:S(2)}) async-start(bf16[8,64,512]{2,1,0:T(8,128)(2,1)} %broadcast_in_dim.32), calls=%async_computation.2 | async-start | bytes 1048576 | tf_op jit(solution)/shard_map/all_to_all | solution.py:93
  112.3 0.1 convert_reduce_fusion.1
  112.5 0.2 fusion.25
  112.7 8.7 %all-to-all-done.2 = bf16[8,64,512]{2,1,0:T(8,128)(2,1)S(1)} async-done(((bf16[8,64,512]{2,1,0:T(8,128)(2,1)}), bf16[8,64,512]{2,1,0:T(8,128)(2,1)S(1)}, u32[]{:S(2)}, u32[]{:S(2)}) %all-to-all-start.2) | async-done | bytes 524320 | tf_op jit(solution)/shard_map/all_to_all | solution.py:93
  121.3 0.1 convert_reduce_fusion
  121.5 0.3 multiply_reduce_fusion.3
  121.8 1.3 convolution_bitcast_fusion
  123.2 0.2 bitcast_dynamic-update-slice_fusion
  123.5 0.1 copy.47
  123.7 0.2 copy.48
  123.9 22.5 %all_to_all.27 = f32[64,1,656]{2,1,0:T(1,128)S(1)} all-to-all(f32[64,1,656]{2,1,0:T(1,128)S(1)} %copy.48), channel_id=1, replica_groups=mesh['z'=8,'y_hi'=4,'core'=2,'x'=4,'y_lo'=2] {'z','y_hi','core'}, dimensions={0} | all-to-all | bytes 335872 | tf_op jit(solution)/shard_map/all_to_all | solution.py:166
  146.4 0.1 slice_reduce_fusion.1
  146.5 0.1 slice_reduce_fusion.2
  146.6 0.1 reduce_sum.175
  146.9 0.1 multiply_reduce_fusion.4
  147.0 0.7 rsqrt_multiply_fusion
  (32 shorter events, 0.6 us)
Async XLA Ops:
  0.0 17.3 %copy-start = (bf16[512,128]{1,0:T(8,128)(2,1)S(1)}, bf16[512,128]{1,0:T(8,128)(2,1)}, u32[]{:S(2)}) copy-start(bf16[512,128]{1,0:T(8,128)(2,1)} %param.7) | copy-start | bytes 393220
  20.0 50.5 %all-to-all-start = ((bf16[64,8,1024]{2,1,0:T(8,128)(2,1)}), bf16[64,8,1024]{2,1,0:T(8,128)(2,1)S(1)}, u32[]{:S(2)}, u32[]{:S(2)}) async-start(bf16[64,8,1024]{2,1,0:T(8,128)(2,1)} %bitcast.19), calls=%async_computation | async-start | bytes 2097152 | tf_op jit(solution)/shard_map/all_to_all | solution.py:85
  37.7 4.5 %copy-start.3 = (bf16[512,128]{1,0:T(8,128)(2,1)S(1)}, bf16[512,128]{1,0:T(8,128)(2,1)}, u32[]{:S(2)}) copy-start(bf16[512,128]{1,0:T(8,128)(2,1)} %param.8) | copy-start | bytes 393220
  42.2 4.8 %copy-start.1 = (bf16[512,1024]{1,0:T(8,128)(2,1)S(1)}, bf16[512,1024]{1,0:T(8,128)(2,1)}, u32[]{:S(2)}) copy-start(bf16[512,1024]{1,0:T(8,128)(2,1)} %param.6) | copy-start | bytes 3145732
  47.2 4.6 %collective-permute-start = (bf16[512,1024]{1,0:T(8,128)(2,1)S(1)}, bf16[512,1024]{1,0:T(8,128)(2,1)S(1)}, u32[]{:S(2)}, u32[]{:S(2)}) collective-permute-start(bf16[512,1024]{1,0:T(8,128)(2,1)S(1)} %broadcast_select_fusion.2), channel_id=1, source_target_pairs={{0,8},{8,0},{1,9},{9,1},{2,10},{10,2},{3,11},{11,3},{4,12},{12,4},... | collective-permute-start | bytes 3145736 | tf_op jit(solution)/shard_map/ppermute | solution.py:78
  51.8 1.0 copy-start.2
  70.9 9.3 %copy-start.4 = (f32[512]{0:T(512)S(1)}, f32[512]{0:T(512)}, u32[]{:S(2)}) copy-start(f32[512]{0:T(512)} %param.11) | copy-start | bytes 6148
  70.9 9.2 %copy-start.5 = (f32[512]{0:T(512)S(1)}, f32[512]{0:T(512)}, u32[]{:S(2)}) copy-start(f32[512]{0:T(512)} %param.10) | copy-start | bytes 6148
  75.3 31.9 %all-to-all-start.1 = ((f32[16,64,512]{2,1,0:T(8,128)}), f32[16,64,512]{2,1,0:T(8,128)S(1)}, u32[]{:S(2)}, u32[]{:S(2)}) async-start(f32[16,64,512]{2,1,0:T(8,128)} %bitcast.124), calls=%async_computation.1 | async-start | bytes 4194304 | tf_op jit(solution)/shard_map/all_to_all | solution.py:127
  108.4 12.9 %all-to-all-start.2 = ((bf16[8,64,512]{2,1,0:T(8,128)(2,1)}), bf16[8,64,512]{2,1,0:T(8,128)(2,1)S(1)}, u32[]{:S(2)}, u32[]{:S(2)}) async-start(bf16[8,64,512]{2,1,0:T(8,128)(2,1)} %broadcast_in_dim.32), calls=%async_computation.2 | async-start | bytes 1048576 | tf_op jit(solution)/shard_map/all_to_all | solution.py:93

commit v14 on v11

--- a/solution.py
+++ b/solution.py
@@ -164,7 +164,10 @@
         ],
         axis=1,
     )
-    received = lax.all_to_all(packed, DATA, 0, 0, tiled=True)
+    width = packed.shape[1]
+    padded = jnp.pad(packed, ((0, 0), (0, -width % 1024))).reshape(data_count, -1, 8, 128)
+    received = lax.all_to_all(padded, DATA, 0, 0, tiled=True)
+    received = received.reshape(data_count, -1)[:, :width]
     cut = row_share * column_share
     second_parts = received[:, :cut].reshape(data_count, row_share, column_share)
     row_means = received[:, cut : cut + row_share]

time: 133 us -> 134 us (level)
  no operation moved by 1% of the time
where the time goes in v14:
time: 134 us
  waiting for transfers between devices  54.6 us (41%)
  starting transfers between devices  28.9 us (22%)
  blocking collectives  23.6 us (18%)
  matrix products  12.9 us (10%)
  other arithmetic  8.02 us (6%)
  local copies, waits for them, and re-layouts  5.61 us (4%)
    all_to_all x1, waiting for transfers between devices, shards(): received = lax.all_to_all(distance_part, PAIR, 0, 0, tiled=True)  26.9 us
    all_to_all x1, blocking collectives, shards(): received = lax.all_to_all(padded, DATA, 0, 0, tiled=True)  23.6 us
    all_to_all x1, starting transfers between devices, gather_marks(): lax.all_to_all(spread.reshape((data_count,) + query_marks.shape), DATA, 0...  17.6 us
    all_to_all x1, waiting for transfers between devices, gather_marks(): lax.all_to_all(spread.reshape((data_count,) + query_marks.shape), DATA, 0...  16.8 us
    all_to_all x1, waiting for transfers between devices, broadcast_gather(): return lax.all_to_all(spread, axis_name, 0, 0, tiled=True)  8.66 us
    all_to_all x1, starting transfers between devices, shards(): received = lax.all_to_all(distance_part, PAIR, 0, 0, tiled=True)  4.9 us
    all_to_all x1, starting transfers between devices, broadcast_gather(): return lax.all_to_all(spread, axis_name, 0, 0, tiled=True)  3.97 us
    dot_general x1, matrix products, attend(): jnp.einsum('kgts,skd->tkgd', weights, value_three, preferred_element_type...  3.33 us
  transfers between devices with their start and end apart: 4, of which 4 were waited for; matrix products, arithmetic and copies ran while one was open for 8% of the time, Pallas kernels for 0%

profile of v14, /device:TPU:1, one launch (start us, length us, event | category | flops | bytes accessed | tf_op | source)
XLA Modules:
  0.0 133.9 jit_solution(15407434374242880066)
XLA Ops:
  0.0 0.7 compare_select_fusion
  0.7 0.1 iota_compare_fusion.1
  0.8 1.5 %convolution_convert_fusion.1 = bf16[8,1024]{1,0:T(8,128)(2,1)S(1)} fusion(bf16[512,1024]{1,0:T(8,128)(2,1)} %param.6, s32[8]{0:T(128)S(1)} %compare_select_fusion), kind=kOutput, calls=%fused_computation.23 | convolution fusion | flops 8400896 | bytes 1064992 | tf_op jit(solution)/shard_map/dot_general | solution.py:73
  2.3 0.3 fusion.42
  2.5 0.2 fusion.30
  2.7 0.1 fusion.33
  2.8 1.1 fusion.10
  3.9 1.1 broadcast_in_dim.28
  5.0 17.6 %all-to-all-start = ((bf16[64,8,1024]{2,1,0:T(8,128)(2,1)}), bf16[64,8,1024]{2,1,0:T(8,128)(2,1)S(1)}, u32[]{:S(2)}, u32[]{:S(2)}) async-start(bf16[64,8,1024]{2,1,0:T(8,128)(2,1)} %bitcast.12), calls=%async_computation | async-start | bytes 2097152 | tf_op jit(solution)/shard_map/all_to_all | solution.py:86
  22.7 0.1 iota_compare_fusion
  22.8 2.7 %fusion.1 = (f32[8,512]{1,0:T(8,128)S(1)}, f32[512,512,8]{1,0,2:T(8,128)S(1)}) fusion(pred[512,512]{0,1:T(8,128)(4,1)S(1)} %iota_compare_fusion, bf16[512,128]{1,0:T(8,128)(2,1)S(1)} %copy-done, bf16[512,1024]{1,0:T(8,128)(2,1)} %param.6), kind=kOutput, calls=%fused_computation.4 | convolution fusion | flops 543158272 | bytes 9846784 | tf_op jit(solution)/shard_map/tkgd,skd->kgts/dot_general | solution.py:28
  25.5 1.7 %fusion = f32[8,512]{1,0:T(8,128)S(1)} fusion(f32[512,512,8]{1,0,2:T(8,128)S(1)} %get-tuple-element.18, f32[8,512]{1,0:T(8,128)S(1)} %get-tuple-element.17, pred[512,512]{0,1:T(8,128)(4,1)S(1)} %iota_compare_fusion), kind=kLoop, calls=%fused_computation.3 | loop fusion | flops 8384512 | bytes 8683520 | tf_op jit(solution)/shard_map/reduce_sum | solution.py:34
  27.2 3.3 %fusion.5 = bf16[8,512,128]{1,2,0:T(8,128)(2,1)} fusion(f32[8,512]{1,0:T(8,128)S(1)} %fusion, f32[8,512]{1,0:T(8,128)S(1)} %get-tuple-element.17, f32[512,512,8]{1,0,2:T(8,128)S(1)} %get-tuple-element.18, pred[512,512]{0,1:T(8,128)(4,1)S(1)} %iota_compare_fusion, bf16[512,128]{1,0:T(8,128)(2,1)S(1)} %copy-done.3), kind=kOutput, calls=%fused_computation.13 | convolution fusion | flops 547880960 | bytes 9863168 | tf_op jit(solution)/shard_map/kgts,skd->tkgd/dot_general | solution.py:35
  30.6 1.5 %copy.46 = bf16[512,1024]{1,0:T(8,128)(2,1)S(1)} copy(bf16[512,1024]{0,1:T(8,128)(2,1)} %bitcast.122) | data formatting | bytes 2097152 | tf_op jit(solution)/shard_map/reshape | solution.py:38
  32.1 0.1 broadcast_select_fusion.2
  32.2 2.4 %collective-permute-start = (bf16[512,1024]{1,0:T(8,128)(2,1)S(1)}, bf16[512,1024]{1,0:T(8,128)(2,1)S(1)}, u32[]{:S(2)}, u32[]{:S(2)}) collective-permute-start(bf16[512,1024]{1,0:T(8,128)(2,1)S(1)} %broadcast_select_fusion.2), channel_id=1, source_target_pairs={{0,8},{8,0},{1,9},{9,1},{2,10},{10,2},{3,11},{11,3},{4,12},{12,4},... | collective-permute-start | bytes 3145736 | tf_op jit(solution)/shard_map/ppermute | solution.py:79
  34.6 2.3 %collective-permute-done = bf16[512,1024]{1,0:T(8,128)(2,1)S(1)} collective-permute-done((bf16[512,1024]{1,0:T(8,128)(2,1)S(1)}, bf16[512,1024]{1,0:T(8,128)(2,1)S(1)}, u32[]{:S(2)}, u32[]{:S(2)}) %collective-permute-start) | collective-permute-done | bytes 1048608 | tf_op jit(solution)/shard_map/ppermute | solution.py:79
  36.8 1.0 copy-done.2
  37.9 0.9 multiply_reduce_fusion.1
  38.8 16.8 %all-to-all-done = bf16[64,8,1024]{2,1,0:T(8,128)(2,1)S(1)} async-done(((bf16[64,8,1024]{2,1,0:T(8,128)(2,1)}), bf16[64,8,1024]{2,1,0:T(8,128)(2,1)S(1)}, u32[]{:S(2)}, u32[]{:S(2)}) %all-to-all-start) | async-done | bytes 1048608 | tf_op jit(solution)/shard_map/all_to_all | solution.py:86
  55.6 0.3 multiply_reduce_fusion.2
  55.9 0.1 add.68
  56.0 2.0 %add_subtract_fusion.1 = f32[512,512]{1,0:T(8,128)S(1)} fusion(bf16[64,8,1024]{2,1,0:T(8,128)(2,1)S(1)} %all-to-all-done, f32[512]{0:T(512)S(1)} %get-tuple-element.5, f32[512]{0:T(512)S(1)} %add.68, bf16[512,1024]{1,0:T(8,128)(2,1)S(1)} %copy-done.1, bf16[512,1024]{1,0:T(8,128)(2,1)} %copy-done.2, pred[]{:T(512)S(6)} %eq.8), kind=kOutput, calls=%fused_computation.33 | convolution fusion | flops 538181632 | bytes 4198401 | tf_op jit(solution)/shard_map/dot_general | solution.py:46
  58.0 0.8 add_subtract_fusion
  58.7 1.6 %pad_maximum_fusion = f32[2,8,64,512]{3,2,1,0:T(8,128)} fusion(f32[1,8,64,512]{3,2,1,0:T(8,128)S(1)} %bitcast.125, f32[1,8,64,512]{3,2,1,0:T(8,128)S(1)} %bitcast.124), kind=kLoop, calls=%fused_computation.8 | loop fusion | flops 524288 | bytes 4194304 | tf_op jit(solution)/shard_map/stack | solution.py:118
  60.3 4.9 %all-to-all-start.1 = ((f32[16,64,512]{2,1,0:T(8,128)}), f32[16,64,512]{2,1,0:T(8,128)S(1)}, u32[]{:S(2)}, u32[]{:S(2)}) async-start(f32[16,64,512]{2,1,0:T(8,128)} %bitcast.114), calls=%async_computation.1 | async-start | bytes 4194304 | tf_op jit(solution)/shard_map/all_to_all | solution.py:128
  65.2 0.1 fusion.38
  65.3 26.9 %all-to-all-done.1 = f32[16,64,512]{2,1,0:T(8,128)S(1)} async-done(((f32[16,64,512]{2,1,0:T(8,128)}), f32[16,64,512]{2,1,0:T(8,128)S(1)}, u32[]{:S(2)}, u32[]{:S(2)}) %all-to-all-start.1) | async-done | bytes 2097184 | tf_op jit(solution)/shard_map/all_to_all | solution.py:128
  92.2 0.2 bitcast_reduce_fusion
  92.5 0.1 exponential_convert_fusion
  92.6 0.8 broadcast_in_dim.32
  93.4 4.0 %all-to-all-start.2 = ((bf16[8,64,512]{2,1,0:T(8,128)(2,1)}), bf16[8,64,512]{2,1,0:T(8,128)(2,1)S(1)}, u32[]{:S(2)}, u32[]{:S(2)}) async-start(bf16[8,64,512]{2,1,0:T(8,128)(2,1)} %broadcast_in_dim.32), calls=%async_computation.2 | async-start | bytes 1048576 | tf_op jit(solution)/shard_map/all_to_all | solution.py:94
  97.4 0.1 convert_reduce_fusion.1
  97.5 0.2 fusion.25
  97.7 8.7 %all-to-all-done.2 = bf16[8,64,512]{2,1,0:T(8,128)(2,1)S(1)} async-done(((bf16[8,64,512]{2,1,0:T(8,128)(2,1)}), bf16[8,64,512]{2,1,0:T(8,128)(2,1)S(1)}, u32[]{:S(2)}, u32[]{:S(2)}) %all-to-all-start.2) | async-done | bytes 524320 | tf_op jit(solution)/shard_map/all_to_all | solution.py:94
  106.4 0.1 convert_reduce_fusion
  106.5 0.1 div.102
  106.6 0.3 multiply_reduce_fusion.3
  106.9 1.3 convolution_bitcast_fusion
  108.2 0.2 bitcast_dynamic-update-slice_fusion
  108.6 0.1 copy.51
  108.8 0.2 copy.52
  109.0 23.6 %all_to_all.20 = f32[64,1,8,128]{3,2,1,0:T(8,128)S(1)} all-to-all(f32[64,1,8,128]{3,2,1,0:T(8,128)S(1)} %copy.52), channel_id=1, replica_groups=mesh['z'=8,'y_hi'=4,'core'=2,'x'=4,'y_lo'=2] {'z','y_hi','core'}, dimensions={0} | all-to-all | bytes 524288 | tf_op jit(solution)/shard_map/all_to_all | solution.py:169
  132.6 0.1 slice_reduce_fusion.2
  132.7 0.1 slice_reduce_fusion.1
  132.9 0.1 reduce_sum.175
  133.1 0.1 multiply_reduce_fusion.4
  133.2 0.7 rsqrt_multiply_fusion
  (31 shorter events, 0.6 us)
Async XLA Ops:
  0.0 2.3 %copy-start = (bf16[512,128]{1,0:T(8,128)(2,1)S(1)}, bf16[512,128]{1,0:T(8,128)(2,1)}, u32[]{:S(2)}) copy-start(bf16[512,128]{1,0:T(8,128)(2,1)} %param.7) | copy-start | bytes 393220
  5.0 50.6 %all-to-all-start = ((bf16[64,8,1024]{2,1,0:T(8,128)(2,1)}), bf16[64,8,1024]{2,1,0:T(8,128)(2,1)S(1)}, u32[]{:S(2)}, u32[]{:S(2)}) async-start(bf16[64,8,1024]{2,1,0:T(8,128)(2,1)} %bitcast.12), calls=%async_computation | async-start | bytes 2097152 | tf_op jit(solution)/shard_map/all_to_all | solution.py:86
  22.8 4.5 %copy-start.3 = (bf16[512,128]{1,0:T(8,128)(2,1)S(1)}, bf16[512,128]{1,0:T(8,128)(2,1)}, u32[]{:S(2)}) copy-start(bf16[512,128]{1,0:T(8,128)(2,1)} %param.8) | copy-start | bytes 393220
  27.2 4.8 %copy-start.1 = (bf16[512,1024]{1,0:T(8,128)(2,1)S(1)}, bf16[512,1024]{1,0:T(8,128)(2,1)}, u32[]{:S(2)}) copy-start(bf16[512,1024]{1,0:T(8,128)(2,1)} %param.6) | copy-start | bytes 3145732
  32.2 4.6 %collective-permute-start = (bf16[512,1024]{1,0:T(8,128)(2,1)S(1)}, bf16[512,1024]{1,0:T(8,128)(2,1)S(1)}, u32[]{:S(2)}, u32[]{:S(2)}) collective-permute-start(bf16[512,1024]{1,0:T(8,128)(2,1)S(1)} %broadcast_select_fusion.2), channel_id=1, source_target_pairs={{0,8},{8,0},{1,9},{9,1},{2,10},{10,2},{3,11},{11,3},{4,12},{12,4},... | collective-permute-start | bytes 3145736 | tf_op jit(solution)/shard_map/ppermute | solution.py:79
  36.8 1.0 copy-start.2
  55.9 9.3 %copy-start.4 = (f32[512]{0:T(512)S(1)}, f32[512]{0:T(512)}, u32[]{:S(2)}) copy-start(f32[512]{0:T(512)} %param.11) | copy-start | bytes 6148
  56.0 9.3 %copy-start.5 = (f32[512]{0:T(512)S(1)}, f32[512]{0:T(512)}, u32[]{:S(2)}) copy-start(f32[512]{0:T(512)} %param.10) | copy-start | bytes 6148
  60.3 31.9 %all-to-all-start.1 = ((f32[16,64,512]{2,1,0:T(8,128)}), f32[16,64,512]{2,1,0:T(8,128)S(1)}, u32[]{:S(2)}, u32[]{:S(2)}) async-start(f32[16,64,512]{2,1,0:T(8,128)} %bitcast.114), calls=%async_computation.1 | async-start | bytes 4194304 | tf_op jit(solution)/shard_map/all_to_all | solution.py:128
  93.4 12.9 %all-to-all-start.2 = ((bf16[8,64,512]{2,1,0:T(8,128)(2,1)}), bf16[8,64,512]{2,1,0:T(8,128)(2,1)S(1)}, u32[]{:S(2)}, u32[]{:S(2)}) async-start(bf16[8,64,512]{2,1,0:T(8,128)(2,1)} %broadcast_in_dim.32), calls=%async_computation.2 | async-start | bytes 1048576 | tf_op jit(solution)/shard_map/all_to_all | solution.py:94

commit v15 on v11

--- a/solution.py
+++ b/solution.py
@@ -48,11 +48,11 @@
     )
 
 
-def attend_rows(queries, key_rows, value_rows, rows):
+def attend_rows(queries, key_rows, value_rows, rows, start):
     length = queries.shape[0]
     kv_heads = key_rows.shape[1] // HEAD_DIM
     group_size = queries.shape[1] // HEAD_DIM // kv_heads
-    picked = pick_rows(queries, rows)
+    picked = pick_rows(queries, rows, start)
     query_four = picked.reshape(rows.shape[0], kv_heads, group_size, HEAD_DIM)
     key_three = key_rows.reshape(length, kv_heads, HEAD_DIM)
     value_three = value_rows.reshape(length, kv_heads, HEAD_DIM)
@@ -60,7 +60,7 @@
         "tkgd,skd->kgts", query_four, key_three, preferred_element_type=jnp.float32
     ) / math.sqrt(HEAD_DIM)
     column_position = lax.broadcasted_iota(jnp.int32, (rows.shape[0], length), 1)
-    scores = jnp.where(column_position <= rows[:, None], scores, -jnp.inf)
+    scores = jnp.where(column_position + start <= rows[:, None], scores, -jnp.inf)
     weights = jax.nn.softmax(scores, axis=-1).astype(jnp.bfloat16)
     mixture = jnp.einsum(
         "kgts,skd->tkgd", weights, value_three, preferred_element_type=jnp.float32
@@ -68,8 +68,8 @@
     return mixture.astype(jnp.bfloat16).reshape(rows.shape[0], queries.shape[1])
 
 
-def pick_rows(matrix, rows):
-    hits = rows[:, None] == lax.broadcasted_iota(jnp.int32, (rows.shape[0], matrix.shape[0]), 1)
+def pick_rows(matrix, rows, start):
+    hits = rows[:, None] == start + lax.broadcasted_iota(jnp.int32, (rows.shape[0], matrix.shape[0]), 1)
     return jnp.dot(
         hits.astype(matrix.dtype), matrix, preferred_element_type=jnp.float32
     ).astype(matrix.dtype)
@@ -104,11 +104,11 @@
     column_share = landmarks // data_count
     token_count = length * data_count
 
-    own_rows = lax.rem(landmark_index, length)
+    start = lax.axis_index(DATA) * length
     first = lax.axis_index(CORE) == 0
     marks = gather_marks(
-        pick_rows(queries, own_rows),
-        attend_rows(queries, key_rows, value_rows, own_rows),
+        pick_rows(queries, landmark_index, start),
+        attend_rows(queries, key_rows, value_rows, landmark_index, start),
     ).reshape(landmarks, queries.shape[1])
     attended = attend(queries, key_rows, value_rows)
     swapped = swap_cores(jnp.where(first, attended, queries))

time: 133 us -> 133 us (level)
  no operation moved by 1% of the time
where the time goes in v15:
time: 133 us
  waiting for transfers between devices  54.6 us (41%)
  starting transfers between devices  28.9 us (22%)
  blocking collectives  22.5 us (17%)
  matrix products  12.9 us (10%)
  other arithmetic  8 us (6%)
  local copies, waits for them, and re-layouts  5.52 us (4%)
    all_to_all x1, waiting for transfers between devices, shards(): received = lax.all_to_all(distance_part, PAIR, 0, 0, tiled=True)  26.9 us
    all_to_all x1, blocking collectives, shards(): received = lax.all_to_all(packed, DATA, 0, 0, tiled=True)  22.5 us
    all_to_all x1, starting transfers between devices, gather_marks(): lax.all_to_all(spread.reshape((data_count,) + query_marks.shape), DATA, 0...  17.6 us
    all_to_all x1, waiting for transfers between devices, gather_marks(): lax.all_to_all(spread.reshape((data_count,) + query_marks.shape), DATA, 0...  16.8 us
    all_to_all x1, waiting for transfers between devices, broadcast_gather(): return lax.all_to_all(spread, axis_name, 0, 0, tiled=True)  8.66 us
    all_to_all x1, starting transfers between devices, shards(): received = lax.all_to_all(distance_part, PAIR, 0, 0, tiled=True)  4.91 us
    all_to_all x1, starting transfers between devices, broadcast_gather(): return lax.all_to_all(spread, axis_name, 0, 0, tiled=True)  3.97 us
    dot_general x1, matrix products, attend(): jnp.einsum('kgts,skd->tkgd', weights, value_three, preferred_element_type...  3.33 us
  transfers between devices with their start and end apart: 4, of which 4 were waited for; matrix products, arithmetic and copies ran while one was open for 8% of the time, Pallas kernels for 0%

profile of v15, /device:TPU:1, one launch (start us, length us, event | category | flops | bytes accessed | tf_op | source)
XLA Modules:
  0.0 132.8 jit_solution(6528505502630267986)
XLA Ops:
  0.0 0.8 broadcast_compare_fusion
  0.8 1.5 %convolution_convert_fusion.1 = bf16[8,1024]{1,0:T(8,128)(2,1)S(1)} fusion(bf16[512,1024]{1,0:T(8,128)(2,1)} %param.6, s32[512]{0:T(512)S(1)} %iota_add_fusion, s32[8]{0:T(128)} %param.9), kind=kOutput, calls=%fused_computation.23 | convolution fusion | flops 8400896 | bytes 1067040 | tf_op jit(solution)/shard_map/dot_general | solution.py:73
  2.3 0.3 fusion.43
  2.6 0.2 fusion.30
  2.7 0.1 fusion.33
  2.8 1.1 fusion.10
  3.9 1.1 broadcast_in_dim.28
  5.0 17.6 %all-to-all-start = ((bf16[64,8,1024]{2,1,0:T(8,128)(2,1)}), bf16[64,8,1024]{2,1,0:T(8,128)(2,1)S(1)}, u32[]{:S(2)}, u32[]{:S(2)}) async-start(bf16[64,8,1024]{2,1,0:T(8,128)(2,1)} %bitcast.12), calls=%async_computation | async-start | bytes 2097152 | tf_op jit(solution)/shard_map/all_to_all | solution.py:86
  22.7 0.1 iota_compare_fusion
  22.8 2.7 %fusion.1 = (f32[8,512]{1,0:T(8,128)S(1)}, f32[512,512,8]{1,0,2:T(8,128)S(1)}) fusion(pred[512,512]{0,1:T(8,128)(4,1)S(1)} %iota_compare_fusion, bf16[512,128]{1,0:T(8,128)(2,1)S(1)} %copy-done, bf16[512,1024]{1,0:T(8,128)(2,1)} %param.6), kind=kOutput, calls=%fused_computation.4 | convolution fusion | flops 543158272 | bytes 9846784 | tf_op jit(solution)/shard_map/tkgd,skd->kgts/dot_general | solution.py:28
  25.5 1.7 %fusion = f32[8,512]{1,0:T(8,128)S(1)} fusion(f32[512,512,8]{1,0,2:T(8,128)S(1)} %get-tuple-element.18, f32[8,512]{1,0:T(8,128)S(1)} %get-tuple-element.17, pred[512,512]{0,1:T(8,128)(4,1)S(1)} %iota_compare_fusion), kind=kLoop, calls=%fused_computation.3 | loop fusion | flops 8384512 | bytes 8683520 | tf_op jit(solution)/shard_map/reduce_sum | solution.py:34
  27.2 3.3 %fusion.5 = bf16[8,512,128]{1,2,0:T(8,128)(2,1)} fusion(f32[8,512]{1,0:T(8,128)S(1)} %fusion, f32[8,512]{1,0:T(8,128)S(1)} %get-tuple-element.17, f32[512,512,8]{1,0,2:T(8,128)S(1)} %get-tuple-element.18, pred[512,512]{0,1:T(8,128)(4,1)S(1)} %iota_compare_fusion, bf16[512,128]{1,0:T(8,128)(2,1)S(1)} %copy-done.3), kind=kOutput, calls=%fused_computation.13 | convolution fusion | flops 547880960 | bytes 9863168 | tf_op jit(solution)/shard_map/kgts,skd->tkgd/dot_general | solution.py:35
  30.6 1.5 %copy.46 = bf16[512,1024]{1,0:T(8,128)(2,1)S(1)} copy(bf16[512,1024]{0,1:T(8,128)(2,1)} %bitcast.120) | data formatting | bytes 2097152 | tf_op jit(solution)/shard_map/reshape | solution.py:38
  32.1 0.1 broadcast_select_fusion.2
  32.2 2.4 %collective-permute-start = (bf16[512,1024]{1,0:T(8,128)(2,1)S(1)}, bf16[512,1024]{1,0:T(8,128)(2,1)S(1)}, u32[]{:S(2)}, u32[]{:S(2)}) collective-permute-start(bf16[512,1024]{1,0:T(8,128)(2,1)S(1)} %broadcast_select_fusion.2), channel_id=1, source_target_pairs={{0,8},{8,0},{1,9},{9,1},{2,10},{10,2},{3,11},{11,3},{4,12},{12,4},... | collective-permute-start | bytes 3145736 | tf_op jit(solution)/shard_map/ppermute | solution.py:79
  34.6 2.3 %collective-permute-done = bf16[512,1024]{1,0:T(8,128)(2,1)S(1)} collective-permute-done((bf16[512,1024]{1,0:T(8,128)(2,1)S(1)}, bf16[512,1024]{1,0:T(8,128)(2,1)S(1)}, u32[]{:S(2)}, u32[]{:S(2)}) %collective-permute-start) | collective-permute-done | bytes 1048608 | tf_op jit(solution)/shard_map/ppermute | solution.py:79
  36.8 1.0 copy-done.2
  37.9 0.9 multiply_reduce_fusion.1
  38.8 16.8 %all-to-all-done = bf16[64,8,1024]{2,1,0:T(8,128)(2,1)S(1)} async-done(((bf16[64,8,1024]{2,1,0:T(8,128)(2,1)}), bf16[64,8,1024]{2,1,0:T(8,128)(2,1)S(1)}, u32[]{:S(2)}, u32[]{:S(2)}) %all-to-all-start) | async-done | bytes 1048608 | tf_op jit(solution)/shard_map/all_to_all | solution.py:86
  55.6 0.3 multiply_reduce_fusion.2
  55.9 0.1 add.87
  56.0 0.8 add_subtract_fusion
  56.7 2.0 %add_subtract_fusion.1 = f32[512,512]{1,0:T(8,128)S(1)} fusion(bf16[64,8,1024]{2,1,0:T(8,128)(2,1)S(1)} %all-to-all-done, f32[512]{0:T(512)S(1)} %get-tuple-element.5, f32[512]{0:T(512)S(1)} %add.87, bf16[512,1024]{1,0:T(8,128)(2,1)S(1)} %copy-done.1, bf16[512,1024]{1,0:T(8,128)(2,1)} %copy-done.2, pred[]{:T(512)S(6)} %eq.8), kind=kOutput, calls=%fused_computation.33 | convolution fusion | flops 538181632 | bytes 4198401 | tf_op jit(solution)/shard_map/dot_general | solution.py:46
  58.7 1.6 %pad_maximum_fusion = f32[2,8,64,512]{3,2,1,0:T(8,128)} fusion(f32[1,8,64,512]{3,2,1,0:T(8,128)S(1)} %bitcast.121, f32[1,8,64,512]{3,2,1,0:T(8,128)S(1)} %bitcast.122), kind=kLoop, calls=%fused_computation.8 | loop fusion | flops 524288 | bytes 4194304 | tf_op jit(solution)/shard_map/stack | solution.py:118
  60.3 4.9 %all-to-all-start.1 = ((f32[16,64,512]{2,1,0:T(8,128)}), f32[16,64,512]{2,1,0:T(8,128)S(1)}, u32[]{:S(2)}, u32[]{:S(2)}) async-start(f32[16,64,512]{2,1,0:T(8,128)} %bitcast.112), calls=%async_computation.1 | async-start | bytes 4194304 | tf_op jit(solution)/shard_map/all_to_all | solution.py:128
  65.2 0.1 fusion.40
  65.3 26.9 %all-to-all-done.1 = f32[16,64,512]{2,1,0:T(8,128)S(1)} async-done(((f32[16,64,512]{2,1,0:T(8,128)}), f32[16,64,512]{2,1,0:T(8,128)S(1)}, u32[]{:S(2)}, u32[]{:S(2)}) %all-to-all-start.1) | async-done | bytes 2097184 | tf_op jit(solution)/shard_map/all_to_all | solution.py:128
  92.2 0.2 bitcast_reduce_fusion
  92.4 0.1 exponential_convert_fusion
  92.6 0.8 broadcast_in_dim.32
  93.4 4.0 %all-to-all-start.2 = ((bf16[8,64,512]{2,1,0:T(8,128)(2,1)}), bf16[8,64,512]{2,1,0:T(8,128)(2,1)S(1)}, u32[]{:S(2)}, u32[]{:S(2)}) async-start(bf16[8,64,512]{2,1,0:T(8,128)(2,1)} %broadcast_in_dim.32), calls=%async_computation.2 | async-start | bytes 1048576 | tf_op jit(solution)/shard_map/all_to_all | solution.py:94
  97.4 0.1 convert_reduce_fusion.1
  97.5 0.2 fusion.25
  97.7 8.7 %all-to-all-done.2 = bf16[8,64,512]{2,1,0:T(8,128)(2,1)S(1)} async-done(((bf16[8,64,512]{2,1,0:T(8,128)(2,1)}), bf16[8,64,512]{2,1,0:T(8,128)(2,1)S(1)}, u32[]{:S(2)}, u32[]{:S(2)}) %all-to-all-start.2) | async-done | bytes 524320 | tf_op jit(solution)/shard_map/all_to_all | solution.py:94
  106.4 0.1 convert_reduce_fusion
  106.5 0.1 div.102
  106.6 0.3 multiply_reduce_fusion.3
  106.9 1.3 convolution_bitcast_fusion
  108.2 0.2 bitcast_dynamic-update-slice_fusion
  108.4 0.1 broadcast_dynamic-update-slice_fusion.1
  108.6 0.1 copy.51
  108.7 0.2 copy.52
  108.9 22.5 %all_to_all.27 = f32[64,1,656]{2,1,0:T(1,128)S(1)} all-to-all(f32[64,1,656]{2,1,0:T(1,128)S(1)} %copy.52), channel_id=1, replica_groups=mesh['z'=8,'y_hi'=4,'core'=2,'x'=4,'y_lo'=2] {'z','y_hi','core'}, dimensions={0} | all-to-all | bytes 335872 | tf_op jit(solution)/shard_map/all_to_all | solution.py:167
  131.5 0.1 slice_reduce_fusion.1
  131.6 0.1 slice_reduce_fusion.2
  131.7 0.1 reduce_sum.175
  131.9 0.1 multiply_reduce_fusion.4
  132.1 0.7 rsqrt_multiply_fusion
  (30 shorter events, 0.4 us)
Async XLA Ops:
  0.0 2.3 %copy-start = (bf16[512,128]{1,0:T(8,128)(2,1)S(1)}, bf16[512,128]{1,0:T(8,128)(2,1)}, u32[]{:S(2)}) copy-start(bf16[512,128]{1,0:T(8,128)(2,1)} %param.7) | copy-start | bytes 393220
  5.0 50.5 %all-to-all-start = ((bf16[64,8,1024]{2,1,0:T(8,128)(2,1)}), bf16[64,8,1024]{2,1,0:T(8,128)(2,1)S(1)}, u32[]{:S(2)}, u32[]{:S(2)}) async-start(bf16[64,8,1024]{2,1,0:T(8,128)(2,1)} %bitcast.12), calls=%async_computation | async-start | bytes 2097152 | tf_op jit(solution)/shard_map/all_to_all | solution.py:86
  22.8 4.5 %copy-start.3 = (bf16[512,128]{1,0:T(8,128)(2,1)S(1)}, bf16[512,128]{1,0:T(8,128)(2,1)}, u32[]{:S(2)}) copy-start(bf16[512,128]{1,0:T(8,128)(2,1)} %param.8) | copy-start | bytes 393220
  27.2 4.8 %copy-start.1 = (bf16[512,1024]{1,0:T(8,128)(2,1)S(1)}, bf16[512,1024]{1,0:T(8,128)(2,1)}, u32[]{:S(2)}) copy-start(bf16[512,1024]{1,0:T(8,128)(2,1)} %param.6) | copy-start | bytes 3145732
  32.2 4.6 %collective-permute-start = (bf16[512,1024]{1,0:T(8,128)(2,1)S(1)}, bf16[512,1024]{1,0:T(8,128)(2,1)S(1)}, u32[]{:S(2)}, u32[]{:S(2)}) collective-permute-start(bf16[512,1024]{1,0:T(8,128)(2,1)S(1)} %broadcast_select_fusion.2), channel_id=1, source_target_pairs={{0,8},{8,0},{1,9},{9,1},{2,10},{10,2},{3,11},{11,3},{4,12},{12,4},... | collective-permute-start | bytes 3145736 | tf_op jit(solution)/shard_map/ppermute | solution.py:79
  36.8 1.0 copy-start.2
  56.0 9.3 %copy-start.4 = (f32[512]{0:T(512)S(1)}, f32[512]{0:T(512)}, u32[]{:S(2)}) copy-start(f32[512]{0:T(512)} %param.11) | copy-start | bytes 6148
  56.0 9.3 %copy-start.5 = (f32[512]{0:T(512)S(1)}, f32[512]{0:T(512)}, u32[]{:S(2)}) copy-start(f32[512]{0:T(512)} %param.10) | copy-start | bytes 6148
  60.3 31.9 %all-to-all-start.1 = ((f32[16,64,512]{2,1,0:T(8,128)}), f32[16,64,512]{2,1,0:T(8,128)S(1)}, u32[]{:S(2)}, u32[]{:S(2)}) async-start(f32[16,64,512]{2,1,0:T(8,128)} %bitcast.112), calls=%async_computation.1 | async-start | bytes 4194304 | tf_op jit(solution)/shard_map/all_to_all | solution.py:128
  93.4 12.9 %all-to-all-start.2 = ((bf16[8,64,512]{2,1,0:T(8,128)(2,1)}), bf16[8,64,512]{2,1,0:T(8,128)(2,1)S(1)}, u32[]{:S(2)}, u32[]{:S(2)}) async-start(bf16[8,64,512]{2,1,0:T(8,128)(2,1)} %broadcast_in_dim.32), calls=%async_computation.2 | async-start | bytes 1048576 | tf_op jit(solution)/shard_map/all_to_all | solution.py:94

commit v16 on v11

--- a/solution.py
+++ b/solution.py
@@ -140,17 +140,16 @@
     columns32 = column_features.astype(jnp.float32)
     row_mean = jnp.mean(rows32, axis=1)
     column_mean = jnp.mean(columns32, axis=1)
-    rows_centered = rows32 - row_mean[:, None]
-    columns_centered = columns32 - column_mean[:, None]
+    rows_centered = (rows32 - row_mean[:, None]).astype(jnp.bfloat16)
+    columns_centered = (columns32 - column_mean[:, None]).astype(jnp.bfloat16)
     second = lax.dot_general(
         rows_centered,
         columns_centered,
         (((1,), (1,)), ((), ())),
-        precision=lax.Precision.HIGH,
         preferred_element_type=jnp.float32,
     )
-    row_square = jnp.sum(jnp.square(rows_centered), axis=1)
-    column_square = jnp.sum(jnp.square(columns_centered), axis=1)
+    row_square = jnp.sum(jnp.square(rows_centered.astype(jnp.float32)), axis=1)
+    column_square = jnp.sum(jnp.square(columns_centered.astype(jnp.float32)), axis=1)
 
     packed = jnp.concatenate(
         [

time: 133 us -> 132 us (level)
  no operation moved by 1% of the time
where the time goes in v16:
time: 132 us
  waiting for transfers between devices  54.6 us (41%)
  starting transfers between devices  28.9 us (22%)
  blocking collectives  22.5 us (17%)
  matrix products  12 us (9%)
  other arithmetic  8.04 us (6%)
  local copies, waits for them, and re-layouts  5.52 us (4%)
    all_to_all x1, waiting for transfers between devices, shards(): received = lax.all_to_all(distance_part, PAIR, 0, 0, tiled=True)  26.9 us
    all_to_all x1, blocking collectives, shards(): received = lax.all_to_all(packed, DATA, 0, 0, tiled=True)  22.5 us
    all_to_all x1, starting transfers between devices, gather_marks(): lax.all_to_all(spread.reshape((data_count,) + query_marks.shape), DATA, 0...  17.6 us
    all_to_all x1, waiting for transfers between devices, gather_marks(): lax.all_to_all(spread.reshape((data_count,) + query_marks.shape), DATA, 0...  16.8 us
    all_to_all x1, waiting for transfers between devices, broadcast_gather(): return lax.all_to_all(spread, axis_name, 0, 0, tiled=True)  8.66 us
    all_to_all x1, starting transfers between devices, shards(): received = lax.all_to_all(distance_part, PAIR, 0, 0, tiled=True)  4.91 us
    all_to_all x1, starting transfers between devices, broadcast_gather(): return lax.all_to_all(spread, axis_name, 0, 0, tiled=True)  3.97 us
    dot_general x1, matrix products, attend(): jnp.einsum('kgts,skd->tkgd', weights, value_three, preferred_element_type...  3.33 us
  transfers between devices with their start and end apart: 4, of which 4 were waited for; matrix products, arithmetic and copies ran while one was open for 8% of the time, Pallas kernels for 0%

profile of v16, /device:TPU:1, one launch (start us, length us, event | category | flops | bytes accessed | tf_op | source)
XLA Modules:
  0.0 131.9 jit_solution(14574593562330214953)
XLA Ops:
  0.0 0.7 compare_select_fusion
  0.7 0.1 iota_compare_fusion.1
  0.8 1.5 %convolution_convert_fusion.1 = bf16[8,1024]{1,0:T(8,128)(2,1)S(1)} fusion(bf16[512,1024]{1,0:T(8,128)(2,1)} %param.6, s32[8]{0:T(128)S(1)} %compare_select_fusion), kind=kOutput, calls=%fused_computation.23 | convolution fusion | flops 8400896 | bytes 1064992 | tf_op jit(solution)/shard_map/dot_general | solution.py:73
  2.3 0.3 fusion.44
  2.5 0.2 fusion.29
  2.7 0.1 fusion.34
  2.8 1.1 fusion.10
  3.9 1.1 broadcast_in_dim.28
  5.0 17.6 %all-to-all-start = ((bf16[64,8,1024]{2,1,0:T(8,128)(2,1)}), bf16[64,8,1024]{2,1,0:T(8,128)(2,1)S(1)}, u32[]{:S(2)}, u32[]{:S(2)}) async-start(bf16[64,8,1024]{2,1,0:T(8,128)(2,1)} %bitcast.12), calls=%async_computation | async-start | bytes 2097152 | tf_op jit(solution)/shard_map/all_to_all | solution.py:86
  22.7 0.1 iota_compare_fusion
  22.8 2.7 %fusion.1 = (f32[8,512]{1,0:T(8,128)S(1)}, f32[512,512,8]{1,0,2:T(8,128)S(1)}) fusion(pred[512,512]{0,1:T(8,128)(4,1)S(1)} %iota_compare_fusion, bf16[512,128]{1,0:T(8,128)(2,1)S(1)} %copy-done, bf16[512,1024]{1,0:T(8,128)(2,1)} %param.6), kind=kOutput, calls=%fused_computation.4 | convolution fusion | flops 543158272 | bytes 9846784 | tf_op jit(solution)/shard_map/tkgd,skd->kgts/dot_general | solution.py:28
  25.5 1.7 %fusion = f32[8,512]{1,0:T(8,128)S(1)} fusion(f32[512,512,8]{1,0,2:T(8,128)S(1)} %get-tuple-element.18, f32[8,512]{1,0:T(8,128)S(1)} %get-tuple-element.17, pred[512,512]{0,1:T(8,128)(4,1)S(1)} %iota_compare_fusion), kind=kLoop, calls=%fused_computation.3 | loop fusion | flops 8384512 | bytes 8683520 | tf_op jit(solution)/shard_map/reduce_sum | solution.py:34
  27.2 3.3 %fusion.5 = bf16[8,512,128]{1,2,0:T(8,128)(2,1)} fusion(f32[8,512]{1,0:T(8,128)S(1)} %fusion, f32[8,512]{1,0:T(8,128)S(1)} %get-tuple-element.17, f32[512,512,8]{1,0,2:T(8,128)S(1)} %get-tuple-element.18, pred[512,512]{0,1:T(8,128)(4,1)S(1)} %iota_compare_fusion, bf16[512,128]{1,0:T(8,128)(2,1)S(1)} %copy-done.3), kind=kOutput, calls=%fused_computation.13 | convolution fusion | flops 547880960 | bytes 9863168 | tf_op jit(solution)/shard_map/kgts,skd->tkgd/dot_general | solution.py:35
  30.6 1.5 %copy.46 = bf16[512,1024]{1,0:T(8,128)(2,1)S(1)} copy(bf16[512,1024]{0,1:T(8,128)(2,1)} %bitcast.120) | data formatting | bytes 2097152 | tf_op jit(solution)/shard_map/reshape | solution.py:38
  32.1 0.1 broadcast_select_fusion.2
  32.2 2.4 %collective-permute-start = (bf16[512,1024]{1,0:T(8,128)(2,1)S(1)}, bf16[512,1024]{1,0:T(8,128)(2,1)S(1)}, u32[]{:S(2)}, u32[]{:S(2)}) collective-permute-start(bf16[512,1024]{1,0:T(8,128)(2,1)S(1)} %broadcast_select_fusion.2), channel_id=1, source_target_pairs={{0,8},{8,0},{1,9},{9,1},{2,10},{10,2},{3,11},{11,3},{4,12},{12,4},... | collective-permute-start | bytes 3145736 | tf_op jit(solution)/shard_map/ppermute | solution.py:79
  34.6 2.3 %collective-permute-done = bf16[512,1024]{1,0:T(8,128)(2,1)S(1)} collective-permute-done((bf16[512,1024]{1,0:T(8,128)(2,1)S(1)}, bf16[512,1024]{1,0:T(8,128)(2,1)S(1)}, u32[]{:S(2)}, u32[]{:S(2)}) %collective-permute-start) | collective-permute-done | bytes 1048608 | tf_op jit(solution)/shard_map/ppermute | solution.py:79
  36.8 1.0 copy-done.2
  37.9 0.9 multiply_reduce_fusion.1
  38.8 16.8 %all-to-all-done = bf16[64,8,1024]{2,1,0:T(8,128)(2,1)S(1)} async-done(((bf16[64,8,1024]{2,1,0:T(8,128)(2,1)}), bf16[64,8,1024]{2,1,0:T(8,128)(2,1)S(1)}, u32[]{:S(2)}, u32[]{:S(2)}) %all-to-all-start) | async-done | bytes 1048608 | tf_op jit(solution)/shard_map/all_to_all | solution.py:86
  55.6 0.3 multiply_reduce_fusion.2
  55.9 0.1 add.66
  56.0 2.0 %add_subtract_fusion.1 = f32[512,512]{1,0:T(8,128)S(1)} fusion(bf16[64,8,1024]{2,1,0:T(8,128)(2,1)S(1)} %all-to-all-done, f32[512]{0:T(512)S(1)} %get-tuple-element.5, f32[512]{0:T(512)S(1)} %add.66, bf16[512,1024]{1,0:T(8,128)(2,1)S(1)} %copy-done.1, bf16[512,1024]{1,0:T(8,128)(2,1)} %copy-done.2, pred[]{:T(512)S(6)} %eq.8), kind=kOutput, calls=%fused_computation.33 | convolution fusion | flops 538181632 | bytes 4198401 | tf_op jit(solution)/shard_map/dot_general | solution.py:46
  58.0 0.8 add_subtract_fusion
  58.7 1.6 %pad_maximum_fusion = f32[2,8,64,512]{3,2,1,0:T(8,128)} fusion(f32[1,8,64,512]{3,2,1,0:T(8,128)S(1)} %bitcast.122, f32[1,8,64,512]{3,2,1,0:T(8,128)S(1)} %bitcast.121), kind=kLoop, calls=%fused_computation.8 | loop fusion | flops 524288 | bytes 4194304 | tf_op jit(solution)/shard_map/stack | solution.py:118
  60.3 4.9 %all-to-all-start.1 = ((f32[16,64,512]{2,1,0:T(8,128)}), f32[16,64,512]{2,1,0:T(8,128)S(1)}, u32[]{:S(2)}, u32[]{:S(2)}) async-start(f32[16,64,512]{2,1,0:T(8,128)} %bitcast.112), calls=%async_computation.1 | async-start | bytes 4194304 | tf_op jit(solution)/shard_map/all_to_all | solution.py:128
  65.2 0.1 fusion.39
  65.3 26.9 %all-to-all-done.1 = f32[16,64,512]{2,1,0:T(8,128)S(1)} async-done(((f32[16,64,512]{2,1,0:T(8,128)}), f32[16,64,512]{2,1,0:T(8,128)S(1)}, u32[]{:S(2)}, u32[]{:S(2)}) %all-to-all-start.1) | async-done | bytes 2097184 | tf_op jit(solution)/shard_map/all_to_all | solution.py:128
  92.2 0.2 bitcast_reduce_fusion
  92.5 0.1 exponential_convert_fusion
  92.6 0.8 broadcast_in_dim.32
  93.4 4.0 %all-to-all-start.2 = ((bf16[8,64,512]{2,1,0:T(8,128)(2,1)}), bf16[8,64,512]{2,1,0:T(8,128)(2,1)S(1)}, u32[]{:S(2)}, u32[]{:S(2)}) async-start(bf16[8,64,512]{2,1,0:T(8,128)(2,1)} %broadcast_in_dim.32), calls=%async_computation.2 | async-start | bytes 1048576 | tf_op jit(solution)/shard_map/all_to_all | solution.py:94
  97.4 0.1 convert_reduce_fusion.1
  97.5 0.2 multiply_reduce_fusion.5
  97.7 8.7 %all-to-all-done.2 = bf16[8,64,512]{2,1,0:T(8,128)(2,1)S(1)} async-done(((bf16[8,64,512]{2,1,0:T(8,128)(2,1)}), bf16[8,64,512]{2,1,0:T(8,128)(2,1)S(1)}, u32[]{:S(2)}, u32[]{:S(2)}) %all-to-all-start.2) | async-done | bytes 524320 | tf_op jit(solution)/shard_map/all_to_all | solution.py:94
  106.4 0.1 convert_reduce_fusion
  106.5 0.1 div.102
  106.6 0.3 multiply_reduce_fusion.3
  106.9 0.4 convolution_bitcast_fusion
  107.3 0.2 bitcast_dynamic-update-slice_fusion
  107.7 0.1 copy.51
  107.9 0.2 copy.52
  108.0 22.5 %all_to_all.27 = f32[64,1,656]{2,1,0:T(1,128)S(1)} all-to-all(f32[64,1,656]{2,1,0:T(1,128)S(1)} %copy.52), channel_id=1, replica_groups=mesh['z'=8,'y_hi'=4,'core'=2,'x'=4,'y_lo'=2] {'z','y_hi','core'}, dimensions={0} | all-to-all | bytes 335872 | tf_op jit(solution)/shard_map/all_to_all | solution.py:166
  130.6 0.1 slice_reduce_fusion.2
  130.7 0.1 slice_reduce_fusion.1
  130.9 0.1 reduce_sum.175
  131.1 0.1 multiply_reduce_fusion.4
  131.2 0.7 rsqrt_multiply_fusion
  (30 shorter events, 0.5 us)
Async XLA Ops:
  0.0 2.3 %copy-start = (bf16[512,128]{1,0:T(8,128)(2,1)S(1)}, bf16[512,128]{1,0:T(8,128)(2,1)}, u32[]{:S(2)}) copy-start(bf16[512,128]{1,0:T(8,128)(2,1)} %param.7) | copy-start | bytes 393220
  5.0 50.6 %all-to-all-start = ((bf16[64,8,1024]{2,1,0:T(8,128)(2,1)}), bf16[64,8,1024]{2,1,0:T(8,128)(2,1)S(1)}, u32[]{:S(2)}, u32[]{:S(2)}) async-start(bf16[64,8,1024]{2,1,0:T(8,128)(2,1)} %bitcast.12), calls=%async_computation | async-start | bytes 2097152 | tf_op jit(solution)/shard_map/all_to_all | solution.py:86
  22.8 4.5 %copy-start.3 = (bf16[512,128]{1,0:T(8,128)(2,1)S(1)}, bf16[512,128]{1,0:T(8,128)(2,1)}, u32[]{:S(2)}) copy-start(bf16[512,128]{1,0:T(8,128)(2,1)} %param.8) | copy-start | bytes 393220
  27.2 4.8 %copy-start.1 = (bf16[512,1024]{1,0:T(8,128)(2,1)S(1)}, bf16[512,1024]{1,0:T(8,128)(2,1)}, u32[]{:S(2)}) copy-start(bf16[512,1024]{1,0:T(8,128)(2,1)} %param.6) | copy-start | bytes 3145732
  32.2 4.6 %collective-permute-start = (bf16[512,1024]{1,0:T(8,128)(2,1)S(1)}, bf16[512,1024]{1,0:T(8,128)(2,1)S(1)}, u32[]{:S(2)}, u32[]{:S(2)}) collective-permute-start(bf16[512,1024]{1,0:T(8,128)(2,1)S(1)} %broadcast_select_fusion.2), channel_id=1, source_target_pairs={{0,8},{8,0},{1,9},{9,1},{2,10},{10,2},{3,11},{11,3},{4,12},{12,4},... | collective-permute-start | bytes 3145736 | tf_op jit(solution)/shard_map/ppermute | solution.py:79
  36.8 1.0 copy-start.2
  55.9 9.3 %copy-start.4 = (f32[512]{0:T(512)S(1)}, f32[512]{0:T(512)}, u32[]{:S(2)}) copy-start(f32[512]{0:T(512)} %param.11) | copy-start | bytes 6148
  56.0 9.3 %copy-start.5 = (f32[512]{0:T(512)S(1)}, f32[512]{0:T(512)}, u32[]{:S(2)}) copy-start(f32[512]{0:T(512)} %param.10) | copy-start | bytes 6148
  60.3 31.9 %all-to-all-start.1 = ((f32[16,64,512]{2,1,0:T(8,128)}), f32[16,64,512]{2,1,0:T(8,128)S(1)}, u32[]{:S(2)}, u32[]{:S(2)}) async-start(f32[16,64,512]{2,1,0:T(8,128)} %bitcast.112), calls=%async_computation.1 | async-start | bytes 4194304 | tf_op jit(solution)/shard_map/all_to_all | solution.py:128
  93.4 12.9 %all-to-all-start.2 = ((bf16[8,64,512]{2,1,0:T(8,128)(2,1)}), bf16[8,64,512]{2,1,0:T(8,128)(2,1)S(1)}, u32[]{:S(2)}, u32[]{:S(2)}) async-start(bf16[8,64,512]{2,1,0:T(8,128)(2,1)} %broadcast_in_dim.32), calls=%async_computation.2 | async-start | bytes 1048576 | tf_op jit(solution)/shard_map/all_to_all | solution.py:94

commit v17 on v15

--- a/solution.py
+++ b/solution.py
@@ -140,17 +140,16 @@
     columns32 = column_features.astype(jnp.float32)
     row_mean = jnp.mean(rows32, axis=1)
     column_mean = jnp.mean(columns32, axis=1)
-    rows_centered = rows32 - row_mean[:, None]
-    columns_centered = columns32 - column_mean[:, None]
+    rows_centered = (rows32 - row_mean[:, None]).astype(jnp.bfloat16)
+    columns_centered = (columns32 - column_mean[:, None]).astype(jnp.bfloat16)
     second = lax.dot_general(
         rows_centered,
         columns_centered,
         (((1,), (1,)), ((), ())),
-        precision=lax.Precision.HIGH,
         preferred_element_type=jnp.float32,
     )
-    row_square = jnp.sum(jnp.square(rows_centered), axis=1)
-    column_square = jnp.sum(jnp.square(columns_centered), axis=1)
+    row_square = jnp.sum(jnp.square(rows_centered.astype(jnp.float32)), axis=1)
+    column_square = jnp.sum(jnp.square(columns_centered.astype(jnp.float32)), axis=1)
 
     packed = jnp.concatenate(
         [

time: 133 us -> 132 us (level)
  no operation moved by 1% of the time
where the time goes in v17:
time: 132 us
  waiting for transfers between devices  54.6 us (41%)
  starting transfers between devices  28.9 us (22%)
  blocking collectives  22.5 us (17%)
  matrix products  12 us (9%)
  other arithmetic  8.02 us (6%)
  local copies, waits for them, and re-layouts  5.52 us (4%)
    all_to_all x1, waiting for transfers between devices, shards(): received = lax.all_to_all(distance_part, PAIR, 0, 0, tiled=True)  26.9 us
    all_to_all x1, blocking collectives, shards(): received = lax.all_to_all(packed, DATA, 0, 0, tiled=True)  22.5 us
    all_to_all x1, starting transfers between devices, gather_marks(): lax.all_to_all(spread.reshape((data_count,) + query_marks.shape), DATA, 0...  17.6 us
    all_to_all x1, waiting for transfers between devices, gather_marks(): lax.all_to_all(spread.reshape((data_count,) + query_marks.shape), DATA, 0...  16.8 us
    all_to_all x1, waiting for transfers between devices, broadcast_gather(): return lax.all_to_all(spread, axis_name, 0, 0, tiled=True)  8.66 us
    all_to_all x1, starting transfers between devices, shards(): received = lax.all_to_all(distance_part, PAIR, 0, 0, tiled=True)  4.9 us
    all_to_all x1, starting transfers between devices, broadcast_gather(): return lax.all_to_all(spread, axis_name, 0, 0, tiled=True)  3.97 us
    dot_general x1, matrix products, attend(): jnp.einsum('kgts,skd->tkgd', weights, value_three, preferred_element_type...  3.33 us
  transfers between devices with their start and end apart: 4, of which 4 were waited for; matrix products, arithmetic and copies ran while one was open for 8% of the time, Pallas kernels for 0%

profile of v17, /device:TPU:1, one launch (start us, length us, event | category | flops | bytes accessed | tf_op | source)
XLA Modules:
  0.0 131.9 jit_solution(3630307486867764150)
XLA Ops:
  0.0 0.8 broadcast_compare_fusion
  0.8 1.5 %convolution_convert_fusion.1 = bf16[8,1024]{1,0:T(8,128)(2,1)S(1)} fusion(bf16[512,1024]{1,0:T(8,128)(2,1)} %param.6, s32[512]{0:T(512)S(1)} %iota_add_fusion, s32[8]{0:T(128)} %param.9), kind=kOutput, calls=%fused_computation.23 | convolution fusion | flops 8400896 | bytes 1067040 | tf_op jit(solution)/shard_map/dot_general | solution.py:73
  2.3 0.3 fusion.45
  2.6 0.2 fusion.29
  2.7 0.1 fusion.34
  2.8 1.1 fusion.10
  3.9 1.1 broadcast_in_dim.28
  5.0 17.6 %all-to-all-start = ((bf16[64,8,1024]{2,1,0:T(8,128)(2,1)}), bf16[64,8,1024]{2,1,0:T(8,128)(2,1)S(1)}, u32[]{:S(2)}, u32[]{:S(2)}) async-start(bf16[64,8,1024]{2,1,0:T(8,128)(2,1)} %bitcast.12), calls=%async_computation | async-start | bytes 2097152 | tf_op jit(solution)/shard_map/all_to_all | solution.py:86
  22.7 0.1 iota_compare_fusion
  22.8 2.7 %fusion.1 = (f32[8,512]{1,0:T(8,128)S(1)}, f32[512,512,8]{1,0,2:T(8,128)S(1)}) fusion(pred[512,512]{0,1:T(8,128)(4,1)S(1)} %iota_compare_fusion, bf16[512,128]{1,0:T(8,128)(2,1)S(1)} %copy-done, bf16[512,1024]{1,0:T(8,128)(2,1)} %param.6), kind=kOutput, calls=%fused_computation.4 | convolution fusion | flops 543158272 | bytes 9846784 | tf_op jit(solution)/shard_map/tkgd,skd->kgts/dot_general | solution.py:28
  25.5 1.7 %fusion = f32[8,512]{1,0:T(8,128)S(1)} fusion(f32[512,512,8]{1,0,2:T(8,128)S(1)} %get-tuple-element.18, f32[8,512]{1,0:T(8,128)S(1)} %get-tuple-element.17, pred[512,512]{0,1:T(8,128)(4,1)S(1)} %iota_compare_fusion), kind=kLoop, calls=%fused_computation.3 | loop fusion | flops 8384512 | bytes 8683520 | tf_op jit(solution)/shard_map/reduce_sum | solution.py:34
  27.2 3.3 %fusion.5 = bf16[8,512,128]{1,2,0:T(8,128)(2,1)} fusion(f32[8,512]{1,0:T(8,128)S(1)} %fusion, f32[8,512]{1,0:T(8,128)S(1)} %get-tuple-element.17, f32[512,512,8]{1,0,2:T(8,128)S(1)} %get-tuple-element.18, pred[512,512]{0,1:T(8,128)(4,1)S(1)} %iota_compare_fusion, bf16[512,128]{1,0:T(8,128)(2,1)S(1)} %copy-done.3), kind=kOutput, calls=%fused_computation.13 | convolution fusion | flops 547880960 | bytes 9863168 | tf_op jit(solution)/shard_map/kgts,skd->tkgd/dot_general | solution.py:35
  30.6 1.5 %copy.46 = bf16[512,1024]{1,0:T(8,128)(2,1)S(1)} copy(bf16[512,1024]{0,1:T(8,128)(2,1)} %bitcast.120) | data formatting | bytes 2097152 | tf_op jit(solution)/shard_map/reshape | solution.py:38
  32.1 0.1 broadcast_select_fusion.2
  32.2 2.4 %collective-permute-start = (bf16[512,1024]{1,0:T(8,128)(2,1)S(1)}, bf16[512,1024]{1,0:T(8,128)(2,1)S(1)}, u32[]{:S(2)}, u32[]{:S(2)}) collective-permute-start(bf16[512,1024]{1,0:T(8,128)(2,1)S(1)} %broadcast_select_fusion.2), channel_id=1, source_target_pairs={{0,8},{8,0},{1,9},{9,1},{2,10},{10,2},{3,11},{11,3},{4,12},{12,4},... | collective-permute-start | bytes 3145736 | tf_op jit(solution)/shard_map/ppermute | solution.py:79
  34.6 2.3 %collective-permute-done = bf16[512,1024]{1,0:T(8,128)(2,1)S(1)} collective-permute-done((bf16[512,1024]{1,0:T(8,128)(2,1)S(1)}, bf16[512,1024]{1,0:T(8,128)(2,1)S(1)}, u32[]{:S(2)}, u32[]{:S(2)}) %collective-permute-start) | collective-permute-done | bytes 1048608 | tf_op jit(solution)/shard_map/ppermute | solution.py:79
  36.8 1.0 copy-done.2
  37.9 0.9 multiply_reduce_fusion.1
  38.8 16.8 %all-to-all-done = bf16[64,8,1024]{2,1,0:T(8,128)(2,1)S(1)} async-done(((bf16[64,8,1024]{2,1,0:T(8,128)(2,1)}), bf16[64,8,1024]{2,1,0:T(8,128)(2,1)S(1)}, u32[]{:S(2)}, u32[]{:S(2)}) %all-to-all-start) | async-done | bytes 1048608 | tf_op jit(solution)/shard_map/all_to_all | solution.py:86
  55.6 0.3 multiply_reduce_fusion.2
  55.9 0.1 add.87
  56.0 0.8 add_subtract_fusion
  56.7 2.0 %add_subtract_fusion.1 = f32[512,512]{1,0:T(8,128)S(1)} fusion(bf16[64,8,1024]{2,1,0:T(8,128)(2,1)S(1)} %all-to-all-done, f32[512]{0:T(512)S(1)} %get-tuple-element.5, f32[512]{0:T(512)S(1)} %add.87, bf16[512,1024]{1,0:T(8,128)(2,1)S(1)} %copy-done.1, bf16[512,1024]{1,0:T(8,128)(2,1)} %copy-done.2, pred[]{:T(512)S(6)} %eq.8), kind=kOutput, calls=%fused_computation.33 | convolution fusion | flops 538181632 | bytes 4198401 | tf_op jit(solution)/shard_map/dot_general | solution.py:46
  58.7 1.6 %pad_maximum_fusion = f32[2,8,64,512]{3,2,1,0:T(8,128)} fusion(f32[1,8,64,512]{3,2,1,0:T(8,128)S(1)} %bitcast.121, f32[1,8,64,512]{3,2,1,0:T(8,128)S(1)} %bitcast.122), kind=kLoop, calls=%fused_computation.8 | loop fusion | flops 524288 | bytes 4194304 | tf_op jit(solution)/shard_map/stack | solution.py:118
  60.3 4.9 %all-to-all-start.1 = ((f32[16,64,512]{2,1,0:T(8,128)}), f32[16,64,512]{2,1,0:T(8,128)S(1)}, u32[]{:S(2)}, u32[]{:S(2)}) async-start(f32[16,64,512]{2,1,0:T(8,128)} %bitcast.112), calls=%async_computation.1 | async-start | bytes 4194304 | tf_op jit(solution)/shard_map/all_to_all | solution.py:128
  65.2 0.1 fusion.41
  65.3 26.9 %all-to-all-done.1 = f32[16,64,512]{2,1,0:T(8,128)S(1)} async-done(((f32[16,64,512]{2,1,0:T(8,128)}), f32[16,64,512]{2,1,0:T(8,128)S(1)}, u32[]{:S(2)}, u32[]{:S(2)}) %all-to-all-start.1) | async-done | bytes 2097184 | tf_op jit(solution)/shard_map/all_to_all | solution.py:128
  92.2 0.2 bitcast_reduce_fusion
  92.4 0.1 exponential_convert_fusion
  92.6 0.8 broadcast_in_dim.32
  93.4 4.0 %all-to-all-start.2 = ((bf16[8,64,512]{2,1,0:T(8,128)(2,1)}), bf16[8,64,512]{2,1,0:T(8,128)(2,1)S(1)}, u32[]{:S(2)}, u32[]{:S(2)}) async-start(bf16[8,64,512]{2,1,0:T(8,128)(2,1)} %broadcast_in_dim.32), calls=%async_computation.2 | async-start | bytes 1048576 | tf_op jit(solution)/shard_map/all_to_all | solution.py:94
  97.4 0.1 convert_reduce_fusion.1
  97.5 0.2 multiply_reduce_fusion.5
  97.7 8.7 %all-to-all-done.2 = bf16[8,64,512]{2,1,0:T(8,128)(2,1)S(1)} async-done(((bf16[8,64,512]{2,1,0:T(8,128)(2,1)}), bf16[8,64,512]{2,1,0:T(8,128)(2,1)S(1)}, u32[]{:S(2)}, u32[]{:S(2)}) %all-to-all-start.2) | async-done | bytes 524320 | tf_op jit(solution)/shard_map/all_to_all | solution.py:94
  106.4 0.1 convert_reduce_fusion
  106.5 0.1 div.102
  106.6 0.3 multiply_reduce_fusion.3
  106.9 0.4 convolution_bitcast_fusion
  107.3 0.2 bitcast_dynamic-update-slice_fusion
  107.5 0.1 broadcast_dynamic-update-slice_fusion.1
  107.7 0.1 copy.51
  107.8 0.2 copy.52
  108.0 22.5 %all_to_all.27 = f32[64,1,656]{2,1,0:T(1,128)S(1)} all-to-all(f32[64,1,656]{2,1,0:T(1,128)S(1)} %copy.52), channel_id=1, replica_groups=mesh['z'=8,'y_hi'=4,'core'=2,'x'=4,'y_lo'=2] {'z','y_hi','core'}, dimensions={0} | all-to-all | bytes 335872 | tf_op jit(solution)/shard_map/all_to_all | solution.py:166
  130.6 0.1 slice_reduce_fusion.1
  130.7 0.1 slice_reduce_fusion.2
  130.8 0.1 reduce_sum.175
  131.0 0.1 multiply_reduce_fusion.4
  131.2 0.7 rsqrt_multiply_fusion
  (30 shorter events, 0.4 us)
Async XLA Ops:
  0.0 2.3 %copy-start = (bf16[512,128]{1,0:T(8,128)(2,1)S(1)}, bf16[512,128]{1,0:T(8,128)(2,1)}, u32[]{:S(2)}) copy-start(bf16[512,128]{1,0:T(8,128)(2,1)} %param.7) | copy-start | bytes 393220
  5.0 50.6 %all-to-all-start = ((bf16[64,8,1024]{2,1,0:T(8,128)(2,1)}), bf16[64,8,1024]{2,1,0:T(8,128)(2,1)S(1)}, u32[]{:S(2)}, u32[]{:S(2)}) async-start(bf16[64,8,1024]{2,1,0:T(8,128)(2,1)} %bitcast.12), calls=%async_computation | async-start | bytes 2097152 | tf_op jit(solution)/shard_map/all_to_all | solution.py:86
  22.8 4.5 %copy-start.3 = (bf16[512,128]{1,0:T(8,128)(2,1)S(1)}, bf16[512,128]{1,0:T(8,128)(2,1)}, u32[]{:S(2)}) copy-start(bf16[512,128]{1,0:T(8,128)(2,1)} %param.8) | copy-start | bytes 393220
  27.2 4.8 %copy-start.1 = (bf16[512,1024]{1,0:T(8,128)(2,1)S(1)}, bf16[512,1024]{1,0:T(8,128)(2,1)}, u32[]{:S(2)}) copy-start(bf16[512,1024]{1,0:T(8,128)(2,1)} %param.6) | copy-start | bytes 3145732
  32.2 4.6 %collective-permute-start = (bf16[512,1024]{1,0:T(8,128)(2,1)S(1)}, bf16[512,1024]{1,0:T(8,128)(2,1)S(1)}, u32[]{:S(2)}, u32[]{:S(2)}) collective-permute-start(bf16[512,1024]{1,0:T(8,128)(2,1)S(1)} %broadcast_select_fusion.2), channel_id=1, source_target_pairs={{0,8},{8,0},{1,9},{9,1},{2,10},{10,2},{3,11},{11,3},{4,12},{12,4},... | collective-permute-start | bytes 3145736 | tf_op jit(solution)/shard_map/ppermute | solution.py:79
  36.8 1.0 copy-start.2
  56.0 9.3 %copy-start.4 = (f32[512]{0:T(512)S(1)}, f32[512]{0:T(512)}, u32[]{:S(2)}) copy-start(f32[512]{0:T(512)} %param.11) | copy-start | bytes 6148
  56.0 9.3 %copy-start.5 = (f32[512]{0:T(512)S(1)}, f32[512]{0:T(512)}, u32[]{:S(2)}) copy-start(f32[512]{0:T(512)} %param.10) | copy-start | bytes 6148
  60.3 31.9 %all-to-all-start.1 = ((f32[16,64,512]{2,1,0:T(8,128)}), f32[16,64,512]{2,1,0:T(8,128)S(1)}, u32[]{:S(2)}, u32[]{:S(2)}) async-start(f32[16,64,512]{2,1,0:T(8,128)} %bitcast.112), calls=%async_computation.1 | async-start | bytes 4194304 | tf_op jit(solution)/shard_map/all_to_all | solution.py:128
  93.4 12.9 %all-to-all-start.2 = ((bf16[8,64,512]{2,1,0:T(8,128)(2,1)}), bf16[8,64,512]{2,1,0:T(8,128)(2,1)S(1)}, u32[]{:S(2)}, u32[]{:S(2)}) async-start(bf16[8,64,512]{2,1,0:T(8,128)(2,1)} %broadcast_in_dim.32), calls=%async_computation.2 | async-start | bytes 1048576 | tf_op jit(solution)/shard_map/all_to_all | solution.py:94
